TPU v7x, 512 devices: a whole 4x8x8 slice. The times are simulated.
512 devices in a mesh: rows: 64 (over x, y, z_lo), feat: 8 (over z_hi, core).
Axes of the slice: x: 4, y: 8, z: 8 (z_hi: 4, z_lo: 2; z = z_hi * 2 + z_lo), core: 2. Of those that a mesh axis runs over, the one named last changes fastest.
Arguments:
- train_cells: bfloat16 [1024, 64, 192], P(('rows', 'feat')), may hold values from -7 to 7
- test_cells: bfloat16 [2048, 64, 192], P(('rows', 'feat')), may hold values from -7 to 7
- train_mask: int32 [1024, 64], P(('rows', 'feat')), may hold values from 0 to 1, as said below
- test_mask: int32 [2048, 64], P(('rows', 'feat')), may hold values 0 or 1
- feat_qkv: bfloat16 [192, 576], replicated, may hold values from -4 to 4
- feat_out: bfloat16 [192, 192], replicated, may hold values from -0.4375 to 0.4375
- feat_gain: float32 [192], replicated, may hold values from 0.5 to 1.5
- feat_bias: float32 [192], replicated, may hold values from -1 to 1
- item_qkv: bfloat16 [192, 576], replicated, may hold values from -4 to 4
- item_out: bfloat16 [192, 192], replicated, may hold values from -0.4375 to 0.4375
- item_gain: float32 [192], replicated, may hold values from 0.5 to 1.5
- item_bias: float32 [192], replicated, may hold values from -1 to 1
- mlp_in: bfloat16 [192, 768], replicated, may hold values from -0.4375 to 0.4375
- mlp_out: bfloat16 [768, 192], replicated, may hold values from -0.21875 to 0.21875
- mlp_gain: float32 [192], replicated, may hold values from 0.5 to 1.5
- mlp_bias: float32 [192], replicated, may hold values from -1 to 1
Outputs:
- train_out: bfloat16 [1024, 64, 192], P(('rows', 'feat'))
- test_out: bfloat16 [2048, 64, 192], P(('rows', 'feat'))
Inputs may be any that keep to these rules, and one draw needn't show every extreme that they name: `train_mask`: each of the 64 features has at least one training row marked 1.
All inputs are finite; a program needn't handle non-finite values. No bound on the sum of `test_mask` on one device may be relied on, other than what follows from the above.
Results may differ from a plain program's by a relative error of at most 0.02.
The roundings to bfloat16 on the way count: a program that leaves them out, or rounds other values in their place, can miss the bound.
Values may be sent and summed in bfloat16 or wider, within the bound.
No kernel may reach another device: no remote copies, remote signals or barrier semaphores. Data moves between devices by JAX's collectives and lax.ppermute only.
A program may use at most 128 MiB of HBM per device.

v0:
```python
import math

import jax
import jax.numpy as jnp
from jax import lax
from jax.sharding import PartitionSpec as P

HEADS = 6


EPS = 1e-05
NEG = -1e30
key_block = 512


def layer_norm(values, norm_gain, norm_bias):
    centre = jnp.mean(values, axis=-1, keepdims=True)
    centred = values - centre
    variance = jnp.mean(centred * centred, axis=-1, keepdims=True)
    return centred * lax.rsqrt(variance + EPS) * norm_gain + norm_bias


def feature_block(cell_rows, qkv_weight, out_weight, norm_gain, norm_bias):
    row_count, feat_count, model_width = cell_rows.shape
    head_size = model_width // HEADS
    flat_rows = cell_rows.reshape(row_count * feat_count, model_width)
    packed = jnp.dot(flat_rows, qkv_weight, preferred_element_type=jnp.float32).astype(jnp.bfloat16)
    packed = packed.reshape(row_count, feat_count, 3, HEADS, head_size)
    scores = jnp.einsum(
        "rqhd,rkhd->rhqk", packed[:, :, 0], packed[:, :, 1], preferred_element_type=jnp.float32
    ) / math.sqrt(head_size)
    row_top = jnp.max(scores, axis=-1, keepdims=True)
    weights_exp = jnp.exp(scores - row_top)
    weights = (weights_exp / jnp.sum(weights_exp, axis=-1, keepdims=True)).astype(jnp.bfloat16)
    attended = jnp.einsum(
        "rhqk,rkhd->rqhd", weights, packed[:, :, 2], preferred_element_type=jnp.float32
    ).astype(jnp.bfloat16)
    branch = jnp.dot(
        attended.reshape(row_count * feat_count, model_width),
        out_weight,
        preferred_element_type=jnp.float32,
    )
    settled = layer_norm(flat_rows.astype(jnp.float32) + branch, norm_gain, norm_bias)
    return settled.astype(jnp.bfloat16).reshape(row_count, feat_count, model_width)


def project_pairs(cell_rows, item_qkv):
    row_count, feat_count, model_width = cell_rows.shape
    key_values = jnp.dot(
        cell_rows.reshape(row_count * feat_count, model_width),
        item_qkv[:, model_width:],
        preferred_element_type=jnp.float32,
    )
    return key_values.astype(jnp.bfloat16).reshape(row_count, feat_count, 2 * model_width)


def absorb_keys(state_now, queries, key_values, key_marks):
    row_top, totals, weighted = state_now
    row_count, feat_count, double = key_values.shape
    head_size = double // (2 * HEADS)
    halves = key_values.reshape(row_count, feat_count, 2, HEADS, head_size)
    scores = jnp.einsum(
        "qfhd,kfhd->fhqk", queries, halves[:, :, 0], preferred_element_type=jnp.float32
    ) / math.sqrt(head_size)
    alive_keys = jnp.transpose(key_marks > 0)[:, None, None, :]
    masked = jnp.where(alive_keys, scores, NEG)
    new_top = jnp.maximum(row_top, jnp.max(masked, axis=-1))
    weights_exp = jnp.where(alive_keys, jnp.exp(masked - new_top[..., None]), 0.0)
    factor = jnp.exp(row_top - new_top)
    totals = totals * factor + jnp.sum(weights_exp, axis=-1)
    weighted = weighted * factor[..., None] + jnp.einsum(
        "fhqk,kfhd->fhqd",
        weights_exp.astype(jnp.bfloat16),
        halves[:, :, 1],
        preferred_element_type=jnp.float32,
    )
    return (new_top, totals, weighted)


def fold_keys(state_now, queries, key_values, key_marks):
    row_count = key_values.shape[0]
    for first_row in range(0, row_count, key_block):
        finish = min(first_row + key_block, row_count)
        state_now = absorb_keys(
            state_now, queries, key_values[first_row:finish], key_marks[first_row:finish]
        )
    return state_now


def item_section(col_train, col_test, col_marks, col_test_marks, item_weights, gather_keys):
    item_qkv, item_out, item_gain, item_bias, mlp_in, mlp_out, mlp_gain, mlp_bias = item_weights
    train_rows, feat_count, model_width = col_train.shape
    head_size = model_width // HEADS
    all_rows = jnp.concatenate([col_train, col_test], axis=0)
    total_rows = all_rows.shape[0]
    flat_rows = all_rows.reshape(total_rows * feat_count, model_width)
    queries = jnp.dot(
        flat_rows, item_qkv[:, :model_width], preferred_element_type=jnp.float32
    ).astype(jnp.bfloat16)
    queries = queries.reshape(total_rows, feat_count, HEADS, head_size)
    initial = (
        jnp.full((feat_count, HEADS, total_rows), NEG, jnp.float32),
        jnp.zeros((feat_count, HEADS, total_rows), jnp.float32),
        jnp.zeros((feat_count, HEADS, total_rows, head_size), jnp.float32),
    )
    payload = project_pairs(col_train, item_qkv)

    def absorb(state_now, shard_piece, offset):
        key_values = shard_piece[0]
        return fold_keys(state_now, queries, key_values, shard_piece[1])

    row_top, totals, weighted = gather_keys(payload, col_marks, absorb, initial)
    attended = (weighted / totals[..., None]).astype(jnp.bfloat16)
    attended = jnp.transpose(attended, (2, 0, 1, 3)).reshape(total_rows * feat_count, model_width)
    branch = jnp.dot(attended, item_out, preferred_element_type=jnp.float32).reshape(
        total_rows, feat_count, model_width
    )
    keep_gate = jnp.concatenate(
        [jnp.ones((train_rows, feat_count), jnp.float32), col_test_marks.astype(jnp.float32)],
        axis=0,
    )
    branch = branch * keep_gate[:, :, None]
    settled = layer_norm(all_rows.astype(jnp.float32) + branch, item_gain, item_bias).astype(
        jnp.bfloat16
    )
    settled = settled.reshape(total_rows * feat_count, model_width)
    hidden_units = jax.nn.gelu(
        jnp.dot(settled, mlp_in, preferred_element_type=jnp.float32), approximate=False
    ).astype(jnp.bfloat16)
    result_rows = layer_norm(
        settled.astype(jnp.float32)
        + jnp.dot(hidden_units, mlp_out, preferred_element_type=jnp.float32),
        mlp_gain,
        mlp_bias,
    )
    result_rows = result_rows.astype(jnp.bfloat16).reshape(total_rows, feat_count, model_width)
    return (result_rows[:train_rows], result_rows[train_rows:])


def per_device(
    train_cells,
    test_cells,
    train_mask,
    test_mask,
    feat_qkv,
    feat_out,
    feat_gain,
    feat_bias,
    item_qkv,
    item_out,
    item_gain,
    item_bias,
    mlp_in,
    mlp_out,
    mlp_gain,
    mlp_bias,
):
    train_count = train_cells.shape[0]
    both_rows = jnp.concatenate([train_cells, test_cells], axis=0)
    settled = feature_block(both_rows, feat_qkv, feat_out, feat_gain, feat_bias)
    train_h = settled[:train_count]
    test_h = settled[train_count:]
    train_marks = train_mask.astype(jnp.bfloat16)
    test_marks = test_mask.astype(jnp.bfloat16)
    item_weights = (item_qkv, item_out, item_gain, item_bias, mlp_in, mlp_out, mlp_gain, mlp_bias)
    col_train, col_test, col_marks, col_test_marks = (
        lax.all_to_all(train_h, "rows", split_axis=1, concat_axis=0, tiled=True),
        lax.all_to_all(test_h, "rows", split_axis=1, concat_axis=0, tiled=True),
        lax.all_to_all(train_marks, "rows", split_axis=1, concat_axis=0, tiled=True),
        lax.all_to_all(test_marks, "rows", split_axis=1, concat_axis=0, tiled=True),
    )

    def gather_second(payload, key_marks, absorb, initial):
        return absorb(
            initial,
            (
                lax.all_gather(payload, "feat", axis=0, tiled=True),
                lax.all_gather(key_marks, "feat", axis=0, tiled=True),
            ),
            jnp.int32(0),
        )

    done_train, done_test = item_section(
        col_train, col_test, col_marks, col_test_marks, item_weights, gather_second
    )
    train_out, test_out = (
        lax.all_to_all(done_train, "rows", split_axis=0, concat_axis=1, tiled=True),
        lax.all_to_all(done_test, "rows", split_axis=0, concat_axis=1, tiled=True),
    )
    return (train_out, test_out)


def solution(mesh):
    return jax.shard_map(
        per_device,
        mesh=mesh,
        in_specs=(
            P(("rows", "feat"), None, None),
            P(("rows", "feat"), None, None),
            P(("rows", "feat"), None),
            P(("rows", "feat"), None),
            P(),
            P(),
            P(),
            P(),
            P(),
            P(),
            P(),
            P(),
            P(),
            P(),
            P(),
            P(),
        ),
        out_specs=(P(("rows", "feat"), None, None), P(("rows", "feat"), None, None)),
        check_vma=False,
    )
```

profile of v0, /device:TPU:1, one launch (start us, length us, event | category | flops | bytes accessed | tf_op | source)
XLA Modules:
  0.0 146.1 jit_solution(11887848519394984525)
XLA Ops:
  0.6 0.7 convert_bitcast_fusion.1
  1.4 0.7 copy.88
  2.1 12.9 %all-to-all-start.2 = ((bf16[2,64,1]{0,2,1:T(2,128)(2,1)}), bf16[2,64,1]{0,2,1:T(2,128)(2,1)S(1)}, u32[]{:S(2)}, u32[]{:S(2)}) async-start(bf16[2,64,1]{0,2,1:T(2,128)(2,1)} %copy.88), calls=%async_computation.2 | async-start | bytes 65536 | tf_op jit(solution)/shard_map/all_to_all | solution.py:169
  15.0 0.9 pad_maximum_fusion
  16.1 1.3 convolution_convert_fusion
  17.5 0.6 reshape.260
  20.7 0.7 copy.92
  21.6 0.7 copy.83
  22.4 0.8 copy.85
  23.1 1.1 all-to-all-done.2
  24.2 9.6 %all-to-all-start.3 = ((bf16[4,64,1]{0,2,1:T(2,128)(2,1)}), bf16[4,64,1]{0,2,1:T(2,128)(2,1)S(1)}, u32[]{:S(2)}, u32[]{:S(2)}) async-start(bf16[4,64,1]{0,2,1:T(2,128)(2,1)} %copy.92), calls=%async_computation.3 | async-start | bytes 65536 | tf_op jit(solution)/shard_map/all_to_all | solution.py:170
  34.1 18.1 %all_gather.6 = bf16[1024,1]{0,1:T(2,128)(2,1)S(1)} all-gather(bf16[128,1]{0,1:T(2,128)(2,1)S(1)} %all_to_all.85), channel_id=1, replica_groups=mesh['rows'=64,'feat'=8] {'feat'}, dimensions={0}, use_global_device_ids=true | all-gather | bytes 2304 | tf_op jit(solution)/shard_map/all_gather | solution.py:178
  52.2 11.0 %all-to-all-start = ((bf16[2,64,192]{2,0,1:T(2,128)(2,1)}), bf16[2,64,192]{2,0,1:T(2,128)(2,1)S(1)}, u32[]{:S(2)}, u32[]{:S(2)}) async-start(bf16[2,64,192]{2,0,1:T(2,128)(2,1)} %copy.83), calls=%async_computation | async-start | bytes 131072 | tf_op jit(solution)/shard_map/all_to_all | solution.py:167
  63.4 9.1 %all-to-all-done = bf16[2,64,192]{2,0,1:T(2,128)(2,1)S(1)} async-done(((bf16[2,64,192]{2,0,1:T(2,128)(2,1)}), bf16[2,64,192]{2,0,1:T(2,128)(2,1)S(1)}, u32[]{:S(2)}, u32[]{:S(2)}) %all-to-all-start) | async-done | bytes 49184 | tf_op jit(solution)/shard_map/all_to_all | solution.py:167
  72.5 4.6 %all-to-all-start.1 = ((bf16[4,64,192]{2,0,1:T(4,128)(2,1)}), bf16[4,64,192]{2,0,1:T(4,128)(2,1)S(1)}, u32[]{:S(2)}, u32[]{:S(2)}) async-start(bf16[4,64,192]{2,0,1:T(4,128)(2,1)} %copy.85), calls=%async_computation.1 | async-start | bytes 262144 | tf_op jit(solution)/shard_map/all_to_all | solution.py:168
  77.7 17.3 %all-gather = bf16[1024,384]{1,0:T(8,128)(2,1)S(1)} all-gather(bf16[128,384]{1,0:T(8,128)(2,1)S(1)} %convolution_convert_fusion.3), channel_id=2, replica_groups=mesh['rows'=64,'feat'=8] {'feat'}, dimensions={0}, use_global_device_ids=true | all-gather | bytes 884736 | tf_op jit(solution)/shard_map/all_gather | solution.py:177
  96.0 0.9 fusion.2
  96.9 0.9 fusion.1
  97.9 1.1 fusion.7
  99.0 2.7 %fusion.3 = (f32[6,384]{1,0:T(8,128)S(1)}, f32[6,384]{1,0:T(8,128)S(1)}) fusion(f32[6,384,512]{2,1,0:T(8,128)S(1)} %get-tuple-element.25, f32[6,384]{1,0:T(8,128)S(1)} %get-tuple-element.19, pred[512]{0:T(512)(128)(4,1)S(1)} %get-tuple-element.8, f32[6,384]{1,0:T(8,128)S(1)} %get-tuple-element.18, f32[6,384,512]{2,1,0:T(8,128)S(1)} %get-tuple-element.27, ...), kind=kLoop, calls=%fused_computation.7 | loop fusion | flops 11791872 | bytes 9475072 | tf_op jit(solution)/shard_map/reduce_sum | solution.py:70
  101.8 1.3 fusion.41
  103.6 3.2 %fusion.133 = (f32[384]{0:T(512)S(1)}, f32[384,192]{0,1:T(8,128)S(1)}) fusion(bf16[768,192]{0,1:T(8,128)(2,1)S(1)} %copy-done, bf16[192,768]{1,0:T(8,128)(2,1)S(1)} %copy-done.9, f32[384,192]{0,1:T(8,128)S(1)} %get-tuple-element.29, f32[192]{0:T(256)S(1)} %copy-done.10, f32[192]{0:T(256)S(1)} %copy-done.11, f32[384]{0:T(512)S(1)} %add_rsqrt_fusion.1, ...), kind=kOutput, calls=%fused_computation.172 | convolution fusion | flops 246619776 | bytes 1185792 | tf_op jit(solution)/shard_map/dot_general | solution.py:132
  107.5 0.7 reduce.24
  108.3 0.7 reshape.285
  109.0 11.9 %all-to-all-start.4 = ((bf16[64,2,192]{2,1,0:T(2,128)(2,1)}), bf16[64,2,192]{2,1,0:T(2,128)(2,1)S(1)}, u32[]{:S(2)}, u32[]{:S(2)}) async-start(bf16[64,2,192]{2,1,0:T(2,128)(2,1)} %reshape.285), calls=%async_computation.4 | async-start | bytes 131072 | tf_op jit(solution)/shard_map/all_to_all | solution.py:187
  120.9 0.7 reduce.25
  121.7 0.8 reshape.287
  122.5 7.8 %all-to-all-done.4 = bf16[64,2,192]{2,1,0:T(2,128)(2,1)S(1)} async-done(((bf16[64,2,192]{2,1,0:T(2,128)(2,1)}), bf16[64,2,192]{2,1,0:T(2,128)(2,1)S(1)}, u32[]{:S(2)}, u32[]{:S(2)}) %all-to-all-start.4) | async-done | bytes 49184 | tf_op jit(solution)/shard_map/all_to_all | solution.py:187
  130.2 4.6 %all-to-all-start.5 = ((bf16[64,2,384]{2,1,0:T(2,128)(2,1)}), bf16[64,2,384]{2,1,0:T(2,128)(2,1)S(1)}, u32[]{:S(2)}, u32[]{:S(2)}) async-start(bf16[64,2,384]{2,1,0:T(2,128)(2,1)} %reshape.287), calls=%async_computation.5 | async-start | bytes 196608 | tf_op jit(solution)/shard_map/all_to_all | solution.py:188
  136.0 8.4 %all-to-all-done.5 = bf16[64,2,384]{2,1,0:T(2,128)(2,1)S(1)} async-done(((bf16[64,2,384]{2,1,0:T(2,128)(2,1)}), bf16[64,2,384]{2,1,0:T(2,128)(2,1)S(1)}, u32[]{:S(2)}, u32[]{:S(2)}) %all-to-all-start.5) | async-done | bytes 98336 | tf_op jit(solution)/shard_map/all_to_all | solution.py:188
  144.6 0.8 reduce.18
  145.4 0.7 copy.96
  (80 shorter events, 7.6 us)
Async XLA Ops:
  0.6 102.9 %copy-start = (bf16[768,192]{0,1:T(8,128)(2,1)S(1)}, bf16[768,192]{0,1:T(8,128)(2,1)}, u32[]{:S(2)}) copy-start(bf16[768,192]{0,1:T(8,128)(2,1)} %param.29) | copy-start | bytes 884740
  2.1 22.1 %all-to-all-start.2 = ((bf16[2,64,1]{0,2,1:T(2,128)(2,1)}), bf16[2,64,1]{0,2,1:T(2,128)(2,1)S(1)}, u32[]{:S(2)}, u32[]{:S(2)}) async-start(bf16[2,64,1]{0,2,1:T(2,128)(2,1)} %copy.88), calls=%async_computation.2 | async-start | bytes 65536 | tf_op jit(solution)/shard_map/all_to_all | solution.py:169
  19.3 0.9 copy-start.1
  19.3 1.2 copy-start.5
  19.3 1.2 copy-start.6
  19.3 1.4 copy-start.4
  20.6 56.9 %copy-start.3 = (bf16[192,576]{1,0:T(8,128)(2,1)S(1)}, bf16[192,576]{1,0:T(8,128)(2,1)}, u32[]{:S(2)}) copy-start(bf16[192,576]{1,0:T(8,128)(2,1)} %param.24) | copy-start | bytes 663556
  24.2 27.9 %all-to-all-start.3 = ((bf16[4,64,1]{0,2,1:T(2,128)(2,1)}), bf16[4,64,1]{0,2,1:T(2,128)(2,1)S(1)}, u32[]{:S(2)}, u32[]{:S(2)}) async-start(bf16[4,64,1]{0,2,1:T(2,128)(2,1)} %copy.92), calls=%async_computation.3 | async-start | bytes 65536 | tf_op jit(solution)/shard_map/all_to_all | solution.py:170
  52.2 20.4 %all-to-all-start = ((bf16[2,64,192]{2,0,1:T(2,128)(2,1)}), bf16[2,64,192]{2,0,1:T(2,128)(2,1)S(1)}, u32[]{:S(2)}, u32[]{:S(2)}) async-start(bf16[2,64,192]{2,0,1:T(2,128)(2,1)} %copy.83), calls=%async_computation | async-start | bytes 131072 | tf_op jit(solution)/shard_map/all_to_all | solution.py:167
  72.5 23.0 %all-to-all-start.1 = ((bf16[4,64,192]{2,0,1:T(4,128)(2,1)}), bf16[4,64,192]{2,0,1:T(4,128)(2,1)S(1)}, u32[]{:S(2)}, u32[]{:S(2)}) async-start(bf16[4,64,192]{2,0,1:T(4,128)(2,1)} %copy.85), calls=%async_computation.1 | async-start | bytes 262144 | tf_op jit(solution)/shard_map/all_to_all | solution.py:168
  101.8 1.4 copy-start.2
  101.8 1.7 %copy-start.9 = (bf16[192,768]{1,0:T(8,128)(2,1)S(1)}, bf16[192,768]{1,0:T(8,128)(2,1)}, u32[]{:S(2)}) copy-start(bf16[192,768]{1,0:T(8,128)(2,1)} %param.28) | copy-start | bytes 884740
  101.8 1.7 %copy-start.10 = (f32[192]{0:T(256)S(1)}, f32[192]{0:T(256)}, u32[]{:S(2)}) copy-start(f32[192]{0:T(256)} %param.27) | copy-start | bytes 2308
  101.8 1.7 %copy-start.11 = (f32[192]{0:T(256)S(1)}, f32[192]{0:T(256)}, u32[]{:S(2)}) copy-start(f32[192]{0:T(256)} %param.26) | copy-start | bytes 2308
  103.5 3.3 %copy-start.7 = (f32[192]{0:T(256)S(1)}, f32[192]{0:T(256)}, u32[]{:S(2)}) copy-start(f32[192]{0:T(256)} %param.31) | copy-start | bytes 2308
  103.6 3.3 %copy-start.8 = (f32[192]{0:T(256)S(1)}, f32[192]{0:T(256)}, u32[]{:S(2)}) copy-start(f32[192]{0:T(256)} %param.30) | copy-start | bytes 2308
  109.0 21.3 %all-to-all-start.4 = ((bf16[64,2,192]{2,1,0:T(2,128)(2,1)}), bf16[64,2,192]{2,1,0:T(2,128)(2,1)S(1)}, u32[]{:S(2)}, u32[]{:S(2)}) async-start(bf16[64,2,192]{2,1,0:T(2,128)(2,1)} %reshape.285), calls=%async_computation.4 | async-start | bytes 131072 | tf_op jit(solution)/shard_map/all_to_all | solution.py:187
  130.2 14.2 %all-to-all-start.5 = ((bf16[64,2,384]{2,1,0:T(2,128)(2,1)}), bf16[64,2,384]{2,1,0:T(2,128)(2,1)S(1)}, u32[]{:S(2)}, u32[]{:S(2)}) async-start(bf16[64,2,384]{2,1,0:T(2,128)(2,1)} %reshape.287), calls=%async_computation.5 | async-start | bytes 196608 | tf_op jit(solution)/shard_map/all_to_all | solution.py:188
where the time goes:
time: 147 us; the launch traced here: 146 us
  starting transfers between devices  54.6 us (37%)
  blocking collectives  35.4 us (24%)
  waiting for transfers between devices  26.4 us (18%)
  matrix products  10.8 us (7%)
  local copies, waits for them, and re-layouts  10.4 us (7%)
  other arithmetic  7.46 us (5%)
    all_gather x1, blocking collectives, gather_second(): lax.all_gather(key_marks, 'feat', axis=0, tiled=True)  18.1 us
    all_gather x1, blocking collectives, gather_second(): lax.all_gather(payload, 'feat', axis=0, tiled=True)  17.3 us
    all_to_all x1, starting transfers between devices, per_device(): lax.all_to_all(train_marks, 'rows', split_axis=1, concat_axis=0, tiled=True)  12.9 us
    all_to_all x1, starting transfers between devices, per_device(): lax.all_to_all(done_train, 'rows', split_axis=0, concat_axis=1, tiled=True)  11.9 us
    all_to_all x1, starting transfers between devices, per_device(): lax.all_to_all(train_h, 'rows', split_axis=1, concat_axis=0, tiled=True)  11 us
    all_to_all x1, starting transfers between devices, per_device(): lax.all_to_all(test_marks, 'rows', split_axis=1, concat_axis=0, tiled=True)  9.58 us
    all_to_all x1, waiting for transfers between devices, per_device(): lax.all_to_all(train_h, 'rows', split_axis=1, concat_axis=0, tiled=True)  9.15 us
    all_to_all x1, waiting for transfers between devices, per_device(): lax.all_to_all(done_test, 'rows', split_axis=0, concat_axis=1, tiled=True)  8.37 us
  transfers between devices with their start and end apart: 6, of which 4 were waited for; matrix products, arithmetic and copies ran while one was open for 8% of the time, Pallas kernels for 0%

commit v1 on v0

v1 whole, which is shorter than its diff:
```python
import math

import jax
import jax.numpy as jnp
from jax import lax
from jax.sharding import PartitionSpec as P

HEADS = 6


EPS = 1e-05
NEG = -1e30


def layer_norm(values, norm_gain, norm_bias):
    centre = jnp.mean(values, axis=-1, keepdims=True)
    centred = values - centre
    variance = jnp.mean(centred * centred, axis=-1, keepdims=True)
    return centred * lax.rsqrt(variance + EPS) * norm_gain + norm_bias


def feature_block(cell_rows, qkv_weight, out_weight, norm_gain, norm_bias):
    row_count, feat_count, model_width = cell_rows.shape
    head_size = model_width // HEADS
    flat_rows = cell_rows.reshape(row_count * feat_count, model_width)
    packed = jnp.dot(flat_rows, qkv_weight, preferred_element_type=jnp.float32).astype(jnp.bfloat16)
    packed = packed.reshape(row_count, feat_count, 3, HEADS, head_size)
    scores = jnp.einsum(
        "rqhd,rkhd->rhqk", packed[:, :, 0], packed[:, :, 1], preferred_element_type=jnp.float32
    ) / math.sqrt(head_size)
    row_top = jnp.max(scores, axis=-1, keepdims=True)
    weights_exp = jnp.exp(scores - row_top)
    weights = (weights_exp / jnp.sum(weights_exp, axis=-1, keepdims=True)).astype(jnp.bfloat16)
    attended = jnp.einsum(
        "rhqk,rkhd->rqhd", weights, packed[:, :, 2], preferred_element_type=jnp.float32
    ).astype(jnp.bfloat16)
    branch = jnp.dot(
        attended.reshape(row_count * feat_count, model_width),
        out_weight,
        preferred_element_type=jnp.float32,
    )
    settled = layer_norm(flat_rows.astype(jnp.float32) + branch, norm_gain, norm_bias)
    return settled.astype(jnp.bfloat16).reshape(row_count, feat_count, model_width)


def item_attention(query_rows, key_rows, key_marks, item_qkv):
    query_count, model_width = query_rows.shape
    key_count = key_rows.shape[0]
    head_size = model_width // HEADS
    queries = jnp.dot(
        query_rows, item_qkv[:, :model_width], preferred_element_type=jnp.float32
    ).astype(jnp.bfloat16)
    queries = queries.reshape(query_count, HEADS, head_size)
    key_values = jnp.dot(
        key_rows, item_qkv[:, model_width:], preferred_element_type=jnp.float32
    ).astype(jnp.bfloat16)
    key_values = key_values.reshape(key_count, 2, HEADS, head_size)
    scores = jnp.einsum(
        "qhd,khd->hqk", queries, key_values[:, 0], preferred_element_type=jnp.float32
    ) / math.sqrt(head_size)
    alive_keys = (key_marks > 0)[None, None, :]
    masked = jnp.where(alive_keys, scores, NEG)
    row_top = jnp.max(masked, axis=-1, keepdims=True)
    weights_exp = jnp.where(alive_keys, jnp.exp(masked - row_top), 0.0)
    totals = jnp.sum(weights_exp, axis=-1)
    weighted = jnp.einsum(
        "hqk,khd->hqd",
        weights_exp.astype(jnp.bfloat16),
        key_values[:, 1],
        preferred_element_type=jnp.float32,
    )
    attended = (weighted / totals[..., None]).astype(jnp.bfloat16)
    return jnp.transpose(attended, (1, 0, 2)).reshape(query_count, model_width)


def per_device(
    train_cells,
    test_cells,
    train_mask,
    test_mask,
    feat_qkv,
    feat_out,
    feat_gain,
    feat_bias,
    item_qkv,
    item_out,
    item_gain,
    item_bias,
    mlp_in,
    mlp_out,
    mlp_gain,
    mlp_bias,
):
    train_count = train_cells.shape[0]
    row_count = train_count + test_cells.shape[0]
    feat_count, model_width = train_cells.shape[1], train_cells.shape[2]
    both_rows = jnp.concatenate([train_cells, test_cells], axis=0)
    settled = feature_block(both_rows, feat_qkv, feat_out, feat_gain, feat_bias)
    marks = jnp.concatenate([train_mask, test_mask], axis=0).astype(jnp.bfloat16)
    mark_row = jnp.pad(jnp.transpose(marks), ((0, 0), (0, model_width - row_count)))
    outbound = jnp.concatenate(
        [jnp.swapaxes(settled, 0, 1), mark_row[:, None, :]], axis=1
    )
    inbound = lax.all_to_all(outbound, "rows", split_axis=0, concat_axis=0, tiled=True)
    source_count = inbound.shape[0]
    col_rows = inbound[:, :row_count, :]
    col_marks = inbound[:, row_count, :row_count]
    train_rows = col_rows[:, :train_count].reshape(source_count * train_count, model_width)
    train_marks = col_marks[:, :train_count].reshape(source_count * train_count)
    local_keys = train_rows.shape[0]
    key_mark_row = jnp.pad(train_marks, (0, model_width - local_keys))
    gathered = lax.all_gather(
        jnp.concatenate([train_rows, key_mark_row[None, :]], axis=0), "feat", axis=0
    )
    key_rows = gathered[:, :local_keys].reshape(-1, model_width)
    key_marks = gathered[:, local_keys, :local_keys].reshape(-1)

    query_rows = col_rows.reshape(source_count * row_count, model_width)
    attended = item_attention(query_rows, key_rows, key_marks, item_qkv)
    branch = jnp.dot(attended, item_out, preferred_element_type=jnp.float32)
    is_train = (jnp.arange(row_count) < train_count)[None, :]
    keep_gate = jnp.where(is_train, jnp.ones_like(col_marks), col_marks).astype(jnp.float32)
    branch = branch * keep_gate.reshape(-1, 1)
    settled_item = layer_norm(
        query_rows.astype(jnp.float32) + branch, item_gain, item_bias
    ).astype(jnp.bfloat16)
    hidden_units = jax.nn.gelu(
        jnp.dot(settled_item, mlp_in, preferred_element_type=jnp.float32), approximate=False
    ).astype(jnp.bfloat16)
    result_rows = layer_norm(
        settled_item.astype(jnp.float32)
        + jnp.dot(hidden_units, mlp_out, preferred_element_type=jnp.float32),
        mlp_gain,
        mlp_bias,
    ).astype(jnp.bfloat16)
    result_rows = result_rows.reshape(source_count, row_count, model_width)
    returned = lax.all_to_all(result_rows, "rows", split_axis=0, concat_axis=0, tiled=True)
    final = jnp.swapaxes(returned, 0, 1)
    return (final[:train_count], final[train_count:])


def solution(mesh):
    return jax.shard_map(
        per_device,
        mesh=mesh,
        in_specs=(
            P(("rows", "feat"), None, None),
            P(("rows", "feat"), None, None),
            P(("rows", "feat"), None),
            P(("rows", "feat"), None),
            P(),
            P(),
            P(),
            P(),
            P(),
            P(),
            P(),
            P(),
            P(),
            P(),
            P(),
            P(),
        ),
        out_specs=(P(("rows", "feat"), None, None), P(("rows", "feat"), None, None)),
        check_vma=False,
    )
```

time: 147 us -> 89.1 us (0.61)
  starting transfers between devices: 54.6 us -> 12.9 us
  waiting for transfers between devices: 26.4 us -> 10.1 us
  matrix products: 10.8 us -> 15.6 us
  blocking collectives: 35.4 us -> 40.1 us
  other arithmetic: 7.46 us -> 2.89 us
  local copies, waits for them, and re-layouts: 10.4 us -> 5.92 us
    all_to_all x6 -> x1, starting transfers between devices: 54.6 us -> 12.9 us  [per_device(): lax.all_to_all(outbound, 'rows', split_axis=0, concat_axis=0, tiled=True)]
    all_to_all x0 -> x1, blocking collectives: none -> 17.5 us  [per_device(): lax.all_to_all(result_rows, 'rows', split_axis=0, concat_axis=0, tiled=True)]
    all_to_all x6 -> x1, waiting for transfers between devices: 26.4 us -> 10.1 us  [per_device(): lax.all_to_all(outbound, 'rows', split_axis=0, concat_axis=0, tiled=True)]
    all_gather x2 -> x1, blocking collectives: 35.4 us -> 22.6 us  [per_device(): lax.all_gather(jnp.concatenate([train_rows, key_mark_row[None, :]], axis=...]
    sub x0 -> x1, matrix products: none -> 5.01 us  [item_attention(): weights_exp = jnp.where(alive_keys, jnp.exp(masked - row_top), 0.0)]
    reduce_sum x1 -> x0, other arithmetic: 2.73 us -> none  [absorb_keys(): totals = totals * factor + jnp.sum(weights_exp, axis=-1)]
    slice x12 -> x8, local copies, waits for them, and re-layouts: 2.67 us -> 0.45 us  [the longest x1 0.13 us: per_device(): col_marks = inbound[:, row_count, :row_count]]
    all_to_all x4 -> x0, other arithmetic: 1.94 us -> none  [the longest x1 0.81 us: per_device(): lax.all_to_all(done_test, 'rows', split_axis=0, concat_axis=1, tiled=True)]
  transfers between devices with their start and end apart: 6 -> 1, of which waited for: 4 -> 1; matrix products, arithmetic and copies ran while one was open for 8% -> 0% of each run, Pallas kernels for 0% -> 0%
where the time goes in v1:
time: 89.1 us; the launch traced here: 88.7 us
  blocking collectives  40.1 us (45%)
  matrix products  15.6 us (18%)
  starting transfers between devices  12.9 us (14%)
  waiting for transfers between devices  10.1 us (11%)
  local copies, waits for them, and re-layouts  5.92 us (7%)
  other arithmetic  2.89 us (3%)
  between operations  1.01 us (1%)
    all_gather x1, blocking collectives, per_device(): lax.all_gather(jnp.concatenate([train_rows, key_mark_row[None, :]], axis=...  22.6 us
    all_to_all x1, blocking collectives, per_device(): lax.all_to_all(result_rows, 'rows', split_axis=0, concat_axis=0, tiled=True)  17.5 us
    all_to_all x1, starting transfers between devices, per_device(): lax.all_to_all(outbound, 'rows', split_axis=0, concat_axis=0, tiled=True)  12.9 us
    all_to_all x1, waiting for transfers between devices, per_device(): lax.all_to_all(outbound, 'rows', split_axis=0, concat_axis=0, tiled=True)  10.1 us
    sub x1, matrix products, item_attention(): weights_exp = jnp.where(alive_keys, jnp.exp(masked - row_top), 0.0)  5.01 us
    dot_general x1, matrix products, item_attention(): jnp.einsum('hqk,khd->hqd', weights_exp.astype(jnp.bfloat16), key_values[:...  3.89 us
    dot_general x1, matrix products, per_device(): jnp.dot(hidden_units, mlp_out, preferred_element_type=jnp.float32)  3.22 us
    unnamed x25, local copies, waits for them, and re-layouts  1.83 us
  transfers between devices with their start and end apart: 1, of which 1 were waited for; matrix products, arithmetic and copies ran while one was open for 0% of the time, Pallas kernels for 0%

profile of v1, /device:TPU:1, one launch (start us, length us, event | category | flops | bytes accessed | tf_op | source)
XLA Modules:
  0.0 88.7 jit_solution(321282915551362572)
XLA Ops:
  0.6 0.7 convert.6
  1.4 0.7 convert.7
  2.2 0.9 %pad_maximum_fusion.1 = bf16[6,64,192]{2,1,0:T(8,128)(2,1)S(1)} fusion(bf16[4,64,192]{2,1,0:T(8,128)(2,1)} %param.17, bf16[2,64,192]{2,1,0:T(8,128)(2,1)} %param.16), kind=kLoop, calls=%fused_computation.90 | loop fusion | flops 73728 | bytes 294912 | tf_op jit(solution)/shard_map/concatenate | solution.py:97
  3.1 0.1 copy.56
  3.3 1.3 %convolution_convert_fusion.1 = bf16[384,576]{0,1:T(8,128)(2,1)S(1)} fusion(bf16[384,192]{1,0:T(8,128)(2,1)S(1)} %bitcast.82, bf16[192,576]{1,0:T(8,128)(2,1)} %param.20), kind=kOutput, calls=%fused_computation.15 | convolution fusion | flops 85155840 | bytes 811008 | tf_op jit(solution)/shard_map/dot_general | solution.py:26
  4.6 0.6 reshape.111
  5.2 0.3 fusion.110
  5.5 0.6 fusion.111
  6.2 0.3 fusion.21
  6.5 0.2 copy.61
  6.7 0.3 reshape.112
  7.0 0.4 copy-done.2
  7.3 0.3 fusion.112
  7.8 0.1 copy.62
  8.0 0.8 copy.64
  8.8 12.9 %all-to-all-start = ((bf16[64,7,192]{2,1,0:T(8,128)(2,1)}), bf16[64,7,192]{2,1,0:T(8,128)(2,1)S(1)}, u32[]{:S(2)}, u32[]{:S(2)}) async-start(bf16[64,7,192]{2,1,0:T(8,128)(2,1)} %copy.64), calls=%async_computation | async-start | bytes 524288 | tf_op jit(solution)/shard_map/all_to_all | solution.py:104
  21.8 0.1 broadcast_in_dim.61
  22.0 10.1 %all-to-all-done = bf16[64,7,192]{2,1,0:T(8,128)(2,1)S(1)} async-done(((bf16[64,7,192]{2,1,0:T(8,128)(2,1)}), bf16[64,7,192]{2,1,0:T(8,128)(2,1)S(1)}, u32[]{:S(2)}, u32[]{:S(2)}) %all-to-all-start) | async-done | bytes 172064 | tf_op jit(solution)/shard_map/all_to_all | solution.py:104
  32.4 0.2 reshape.116
  32.8 22.6 %all-gather.1 = bf16[8,129,192]{2,1,0:T(8,128)(2,1)S(1)} all-gather(bf16[1,129,192]{2,1,0:T(8,128)(2,1)S(1)} %maximum_bitcast_fusion), channel_id=2, replica_groups=mesh['rows'=64,'feat'=8] {'feat'}, dimensions={0}, use_global_device_ids=true | all-gather | bytes 445824 | tf_op jit(solution)/shard_map/all_gather | solution.py:112
  55.4 0.1 squeeze.26
  55.7 0.1 copy.65
  55.8 0.3 convolution_convert_fusion.3
  56.1 0.5 convolution_convert_fusion
  56.7 5.0 %fusion.113 = (f32[6,384]{1,0:T(8,128)S(1)}, bf16[6,384,1024]{2,1,0:T(8,128)(2,1)}) fusion(pred[1024]{0:T(1024)(128)(4,1)S(1)} %compare_bitcast_fusion, bf16[384,6,32]{0,2,1:T(8,128)(2,1)S(1)} %bitcast.89, bf16[1024,2,6,32]{0,3,2,1:T(8,128)(2,1)S(1)} %bitcast.86), kind=kOutput, calls=%fused_computation.147 | convolution fusion | flops 165151744 | bytes 5270528 | tf_op jit(solution)/shard_map/sub | solution.py:64
  61.7 3.9 %fusion.30 = bf16[384,6,32]{0,2,1:T(8,128)(2,1)S(1)} fusion(bf16[6,384,1024]{2,1,0:T(8,128)(2,1)} %get-tuple-element.18, bf16[1024,2,6,32]{0,3,2,1:T(8,128)(2,1)S(1)} %bitcast.87, f32[384,6]{0,1:T(8,128)S(1)} %bitcast.93), kind=kOutput, calls=%fused_computation.44 | convolution fusion | flops 151142400 | bytes 5271552 | tf_op jit(solution)/shard_map/hqk,khd->hqd/dot_general | solution.py:66
  65.6 0.3 fusion.114
  66.0 3.2 %fusion.115 = (f32[384]{0:T(512)S(1)}, f32[384,192]{0,1:T(8,128)S(1)}) fusion(bf16[768,192]{0,1:T(8,128)(2,1)S(1)} %copy-done, bf16[192,768]{1,0:T(8,128)(2,1)S(1)} %copy-done.8, f32[384,192]{0,1:T(8,128)S(1)} %get-tuple-element.20, f32[192]{0:T(256)S(1)} %copy-done.9, f32[192]{0:T(256)S(1)} %copy-done.10, f32[384]{0:T(512)S(1)} %add_rsqrt_fusion.1, ...), kind=kOutput, calls=%fused_computation.149 | convolution fusion | flops 246619776 | bytes 1185792 | tf_op jit(solution)/shard_map/dot_general | solution.py:132
  69.4 0.1 copy.70
  69.7 17.5 %all_to_all.10 = bf16[64,6,192]{2,1,0:T(8,128)(2,1)S(1)} all-to-all(bf16[64,6,192]{2,1,0:T(8,128)(2,1)S(1)} %reshape.121), channel_id=1, replica_groups=mesh['rows'=64,'feat'=8] {'rows'}, dimensions={0} | all-to-all | bytes 294912 | tf_op jit(solution)/shard_map/all_to_all | solution.py:137
  87.4 0.7 copy.72
  88.0 0.6 copy.71
  (55 shorter events, 1.5 us)
Async XLA Ops:
  0.6 65.3 %copy-start = (bf16[768,192]{0,1:T(8,128)(2,1)S(1)}, bf16[768,192]{0,1:T(8,128)(2,1)}, u32[]{:S(2)}) copy-start(bf16[768,192]{0,1:T(8,128)(2,1)} %param.29) | copy-start | bytes 884740
  6.4 0.9 %copy-start.2 = (bf16[192,192]{1,0:T(8,128)(2,1)S(1)}, bf16[192,192]{1,0:T(8,128)(2,1)}, u32[]{:S(2)}) copy-start(bf16[192,192]{1,0:T(8,128)(2,1)} %param.21) | copy-start | bytes 221188
  6.5 1.2 %copy-start.4 = (f32[192]{0:T(256)S(1)}, f32[192]{0:T(256)}, u32[]{:S(2)}) copy-start(f32[192]{0:T(256)} %param.23) | copy-start | bytes 2308
  6.5 1.2 %copy-start.5 = (f32[192]{0:T(256)S(1)}, f32[192]{0:T(256)}, u32[]{:S(2)}) copy-start(f32[192]{0:T(256)} %param.22) | copy-start | bytes 2308
  8.8 23.3 %all-to-all-start = ((bf16[64,7,192]{2,1,0:T(8,128)(2,1)}), bf16[64,7,192]{2,1,0:T(8,128)(2,1)S(1)}, u32[]{:S(2)}, u32[]{:S(2)}) async-start(bf16[64,7,192]{2,1,0:T(8,128)(2,1)} %copy.64), calls=%async_computation | async-start | bytes 524288 | tf_op jit(solution)/shard_map/all_to_all | solution.py:104
  32.8 23.1 %copy-start.1 = (bf16[192,576]{1,0:T(8,128)(2,1)S(1)}, bf16[192,576]{1,0:T(8,128)(2,1)}, u32[]{:S(2)}) copy-start(bf16[192,576]{1,0:T(8,128)(2,1)} %param.24) | copy-start | bytes 663556
  61.7 3.9 %copy-start.3 = (bf16[192,192]{1,0:T(8,128)(2,1)S(1)}, bf16[192,192]{1,0:T(8,128)(2,1)}, u32[]{:S(2)}) copy-start(bf16[192,192]{1,0:T(8,128)(2,1)} %param.25) | copy-start | bytes 221188
  61.7 4.3 %copy-start.8 = (bf16[192,768]{1,0:T(8,128)(2,1)S(1)}, bf16[192,768]{1,0:T(8,128)(2,1)}, u32[]{:S(2)}) copy-start(bf16[192,768]{1,0:T(8,128)(2,1)} %param.28) | copy-start | bytes 884740
  61.7 4.3 %copy-start.9 = (f32[192]{0:T(256)S(1)}, f32[192]{0:T(256)}, u32[]{:S(2)}) copy-start(f32[192]{0:T(256)} %param.27) | copy-start | bytes 2308
  61.7 4.3 %copy-start.10 = (f32[192]{0:T(256)S(1)}, f32[192]{0:T(256)}, u32[]{:S(2)}) copy-start(f32[192]{0:T(256)} %param.26) | copy-start | bytes 2308
  66.0 3.3 %copy-start.6 = (f32[192]{0:T(256)S(1)}, f32[192]{0:T(256)}, u32[]{:S(2)}) copy-start(f32[192]{0:T(256)} %param.31) | copy-start | bytes 2308
  66.0 3.3 %copy-start.7 = (f32[192]{0:T(256)S(1)}, f32[192]{0:T(256)}, u32[]{:S(2)}) copy-start(f32[192]{0:T(256)} %param.30) | copy-start | bytes 2308

commit v2 on v1

--- a/solution.py
+++ b/solution.py
@@ -3,6 +3,7 @@
 import jax
 import jax.numpy as jnp
 from jax import lax
+from jax.experimental import pallas as pl
 from jax.sharding import PartitionSpec as P
 
 HEADS = 6
@@ -43,6 +44,22 @@
     return settled.astype(jnp.bfloat16).reshape(row_count, feat_count, model_width)
 
 
+def attention_kernel(query_ref, key_ref, value_ref, mark_ref, out_ref):
+    head_size = query_ref.shape[-1]
+    scores = lax.dot_general(
+        query_ref[0], key_ref[0], (((1,), (1,)), ((), ())), preferred_element_type=jnp.float32
+    ) / math.sqrt(head_size)
+    alive_keys = mark_ref[...] > 0
+    masked = jnp.where(alive_keys, scores, NEG)
+    row_top = jnp.max(masked, axis=-1, keepdims=True)
+    weights_exp = jnp.where(alive_keys, jnp.exp(masked - row_top), 0.0)
+    totals = jnp.sum(weights_exp, axis=-1, keepdims=True)
+    weighted = jnp.dot(
+        weights_exp.astype(jnp.bfloat16), value_ref[0], preferred_element_type=jnp.float32
+    )
+    out_ref[0] = (weighted / totals).astype(out_ref.dtype)
+
+
 def item_attention(query_rows, key_rows, key_marks, item_qkv):
     query_count, model_width = query_rows.shape
     key_count = key_rows.shape[0]
@@ -50,26 +67,29 @@
     queries = jnp.dot(
         query_rows, item_qkv[:, :model_width], preferred_element_type=jnp.float32
     ).astype(jnp.bfloat16)
-    queries = queries.reshape(query_count, HEADS, head_size)
+    queries = jnp.transpose(queries.reshape(query_count, HEADS, head_size), (1, 0, 2))
     key_values = jnp.dot(
         key_rows, item_qkv[:, model_width:], preferred_element_type=jnp.float32
     ).astype(jnp.bfloat16)
-    key_values = key_values.reshape(key_count, 2, HEADS, head_size)
-    scores = jnp.einsum(
-        "qhd,khd->hqk", queries, key_values[:, 0], preferred_element_type=jnp.float32
-    ) / math.sqrt(head_size)
-    alive_keys = (key_marks > 0)[None, None, :]
-    masked = jnp.where(alive_keys, scores, NEG)
-    row_top = jnp.max(masked, axis=-1, keepdims=True)
-    weights_exp = jnp.where(alive_keys, jnp.exp(masked - row_top), 0.0)
-    totals = jnp.sum(weights_exp, axis=-1)
-    weighted = jnp.einsum(
-        "hqk,khd->hqd",
-        weights_exp.astype(jnp.bfloat16),
-        key_values[:, 1],
-        preferred_element_type=jnp.float32,
-    )
-    attended = (weighted / totals[..., None]).astype(jnp.bfloat16)
+    key_values = jnp.transpose(key_values.reshape(key_count, 2 * HEADS, head_size), (1, 0, 2))
+    marks = key_marks.astype(jnp.float32).reshape(1, key_count)
+    attended = pl.pallas_call(
+        attention_kernel,
+        grid=(HEADS,),
+        in_specs=[
+            pl.BlockSpec((1, query_count, head_size), lambda h: (h, 0, 0)),
+            pl.BlockSpec((1, key_count, head_size), lambda h: (h, 0, 0)),
+            pl.BlockSpec((1, key_count, head_size), lambda h: (h + HEADS, 0, 0)),
+            pl.BlockSpec((1, key_count), lambda h: (0, 0)),
+        ],
+        out_specs=pl.BlockSpec((1, query_count, head_size), lambda h: (h, 0, 0)),
+        out_shape=jax.ShapeDtypeStruct((HEADS, query_count, head_size), jnp.bfloat16),
+        cost_estimate=pl.CostEstimate(
+            flops=4 * HEADS * query_count * key_count * head_size,
+            transcendentals=HEADS * query_count * key_count,
+            bytes_accessed=2 * (2 * query_count + 2 * key_count) * model_width,
+        ),
+    )(queries, key_values, key_values, marks)
     return jnp.transpose(attended, (1, 0, 2)).reshape(query_count, model_width)
 
 

time: 89.1 us -> 95.3 us (1.070)
  Pallas kernels: 0 us -> 9.53 us
  matrix products: 15.6 us -> 6.76 us
  local copies, waits for them, and re-layouts: 5.92 us -> 11 us
    pallas_call x0 -> x1, Pallas kernels: none -> 9.53 us  [item_attention(): pl.pallas_call(attention_kernel, grid=(HEADS,), in_specs=[pl.BlockSpec((1...]
    sub x1 -> x0, matrix products: 5.01 us -> none  [item_attention(): weights_exp = jnp.where(alive_keys, jnp.exp(masked - row_top), 0.0)]
    dot_general x1 -> x0, matrix products: 3.89 us -> none  [item_attention(): jnp.einsum('hqk,khd->hqd', weights_exp.astype(jnp.bfloat16), key_values[:...]
    reshape x0 -> x2, local copies, waits for them, and re-layouts: none -> 3.78 us  [the longest x1 2.72 us: item_attention(): key_values.reshape(key_count, 2 * HEADS, head_size)]
    transpose x0 -> x1, local copies, waits for them, and re-layouts: none -> 1.33 us  [item_attention(): return jnp.transpose(attended, (1, 0, 2)).reshape(query_count, model_width)]
where the time goes in v2:
time: 95.3 us; the launch traced here: 94.8 us
  blocking collectives  39.9 us (42%)
  starting transfers between devices  12.9 us (14%)
  local copies, waits for them, and re-layouts  11 us (12%)
  waiting for transfers between devices  10.1 us (11%)
  Pallas kernels  9.53 us (10%)
  matrix products  6.76 us (7%)
  other arithmetic  3.48 us (4%)
  between operations  1 us (1%)
    all_gather x1, blocking collectives, per_device(): lax.all_gather(jnp.concatenate([train_rows, key_mark_row[None, :]], axis=...  22.4 us
    all_to_all x1, blocking collectives, per_device(): lax.all_to_all(result_rows, 'rows', split_axis=0, concat_axis=0, tiled=True)  17.5 us
    all_to_all x1, starting transfers between devices, per_device(): lax.all_to_all(outbound, 'rows', split_axis=0, concat_axis=0, tiled=True)  12.9 us
    all_to_all x1, waiting for transfers between devices, per_device(): lax.all_to_all(outbound, 'rows', split_axis=0, concat_axis=0, tiled=True)  10.1 us
    pallas_call x1, Pallas kernels, item_attention(): pl.pallas_call(attention_kernel, grid=(HEADS,), in_specs=[pl.BlockSpec((1...  9.53 us
    dot_general x1, matrix products, per_device(): jnp.dot(hidden_units, mlp_out, preferred_element_type=jnp.float32)  3.22 us
    reshape x1, local copies, waits for them, and re-layouts, item_attention(): key_values.reshape(key_count, 2 * HEADS, head_size)  2.72 us
  transfers between devices with their start and end apart: 1, of which 1 were waited for; matrix products, arithmetic and copies ran while one was open for 0% of the time, Pallas kernels for 0%

profile of v2, /device:TPU:1, one launch (start us, length us, event | category | flops | bytes accessed | tf_op | source)
XLA Modules:
  0.0 94.8 jit_solution(15899073285572016278)
XLA Ops:
  0.6 0.7 convert.7
  1.4 0.7 convert.8
  2.2 0.9 pad_maximum_fusion.1
  3.3 1.3 %convolution_convert_fusion.1 = bf16[384,576]{0,1:T(8,128)(2,1)S(1)} fusion(bf16[384,192]{1,0:T(8,128)(2,1)S(1)} %bitcast.68, bf16[192,576]{1,0:T(8,128)(2,1)} %param.20), kind=kOutput, calls=%fused_computation.6 | convolution fusion | flops 85155840 | bytes 811008 | tf_op jit(solution)/shard_map/dot_general | solution.py:27
  4.6 0.6 reshape.115
  5.2 0.3 fusion.90
  5.5 0.6 fusion.91
  6.2 0.3 fusion.14
  6.5 0.2 copy.68
  6.7 0.3 reshape.116
  7.0 0.4 copy-done.2
  7.3 0.3 fusion.92
  7.8 0.1 copy.69
  8.0 0.8 copy.71
  8.9 12.9 %all-to-all-start = ((bf16[64,7,192]{2,1,0:T(8,128)(2,1)}), bf16[64,7,192]{2,1,0:T(8,128)(2,1)S(1)}, u32[]{:S(2)}, u32[]{:S(2)}) async-start(bf16[64,7,192]{2,1,0:T(8,128)(2,1)} %copy.71), calls=%async_computation | async-start | bytes 524288 | tf_op jit(solution)/shard_map/all_to_all | solution.py:124
  21.8 0.1 broadcast_in_dim.19
  22.0 10.1 %all-to-all-done = bf16[64,7,192]{2,1,0:T(8,128)(2,1)S(1)} async-done(((bf16[64,7,192]{2,1,0:T(8,128)(2,1)}), bf16[64,7,192]{2,1,0:T(8,128)(2,1)S(1)}, u32[]{:S(2)}, u32[]{:S(2)}) %all-to-all-start) | async-done | bytes 172064 | tf_op jit(solution)/shard_map/all_to_all | solution.py:124
  32.4 0.2 reshape.121
  32.8 22.4 %all-gather.1 = bf16[8,129,192]{2,1,0:T(8,128)(2,1)S(1)} all-gather(bf16[1,129,192]{2,1,0:T(8,128)(2,1)S(1)} %maximum_bitcast_fusion), channel_id=2, replica_groups=mesh['rows'=64,'feat'=8] {'feat'}, dimensions={0}, use_global_device_ids=true | all-gather | bytes 445824 | tf_op jit(solution)/shard_map/all_gather | solution.py:132
  55.2 0.6 fusion.57.mark_ref
  55.8 0.1 squeeze.18
  56.2 0.3 convolution_convert_fusion.3
  56.5 1.1 %copy.73 = bf16[384,6,32]{2,0,1:T(8,128)(2,1)} copy(bf16[384,6,32]{0,2,1:T(8,128)(2,1)S(1)} %bitcast.73) | data formatting | bytes 294912 | tf_op jit(solution)/shard_map/reshape | solution.py:70
  57.6 0.5 convolution_convert_fusion
  58.1 2.7 %copy.77 = bf16[1024,12,32]{2,0,1:T(8,128)(2,1)} copy(bf16[1024,12,32]{0,2,1:T(8,128)(2,1)S(1)} %bitcast.63) | data formatting | bytes 1572864 | tf_op jit(solution)/shard_map/reshape | solution.py:74
  60.9 9.5 %shard_map.167 = bf16[6,384,32]{2,1,0:T(8,128)(2,1)} custom-call(bf16[6,384,32]{2,1,0:T(8,128)(2,1)} %bitcast.64, bf16[12,1024,32]{2,1,0:T(8,128)(2,1)} %bitcast.61, bf16[12,1024,32]{2,1,0:T(8,128)(2,1)} %bitcast.62, f32[1,1024]{1,0:T(1,128)} %fusion.57.mark_ref), custom_call_target="tpu_custom_call" | custom-call | flops 301989888 | bytes 1081344 | tf_op jit(solution)/shard_map/pallas_call | solution.py:76
  70.4 1.3 %copy.78 = bf16[384,6,32]{0,2,1:T(8,128)(2,1)S(1)} copy(bf16[384,6,32]{2,0,1:T(8,128)(2,1)} %bitcast.65) | data formatting | bytes 294912 | tf_op jit(solution)/shard_map/transpose | solution.py:93
  71.8 0.3 fusion.93
  72.2 3.2 %fusion.94 = (f32[384]{0:T(512)S(1)}, f32[384,192]{0,1:T(8,128)S(1)}) fusion(bf16[768,192]{0,1:T(8,128)(2,1)S(1)} %copy-done, bf16[192,768]{1,0:T(8,128)(2,1)S(1)} %copy-done.8, f32[384,192]{0,1:T(8,128)S(1)} %get-tuple-element.18, f32[192]{0:T(256)S(1)} %copy-done.9, f32[192]{0:T(256)S(1)} %copy-done.10, f32[384]{0:T(512)S(1)} %add_rsqrt_fusion.1, ...), kind=kOutput, calls=%fused_computation.131 | convolution fusion | flops 246619776 | bytes 1185792 | tf_op jit(solution)/shard_map/dot_general | solution.py:152
  75.8 17.5 %all_to_all.10 = bf16[64,6,192]{2,1,0:T(8,128)(2,1)S(1)} all-to-all(bf16[64,6,192]{2,1,0:T(8,128)(2,1)S(1)} %reshape.125), channel_id=1, replica_groups=mesh['rows'=64,'feat'=8] {'rows'}, dimensions={0} | all-to-all | bytes 294912 | tf_op jit(solution)/shard_map/all_to_all | solution.py:157
  93.5 0.7 copy.82
  94.1 0.6 copy.81
  (56 shorter events, 1.9 us)
Async XLA Ops:
  0.6 71.5 %copy-start = (bf16[768,192]{0,1:T(8,128)(2,1)S(1)}, bf16[768,192]{0,1:T(8,128)(2,1)}, u32[]{:S(2)}) copy-start(bf16[768,192]{0,1:T(8,128)(2,1)} %param.29) | copy-start | bytes 884740
  6.4 0.9 copy-start.2
  6.5 1.2 %copy-start.4 = (f32[192]{0:T(256)S(1)}, f32[192]{0:T(256)}, u32[]{:S(2)}) copy-start(f32[192]{0:T(256)} %param.23) | copy-start | bytes 2308
  6.5 1.2 %copy-start.5 = (f32[192]{0:T(256)S(1)}, f32[192]{0:T(256)}, u32[]{:S(2)}) copy-start(f32[192]{0:T(256)} %param.22) | copy-start | bytes 2308
  8.9 23.3 %all-to-all-start = ((bf16[64,7,192]{2,1,0:T(8,128)(2,1)}), bf16[64,7,192]{2,1,0:T(8,128)(2,1)S(1)}, u32[]{:S(2)}, u32[]{:S(2)}) async-start(bf16[64,7,192]{2,1,0:T(8,128)(2,1)} %copy.71), calls=%async_computation | async-start | bytes 524288 | tf_op jit(solution)/shard_map/all_to_all | solution.py:124
  32.8 23.5 %copy-start.1 = (bf16[192,576]{1,0:T(8,128)(2,1)S(1)}, bf16[192,576]{1,0:T(8,128)(2,1)}, u32[]{:S(2)}) copy-start(bf16[192,576]{1,0:T(8,128)(2,1)} %param.24) | copy-start | bytes 663556
  60.8 10.9 %copy-start.3 = (bf16[192,192]{1,0:T(8,128)(2,1)S(1)}, bf16[192,192]{1,0:T(8,128)(2,1)}, u32[]{:S(2)}) copy-start(bf16[192,192]{1,0:T(8,128)(2,1)} %param.25) | copy-start | bytes 221188
  70.4 1.7 %copy-start.8 = (bf16[192,768]{1,0:T(8,128)(2,1)S(1)}, bf16[192,768]{1,0:T(8,128)(2,1)}, u32[]{:S(2)}) copy-start(bf16[192,768]{1,0:T(8,128)(2,1)} %param.28) | copy-start | bytes 884740
  70.4 1.7 %copy-start.9 = (f32[192]{0:T(256)S(1)}, f32[192]{0:T(256)}, u32[]{:S(2)}) copy-start(f32[192]{0:T(256)} %param.27) | copy-start | bytes 2308
  70.4 1.7 %copy-start.10 = (f32[192]{0:T(256)S(1)}, f32[192]{0:T(256)}, u32[]{:S(2)}) copy-start(f32[192]{0:T(256)} %param.26) | copy-start | bytes 2308
  72.1 3.3 %copy-start.6 = (f32[192]{0:T(256)S(1)}, f32[192]{0:T(256)}, u32[]{:S(2)}) copy-start(f32[192]{0:T(256)} %param.31) | copy-start | bytes 2308
  72.2 3.3 %copy-start.7 = (f32[192]{0:T(256)S(1)}, f32[192]{0:T(256)}, u32[]{:S(2)}) copy-start(f32[192]{0:T(256)} %param.30) | copy-start | bytes 2308

commit v3 on v2

--- a/solution.py
+++ b/solution.py
@@ -45,52 +45,51 @@
 
 
 def attention_kernel(query_ref, key_ref, value_ref, mark_ref, out_ref):
-    head_size = query_ref.shape[-1]
+    head_size = query_ref.shape[0]
     scores = lax.dot_general(
-        query_ref[0], key_ref[0], (((1,), (1,)), ((), ())), preferred_element_type=jnp.float32
+        key_ref[...], query_ref[...], (((0,), (0,)), ((), ())), preferred_element_type=jnp.float32
     ) / math.sqrt(head_size)
-    alive_keys = mark_ref[...] > 0
-    masked = jnp.where(alive_keys, scores, NEG)
-    row_top = jnp.max(masked, axis=-1, keepdims=True)
-    weights_exp = jnp.where(alive_keys, jnp.exp(masked - row_top), 0.0)
-    totals = jnp.sum(weights_exp, axis=-1, keepdims=True)
+    masked = jnp.where(mark_ref[...] > 0, scores, NEG)
+    row_top = jnp.max(masked, axis=0, keepdims=True)
+    weights_exp = jnp.exp(masked - row_top)
+    totals = jnp.sum(weights_exp, axis=0, keepdims=True)
     weighted = jnp.dot(
-        weights_exp.astype(jnp.bfloat16), value_ref[0], preferred_element_type=jnp.float32
+        value_ref[...], weights_exp.astype(jnp.bfloat16), preferred_element_type=jnp.float32
     )
-    out_ref[0] = (weighted / totals).astype(out_ref.dtype)
+    out_ref[...] = (weighted / totals).astype(out_ref.dtype)
 
 
 def item_attention(query_rows, key_rows, key_marks, item_qkv):
     query_count, model_width = query_rows.shape
     key_count = key_rows.shape[0]
     head_size = model_width // HEADS
-    queries = jnp.dot(
-        query_rows, item_qkv[:, :model_width], preferred_element_type=jnp.float32
+    queries_t = lax.dot_general(
+        item_qkv[:, :model_width], query_rows, (((0,), (1,)), ((), ())),
+        preferred_element_type=jnp.float32,
     ).astype(jnp.bfloat16)
-    queries = jnp.transpose(queries.reshape(query_count, HEADS, head_size), (1, 0, 2))
-    key_values = jnp.dot(
-        key_rows, item_qkv[:, model_width:], preferred_element_type=jnp.float32
+    key_values_t = lax.dot_general(
+        item_qkv[:, model_width:], key_rows, (((0,), (1,)), ((), ())),
+        preferred_element_type=jnp.float32,
     ).astype(jnp.bfloat16)
-    key_values = jnp.transpose(key_values.reshape(key_count, 2 * HEADS, head_size), (1, 0, 2))
-    marks = key_marks.astype(jnp.float32).reshape(1, key_count)
-    attended = pl.pallas_call(
+    marks = key_marks.astype(jnp.float32).reshape(key_count, 1)
+    attended_t = pl.pallas_call(
         attention_kernel,
         grid=(HEADS,),
         in_specs=[
-            pl.BlockSpec((1, query_count, head_size), lambda h: (h, 0, 0)),
-            pl.BlockSpec((1, key_count, head_size), lambda h: (h, 0, 0)),
-            pl.BlockSpec((1, key_count, head_size), lambda h: (h + HEADS, 0, 0)),
-            pl.BlockSpec((1, key_count), lambda h: (0, 0)),
+            pl.BlockSpec((head_size, query_count), lambda h: (h, 0)),
+            pl.BlockSpec((head_size, key_count), lambda h: (h, 0)),
+            pl.BlockSpec((head_size, key_count), lambda h: (h + HEADS, 0)),
+            pl.BlockSpec((key_count, 1), lambda h: (0, 0)),
         ],
-        out_specs=pl.BlockSpec((1, query_count, head_size), lambda h: (h, 0, 0)),
-        out_shape=jax.ShapeDtypeStruct((HEADS, query_count, head_size), jnp.bfloat16),
+        out_specs=pl.BlockSpec((head_size, query_count), lambda h: (h, 0)),
+        out_shape=jax.ShapeDtypeStruct((model_width, query_count), jnp.bfloat16),
         cost_estimate=pl.CostEstimate(
             flops=4 * HEADS * query_count * key_count * head_size,
             transcendentals=HEADS * query_count * key_count,
             bytes_accessed=2 * (2 * query_count + 2 * key_count) * model_width,
         ),
-    )(queries, key_values, key_values, marks)
-    return jnp.transpose(attended, (1, 0, 2)).reshape(query_count, model_width)
+    )(queries_t, key_values_t, key_values_t, marks)
+    return attended_t
 
 
 def per_device(
@@ -136,8 +135,10 @@
     key_marks = gathered[:, local_keys, :local_keys].reshape(-1)
 
     query_rows = col_rows.reshape(source_count * row_count, model_width)
-    attended = item_attention(query_rows, key_rows, key_marks, item_qkv)
-    branch = jnp.dot(attended, item_out, preferred_element_type=jnp.float32)
+    attended_t = item_attention(query_rows, key_rows, key_marks, item_qkv)
+    branch = lax.dot_general(
+        attended_t, item_out, (((0,), (0,)), ((), ())), preferred_element_type=jnp.float32
+    )
     is_train = (jnp.arange(row_count) < train_count)[None, :]
     keep_gate = jnp.where(is_train, jnp.ones_like(col_marks), col_marks).astype(jnp.float32)
     branch = branch * keep_gate.reshape(-1, 1)

time: 95.3 us -> 91.2 us (0.957)
  local copies, waits for them, and re-layouts: 11 us -> 6.96 us
  matrix products: 6.76 us -> 9.21 us
  Pallas kernels: 9.53 us -> 7.7 us
    reshape x2 -> x0, local copies, waits for them, and re-layouts: 3.78 us -> none  [the longest x1 2.72 us: item_attention(): key_values.reshape(key_count, 2 * HEADS, head_size)]
    dot_general x3, matrix products: 1.07 us -> 3.52 us  [the longest x1 1.43 us: item_attention(): lax.dot_general(item_qkv[:, model_width:], key_rows, (((0,), (1,)), ((),...]
    pallas_call x1, Pallas kernels: 9.53 us -> 7.7 us  [item_attention(): pl.pallas_call(attention_kernel, grid=(HEADS,), in_specs=[pl.BlockSpec((h...]
    transpose x1 -> x0, local copies, waits for them, and re-layouts: 1.33 us -> none  [item_attention(): return jnp.transpose(attended, (1, 0, 2)).reshape(query_count, model_width)]
    convert_element_type x0 -> x1, local copies, waits for them, and re-layouts: none -> 1.03 us  [item_attention(): marks = key_marks.astype(jnp.float32).reshape(key_count, 1)]
where the time goes in v3:
time: 91.2 us; the launch traced here: 90.7 us
  blocking collectives  39.9 us (44%)
  starting transfers between devices  12.9 us (14%)
  waiting for transfers between devices  10.1 us (11%)
  matrix products  9.21 us (10%)
  Pallas kernels  7.7 us (8%)
  local copies, waits for them, and re-layouts  6.96 us (8%)
  other arithmetic  2.88 us (3%)
  between operations  0.98 us (1%)
    all_gather x1, blocking collectives, per_device(): lax.all_gather(jnp.concatenate([train_rows, key_mark_row[None, :]], axis=...  22.4 us
    all_to_all x1, blocking collectives, per_device(): lax.all_to_all(result_rows, 'rows', split_axis=0, concat_axis=0, tiled=True)  17.5 us
    all_to_all x1, starting transfers between devices, per_device(): lax.all_to_all(outbound, 'rows', split_axis=0, concat_axis=0, tiled=True)  12.9 us
    all_to_all x1, waiting for transfers between devices, per_device(): lax.all_to_all(outbound, 'rows', split_axis=0, concat_axis=0, tiled=True)  10.1 us
    pallas_call x1, Pallas kernels, item_attention(): pl.pallas_call(attention_kernel, grid=(HEADS,), in_specs=[pl.BlockSpec((h...  7.7 us
    dot_general x1, matrix products, per_device(): jnp.dot(hidden_units, mlp_out, preferred_element_type=jnp.float32)  3.22 us
    unnamed x25, local copies, waits for them, and re-layouts  1.84 us
  transfers between devices with their start and end apart: 1, of which 1 were waited for; matrix products, arithmetic and copies ran while one was open for 0% of the time, Pallas kernels for 0%

profile of v3, /device:TPU:1, one launch (start us, length us, event | category | flops | bytes accessed | tf_op | source)
XLA Modules:
  0.0 90.7 jit_solution(14031434269920224209)
XLA Ops:
  0.6 0.7 convert.7
  1.4 0.7 convert.8
  2.2 0.9 %pad_maximum_fusion.1 = bf16[6,64,192]{2,1,0:T(8,128)(2,1)S(1)} fusion(bf16[4,64,192]{2,1,0:T(8,128)(2,1)} %param.17, bf16[2,64,192]{2,1,0:T(8,128)(2,1)} %param.16), kind=kLoop, calls=%fused_computation.76 | loop fusion | flops 73728 | bytes 294912 | tf_op jit(solution)/shard_map/concatenate | solution.py:116
  3.1 0.1 copy.61
  3.3 1.3 %convolution_convert_fusion.1 = bf16[384,576]{0,1:T(8,128)(2,1)S(1)} fusion(bf16[384,192]{1,0:T(8,128)(2,1)S(1)} %bitcast.57, bf16[192,576]{1,0:T(8,128)(2,1)} %param.20), kind=kOutput, calls=%fused_computation.7 | convolution fusion | flops 85155840 | bytes 811008 | tf_op jit(solution)/shard_map/dot_general | solution.py:27
  4.6 0.6 reshape.106
  5.2 0.3 fusion.91
  5.5 0.6 fusion.92
  6.2 0.3 fusion.15
  6.5 0.2 copy.66
  6.7 0.3 reshape.107
  7.0 0.4 copy-done.2
  7.3 0.3 fusion.93
  7.8 0.1 copy.67
  8.0 0.8 copy.69
  8.8 12.9 %all-to-all-start = ((bf16[64,7,192]{2,1,0:T(8,128)(2,1)}), bf16[64,7,192]{2,1,0:T(8,128)(2,1)S(1)}, u32[]{:S(2)}, u32[]{:S(2)}) async-start(bf16[64,7,192]{2,1,0:T(8,128)(2,1)} %copy.69), calls=%async_computation | async-start | bytes 524288 | tf_op jit(solution)/shard_map/all_to_all | solution.py:123
  21.8 0.1 broadcast_in_dim.19
  22.0 10.1 %all-to-all-done = bf16[64,7,192]{2,1,0:T(8,128)(2,1)S(1)} async-done(((bf16[64,7,192]{2,1,0:T(8,128)(2,1)}), bf16[64,7,192]{2,1,0:T(8,128)(2,1)S(1)}, u32[]{:S(2)}, u32[]{:S(2)}) %all-to-all-start) | async-done | bytes 172064 | tf_op jit(solution)/shard_map/all_to_all | solution.py:123
  32.4 0.2 reshape.111
  32.8 22.4 %all-gather.1 = bf16[8,129,192]{2,1,0:T(8,128)(2,1)S(1)} all-gather(bf16[1,129,192]{2,1,0:T(8,128)(2,1)S(1)} %maximum_bitcast_fusion), channel_id=2, replica_groups=mesh['rows'=64,'feat'=8] {'feat'}, dimensions={0}, use_global_device_ids=true | all-gather | bytes 445824 | tf_op jit(solution)/shard_map/all_gather | solution.py:131
  55.2 0.1 squeeze.18
  55.5 0.1 copy.70
  55.7 0.9 %fusion.18.query_ref = bf16[192,384]{1,0:T(8,128)(2,1)} fusion(bf16[384,192]{1,0:T(8,128)(2,1)S(1)} %reshape.109, bf16[192,576]{1,0:T(8,128)(2,1)S(1)} %copy-done.1), kind=kOutput, calls=%fused_computation.35 | convolution fusion | flops 28385280 | bytes 442368 | tf_op jit(solution)/shard_map/dot_general | solution.py:66
  56.6 1.4 %fusion.3.key_ref.value_ref = bf16[384,1024]{1,0:T(8,128)(2,1)} fusion(bf16[1024,192]{1,0:T(8,128)(2,1)S(1)} %bitcast.55, bf16[192,576]{1,0:T(8,128)(2,1)S(1)} %copy-done.1), kind=kOutput, calls=%fused_computation.6 | convolution fusion | flops 151388160 | bytes 1458176 | tf_op jit(solution)/shard_map/dot_general | solution.py:70
  58.0 1.0 %copy.76.mark_ref = f32[1024,1]{1,0:T(8,128)} copy(f32[1024,1]{0,1:T(1,128)S(1)} %bitcast.63) | data formatting | bytes 8192 | tf_op jit(solution)/shard_map/convert_element_type | solution.py:74
  59.1 7.7 %shard_map.167 = bf16[192,384]{1,0:T(8,128)(2,1)} custom-call(bf16[192,384]{1,0:T(8,128)(2,1)} %fusion.18.query_ref, bf16[384,1024]{1,0:T(8,128)(2,1)} %fusion.3.key_ref.value_ref, bf16[384,1024]{1,0:T(8,128)(2,1)} %fusion.3.key_ref.value_ref, f32[1024,1]{1,0:T(8,128)} %copy.76.mark_ref), custom_call_target="tpu_custom_call" | custom-call | flops 301989888 | bytes 1081344 | tf_op jit(solution)/shard_map/pallas_call | solution.py:75
  66.8 1.2 %fusion.94 = (f32[384]{0:T(512)S(1)}, f32[384,192]{0,1:T(8,128)S(1)}) fusion(f32[384]{0:T(512)S(1)} %select_convert_fusion, bf16[192,384]{1,0:T(8,128)(2,1)} %shard_map.167, bf16[192,192]{1,0:T(8,128)(2,1)S(1)} %copy-done.3, bf16[384,192]{0,1:T(8,128)(2,1)S(1)} %copy.70), kind=kOutput, calls=%fused_computation.131 | convolution fusion | flops 28606080 | bytes 666624 | tf_op jit(solution)/shard_map/dot_general | solution.py:139
  68.1 3.2 %fusion.95 = (f32[384]{0:T(512)S(1)}, f32[384,192]{0,1:T(8,128)S(1)}) fusion(bf16[768,192]{0,1:T(8,128)(2,1)S(1)} %copy-done, bf16[192,768]{1,0:T(8,128)(2,1)S(1)} %copy-done.8, f32[384,192]{0,1:T(8,128)S(1)} %get-tuple-element.18, f32[192]{0:T(256)S(1)} %copy-done.9, f32[192]{0:T(256)S(1)} %copy-done.10, f32[384]{0:T(512)S(1)} %add_rsqrt_fusion.1, ...), kind=kOutput, calls=%fused_computation.132 | convolution fusion | flops 246619776 | bytes 1185792 | tf_op jit(solution)/shard_map/dot_general | solution.py:153
  71.5 0.1 copy.78
  71.8 17.5 %all_to_all.10 = bf16[64,6,192]{2,1,0:T(8,128)(2,1)S(1)} all-to-all(bf16[64,6,192]{2,1,0:T(8,128)(2,1)S(1)} %reshape.113), channel_id=1, replica_groups=mesh['rows'=64,'feat'=8] {'rows'}, dimensions={0} | all-to-all | bytes 294912 | tf_op jit(solution)/shard_map/all_to_all | solution.py:158
  89.4 0.7 copy.80
  90.1 0.6 copy.79
  (55 shorter events, 1.5 us)
Async XLA Ops:
  0.6 67.4 %copy-start = (bf16[768,192]{0,1:T(8,128)(2,1)S(1)}, bf16[768,192]{0,1:T(8,128)(2,1)}, u32[]{:S(2)}) copy-start(bf16[768,192]{0,1:T(8,128)(2,1)} %param.29) | copy-start | bytes 884740
  6.4 0.9 copy-start.2
  6.5 1.2 %copy-start.4 = (f32[192]{0:T(256)S(1)}, f32[192]{0:T(256)}, u32[]{:S(2)}) copy-start(f32[192]{0:T(256)} %param.23) | copy-start | bytes 2308
  6.5 1.2 %copy-start.5 = (f32[192]{0:T(256)S(1)}, f32[192]{0:T(256)}, u32[]{:S(2)}) copy-start(f32[192]{0:T(256)} %param.22) | copy-start | bytes 2308
  8.8 23.3 %all-to-all-start = ((bf16[64,7,192]{2,1,0:T(8,128)(2,1)}), bf16[64,7,192]{2,1,0:T(8,128)(2,1)S(1)}, u32[]{:S(2)}, u32[]{:S(2)}) async-start(bf16[64,7,192]{2,1,0:T(8,128)(2,1)} %copy.69), calls=%async_computation | async-start | bytes 524288 | tf_op jit(solution)/shard_map/all_to_all | solution.py:123
  32.8 22.9 %copy-start.1 = (bf16[192,576]{1,0:T(8,128)(2,1)S(1)}, bf16[192,576]{1,0:T(8,128)(2,1)}, u32[]{:S(2)}) copy-start(bf16[192,576]{1,0:T(8,128)(2,1)} %param.24) | copy-start | bytes 663556
  59.0 7.7 %copy-start.3 = (bf16[192,192]{1,0:T(8,128)(2,1)S(1)}, bf16[192,192]{1,0:T(8,128)(2,1)}, u32[]{:S(2)}) copy-start(bf16[192,192]{1,0:T(8,128)(2,1)} %param.25) | copy-start | bytes 221188
  59.0 9.0 %copy-start.8 = (bf16[192,768]{1,0:T(8,128)(2,1)S(1)}, bf16[192,768]{1,0:T(8,128)(2,1)}, u32[]{:S(2)}) copy-start(bf16[192,768]{1,0:T(8,128)(2,1)} %param.28) | copy-start | bytes 884740
  59.0 9.0 %copy-start.9 = (f32[192]{0:T(256)S(1)}, f32[192]{0:T(256)}, u32[]{:S(2)}) copy-start(f32[192]{0:T(256)} %param.27) | copy-start | bytes 2308
  59.1 9.0 %copy-start.10 = (f32[192]{0:T(256)S(1)}, f32[192]{0:T(256)}, u32[]{:S(2)}) copy-start(f32[192]{0:T(256)} %param.26) | copy-start | bytes 2308
  68.1 3.3 %copy-start.6 = (f32[192]{0:T(256)S(1)}, f32[192]{0:T(256)}, u32[]{:S(2)}) copy-start(f32[192]{0:T(256)} %param.31) | copy-start | bytes 2308
  68.1 3.3 %copy-start.7 = (f32[192]{0:T(256)S(1)}, f32[192]{0:T(256)}, u32[]{:S(2)}) copy-start(f32[192]{0:T(256)} %param.30) | copy-start | bytes 2308

commit v4 on v1

--- a/solution.py
+++ b/solution.py
@@ -23,54 +23,60 @@
     row_count, feat_count, model_width = cell_rows.shape
     head_size = model_width // HEADS
     flat_rows = cell_rows.reshape(row_count * feat_count, model_width)
-    packed = jnp.dot(flat_rows, qkv_weight, preferred_element_type=jnp.float32).astype(jnp.bfloat16)
-    packed = packed.reshape(row_count, feat_count, 3, HEADS, head_size)
+    head_weights = qkv_weight.reshape(model_width, 3, HEADS, head_size)
+    packed = jnp.einsum(
+        "rfc,cthd->trhfd", cell_rows, head_weights, preferred_element_type=jnp.float32
+    ).astype(jnp.bfloat16)
     scores = jnp.einsum(
-        "rqhd,rkhd->rhqk", packed[:, :, 0], packed[:, :, 1], preferred_element_type=jnp.float32
+        "rhqd,rhkd->rhqk", packed[0], packed[1], preferred_element_type=jnp.float32
     ) / math.sqrt(head_size)
     row_top = jnp.max(scores, axis=-1, keepdims=True)
     weights_exp = jnp.exp(scores - row_top)
     weights = (weights_exp / jnp.sum(weights_exp, axis=-1, keepdims=True)).astype(jnp.bfloat16)
     attended = jnp.einsum(
-        "rhqk,rkhd->rqhd", weights, packed[:, :, 2], preferred_element_type=jnp.float32
+        "rhqk,rhkd->rhqd", weights, packed[2], preferred_element_type=jnp.float32
     ).astype(jnp.bfloat16)
-    branch = jnp.dot(
-        attended.reshape(row_count * feat_count, model_width),
-        out_weight,
+    branch = jnp.einsum(
+        "rhqd,hde->rqe",
+        attended,
+        out_weight.reshape(HEADS, head_size, model_width),
         preferred_element_type=jnp.float32,
-    )
+    ).reshape(row_count * feat_count, model_width)
     settled = layer_norm(flat_rows.astype(jnp.float32) + branch, norm_gain, norm_bias)
     return settled.astype(jnp.bfloat16).reshape(row_count, feat_count, model_width)
 
 
-def item_attention(query_rows, key_rows, key_marks, item_qkv):
-    query_count, model_width = query_rows.shape
-    key_count = key_rows.shape[0]
+def item_attention(query_rows, key_rows, key_marks, item_qkv, item_out):
+    model_width = query_rows.shape[1]
     head_size = model_width // HEADS
-    queries = jnp.dot(
-        query_rows, item_qkv[:, :model_width], preferred_element_type=jnp.float32
+    query_weights = item_qkv[:, :model_width].reshape(model_width, HEADS, head_size)
+    pair_weights = item_qkv[:, model_width:].reshape(model_width, 2, HEADS, head_size)
+    queries = jnp.einsum(
+        "nc,chd->hnd", query_rows, query_weights, preferred_element_type=jnp.float32
     ).astype(jnp.bfloat16)
-    queries = queries.reshape(query_count, HEADS, head_size)
-    key_values = jnp.dot(
-        key_rows, item_qkv[:, model_width:], preferred_element_type=jnp.float32
+    key_values = jnp.einsum(
+        "kc,cthd->thkd", key_rows, pair_weights, preferred_element_type=jnp.float32
     ).astype(jnp.bfloat16)
-    key_values = key_values.reshape(key_count, 2, HEADS, head_size)
     scores = jnp.einsum(
-        "qhd,khd->hqk", queries, key_values[:, 0], preferred_element_type=jnp.float32
+        "hnd,hkd->hnk", queries, key_values[0], preferred_element_type=jnp.float32
     ) / math.sqrt(head_size)
-    alive_keys = (key_marks > 0)[None, None, :]
-    masked = jnp.where(alive_keys, scores, NEG)
+    masked = jnp.where((key_marks > 0)[None, None, :], scores, NEG)
     row_top = jnp.max(masked, axis=-1, keepdims=True)
-    weights_exp = jnp.where(alive_keys, jnp.exp(masked - row_top), 0.0)
+    weights_exp = jnp.exp(masked - row_top)
     totals = jnp.sum(weights_exp, axis=-1)
     weighted = jnp.einsum(
-        "hqk,khd->hqd",
+        "hnk,hkd->hnd",
         weights_exp.astype(jnp.bfloat16),
-        key_values[:, 1],
+        key_values[1],
         preferred_element_type=jnp.float32,
     )
     attended = (weighted / totals[..., None]).astype(jnp.bfloat16)
-    return jnp.transpose(attended, (1, 0, 2)).reshape(query_count, model_width)
+    return jnp.einsum(
+        "hnd,hde->ne",
+        attended,
+        item_out.reshape(HEADS, head_size, model_width),
+        preferred_element_type=jnp.float32,
+    )
 
 
 def per_device(
@@ -116,8 +122,7 @@
     key_marks = gathered[:, local_keys, :local_keys].reshape(-1)
 
     query_rows = col_rows.reshape(source_count * row_count, model_width)
-    attended = item_attention(query_rows, key_rows, key_marks, item_qkv)
-    branch = jnp.dot(attended, item_out, preferred_element_type=jnp.float32)
+    branch = item_attention(query_rows, key_rows, key_marks, item_qkv, item_out)
     is_train = (jnp.arange(row_count) < train_count)[None, :]
     keep_gate = jnp.where(is_train, jnp.ones_like(col_marks), col_marks).astype(jnp.float32)
     branch = branch * keep_gate.reshape(-1, 1)

time: 89.1 us -> 90.6 us (1.017)
  local copies, waits for them, and re-layouts: 5.92 us -> 9.13 us
  matrix products: 15.6 us -> 12.4 us
  other arithmetic: 2.89 us -> 4.44 us
    sub x1 -> x0, matrix products: 5.01 us -> none  [item_attention(): weights_exp = jnp.where(alive_keys, jnp.exp(masked - row_top), 0.0)]
    unnamed x25 -> x29, local copies, waits for them, and re-layouts: 1.83 us -> 5.03 us
    reduce_sum x0 -> x1, other arithmetic: none -> 2.35 us  [item_attention(): totals = jnp.sum(weights_exp, axis=-1)]
    reshape x3 -> x0, local copies, waits for them, and re-layouts: 1.04 us -> none  [the longest x1 0.63 us: feature_block(): packed = packed.reshape(row_count, feat_count, 3, HEADS, head_size)]
    dot_general x7 -> x5, matrix products: 6.8 us -> 7.75 us  [the longest x1 5.19 us: item_attention(): jnp.einsum('hnd,hde->ne', attended, item_out.reshape(HEADS, head_size, mo...]
    concatenate x1 -> x0, other arithmetic: 0.94 us -> none  [per_device(): both_rows = jnp.concatenate([train_cells, test_cells], axis=0)]
    concatenate x0 -> x1, local copies, waits for them, and re-layouts: none -> 0.92 us  [per_device(): both_rows = jnp.concatenate([train_cells, test_cells], axis=0)]
where the time goes in v4:
time: 90.6 us; the launch traced here: 90.1 us
  blocking collectives  40 us (44%)
  starting transfers between devices  12.9 us (14%)
  matrix products  12.4 us (14%)
  waiting for transfers between devices  10.1 us (11%)
  local copies, waits for them, and re-layouts  9.13 us (10%)
  other arithmetic  4.44 us (5%)
  between operations  1.01 us (1%)
    all_gather x1, blocking collectives, per_device(): lax.all_gather(jnp.concatenate([train_rows, key_mark_row[None, :]], axis=...  22.6 us
    all_to_all x1, blocking collectives, per_device(): lax.all_to_all(result_rows, 'rows', split_axis=0, concat_axis=0, tiled=True)  17.4 us
    all_to_all x1, starting transfers between devices, per_device(): lax.all_to_all(outbound, 'rows', split_axis=0, concat_axis=0, tiled=True)  12.9 us
    all_to_all x1, waiting for transfers between devices, per_device(): lax.all_to_all(outbound, 'rows', split_axis=0, concat_axis=0, tiled=True)  10.1 us
    dot_general x1, matrix products, item_attention(): jnp.einsum('hnd,hde->ne', attended, item_out.reshape(HEADS, head_size, mo...  5.19 us
    unnamed x29, local copies, waits for them, and re-layouts  5.03 us
    dot_general x1, matrix products, per_device(): jnp.dot(hidden_units, mlp_out, preferred_element_type=jnp.float32)  3.22 us
    reduce_sum x1, other arithmetic, item_attention(): totals = jnp.sum(weights_exp, axis=-1)  2.35 us
  transfers between devices with their start and end apart: 1, of which 1 were waited for; matrix products, arithmetic and copies ran while one was open for 0% of the time, Pallas kernels for 0%

profile of v4, /device:TPU:1, one launch (start us, length us, event | category | flops | bytes accessed | tf_op | source)
XLA Modules:
  0.0 90.1 jit_solution(11013953881888724682)
XLA Ops:
  0.6 0.7 convert.7
  1.4 0.7 convert.8
  2.2 0.8 constant_dynamic-update-slice_fusion.1
  3.0 1.1 %copy.58 = bf16[192,576]{0,1:T(8,128)(2,1)S(1)} copy(bf16[192,576]{1,0:T(8,128)(2,1)} %param.20) | data formatting | bytes 442368 | tf_op args[4]
  4.1 0.9 %constant_dynamic-update-slice_fusion = bf16[6,64,192]{2,1,0:T(8,128)(2,1)S(1)} fusion(bf16[6,64,192]{2,1,0:T(8,128)(2,1)S(1)} %constant_dynamic-update-slice_fusion.1, bf16[4,64,192]{2,1,0:T(8,128)(2,1)} %param.17), kind=kLoop, calls=%fused_computation.103 | loop fusion | bytes 229376 | tf_op jit(solution)/shard_map/concatenate | solution.py:103
  5.1 0.1 copy.61
  5.3 0.4 fusion.9
  5.7 0.6 fusion.117
  6.3 0.3 fusion.21
  6.6 0.2 copy.60
  6.8 0.3 dot_general.38
  7.1 0.4 copy-done.3
  7.5 0.3 fusion.118
  8.0 0.1 copy.62
  8.2 0.8 copy.64
  9.0 12.9 %all-to-all-start = ((bf16[64,7,192]{2,1,0:T(8,128)(2,1)}), bf16[64,7,192]{2,1,0:T(8,128)(2,1)S(1)}, u32[]{:S(2)}, u32[]{:S(2)}) async-start(bf16[64,7,192]{2,1,0:T(8,128)(2,1)} %copy.64), calls=%async_computation | async-start | bytes 524288 | tf_op jit(solution)/shard_map/all_to_all | solution.py:110
  21.9 0.1 broadcast_in_dim.33
  22.1 10.1 %all-to-all-done = bf16[64,7,192]{2,1,0:T(8,128)(2,1)S(1)} async-done(((bf16[64,7,192]{2,1,0:T(8,128)(2,1)}), bf16[64,7,192]{2,1,0:T(8,128)(2,1)S(1)}, u32[]{:S(2)}, u32[]{:S(2)}) %all-to-all-start) | async-done | bytes 172064 | tf_op jit(solution)/shard_map/all_to_all | solution.py:110
  32.6 0.2 reshape.117
  32.9 22.6 %all-gather.1 = bf16[8,129,192]{2,1,0:T(8,128)(2,1)S(1)} all-gather(bf16[1,129,192]{2,1,0:T(8,128)(2,1)S(1)} %maximum_bitcast_fusion), channel_id=2, replica_groups=mesh['rows'=64,'feat'=8] {'feat'}, dimensions={0}, use_global_device_ids=true | all-gather | bytes 445824 | tf_op jit(solution)/shard_map/all_gather | solution.py:118
  55.5 0.1 squeeze.26
  56.0 0.3 fusion.79
  56.2 0.6 fusion.76
  56.9 1.6 %fusion.1 = (f32[6,384]{1,0:T(8,128)S(1)}, f32[6,384,1024]{2,1,0:T(8,128)S(1)}) fusion(pred[1024]{0:T(1024)(128)(4,1)S(1)} %compare_bitcast_fusion, bf16[2,6,1024,32]{2,3,1,0:T(8,128)(2,1)S(1)} %convert_bitcast_fusion, f32[384,6,32]{0,2,1:T(8,128)S(1)} %bitcast.101), kind=kOutput, calls=%fused_computation.3 | convolution fusion | flops 158144256 | bytes 10135552 | tf_op jit(solution)/shard_map/hnd,hkd->hnk/dot_general | solution.py:60
  58.6 2.3 %fusion.2 = f32[6,384]{1,0:T(8,128)S(1)} fusion(f32[6,384,1024]{2,1,0:T(8,128)S(1)} %get-tuple-element.15, f32[6,384]{1,0:T(8,128)S(1)} %get-tuple-element.14, pred[1024]{0:T(1024)(128)(4,1)S(1)} %compare_bitcast_fusion), kind=kLoop, calls=%fused_computation.4 | loop fusion | flops 9434880 | bytes 9456640 | tf_op jit(solution)/shard_map/reduce_sum | solution.py:66
  60.9 1.3 %copy-done.1 = f32[6,384,1024]{2,1,0:T(8,128)} copy-done((f32[6,384,1024]{2,1,0:T(8,128)}, f32[6,384,1024]{2,1,0:T(8,128)S(1)}, u32[]{:S(2)}) %copy-start.1) | copy-done | bytes 9437208
  62.2 5.2 %fusion.119 = (f32[384]{0:T(512)S(1)}, f32[384,192]{0,1:T(8,128)S(1)}) fusion(f32[384]{0:T(512)S(1)} %select_convert_fusion, bf16[6,32,192]{2,1,0:T(8,128)(2,1)S(1)} %bitcast.109, f32[6,384,1024]{2,1,0:T(8,128)} %copy-done.1, f32[6,384]{1,0:T(8,128)S(1)} %get-tuple-element.14, pred[1024]{0:T(1024)(128)(4,1)S(1)} %compare_bitcast_fusion, ...), kind=kOutput, calls=%fused_computation.152 | convolution fusion | flops 189185664 | bytes 10400256 | tf_op jit(solution)/shard_map/hnd,hde->ne/dot_general | solution.py:74
  67.5 3.2 %fusion.122 = (f32[384]{0:T(512)S(1)}, f32[384,192]{0,1:T(8,128)S(1)}) fusion(bf16[768,192]{0,1:T(8,128)(2,1)S(1)} %copy-done, bf16[192,768]{1,0:T(8,128)(2,1)S(1)} %copy-done.8, f32[384,192]{0,1:T(8,128)S(1)} %get-tuple-element.17, f32[192]{0:T(256)S(1)} %copy-done.10, f32[192]{0:T(256)S(1)} %copy-done.11, f32[384]{0:T(512)S(1)} %add_rsqrt_fusion.1, ...), kind=kOutput, calls=%fused_computation.153 | convolution fusion | flops 246619776 | bytes 1185792 | tf_op jit(solution)/shard_map/dot_general | solution.py:137
  70.9 0.1 copy.74
  71.2 17.4 %all_to_all.10 = bf16[64,6,192]{2,1,0:T(8,128)(2,1)S(1)} all-to-all(bf16[64,6,192]{2,1,0:T(8,128)(2,1)S(1)} %reshape.122), channel_id=1, replica_groups=mesh['rows'=64,'feat'=8] {'rows'}, dimensions={0} | all-to-all | bytes 294912 | tf_op jit(solution)/shard_map/all_to_all | solution.py:142
  88.8 0.7 copy.76
  89.4 0.6 copy.75
  (59 shorter events, 1.8 us)
Async XLA Ops:
  0.6 66.8 %copy-start = (bf16[768,192]{0,1:T(8,128)(2,1)S(1)}, bf16[768,192]{0,1:T(8,128)(2,1)}, u32[]{:S(2)}) copy-start(bf16[768,192]{0,1:T(8,128)(2,1)} %param.29) | copy-start | bytes 884740
  6.6 0.9 copy-start.3
  6.6 1.2 %copy-start.4 = (f32[192]{0:T(256)S(1)}, f32[192]{0:T(256)}, u32[]{:S(2)}) copy-start(f32[192]{0:T(256)} %param.23) | copy-start | bytes 2308
  6.6 1.2 %copy-start.5 = (f32[192]{0:T(256)S(1)}, f32[192]{0:T(256)}, u32[]{:S(2)}) copy-start(f32[192]{0:T(256)} %param.22) | copy-start | bytes 2308
  9.0 23.2 %all-to-all-start = ((bf16[64,7,192]{2,1,0:T(8,128)(2,1)}), bf16[64,7,192]{2,1,0:T(8,128)(2,1)S(1)}, u32[]{:S(2)}, u32[]{:S(2)}) async-start(bf16[64,7,192]{2,1,0:T(8,128)(2,1)} %copy.64), calls=%async_computation | async-start | bytes 524288 | tf_op jit(solution)/shard_map/all_to_all | solution.py:110
  32.9 23.1 %copy-start.2 = (bf16[192,576]{1,0:T(8,128)(2,1)S(1)}, bf16[192,576]{1,0:T(8,128)(2,1)}, u32[]{:S(2)}) copy-start(bf16[192,576]{1,0:T(8,128)(2,1)} %param.24) | copy-start | bytes 663556
  58.5 3.6 %copy-start.1 = (f32[6,384,1024]{2,1,0:T(8,128)}, f32[6,384,1024]{2,1,0:T(8,128)S(1)}, u32[]{:S(2)}) copy-start(f32[6,384,1024]{2,1,0:T(8,128)S(1)} %get-tuple-element.15) | copy-start | bytes 28311556
  58.5 3.6 %copy-start.9 = (bf16[192,192]{1,0:T(8,128)(2,1)S(1)}, bf16[192,192]{1,0:T(8,128)(2,1)}, u32[]{:S(2)}) copy-start(bf16[192,192]{1,0:T(8,128)(2,1)} %param.25) | copy-start | bytes 221188
  62.2 5.3 %copy-start.8 = (bf16[192,768]{1,0:T(8,128)(2,1)S(1)}, bf16[192,768]{1,0:T(8,128)(2,1)}, u32[]{:S(2)}) copy-start(bf16[192,768]{1,0:T(8,128)(2,1)} %param.28) | copy-start | bytes 884740
  62.2 5.3 %copy-start.10 = (f32[192]{0:T(256)S(1)}, f32[192]{0:T(256)}, u32[]{:S(2)}) copy-start(f32[192]{0:T(256)} %param.27) | copy-start | bytes 2308
  62.2 5.3 %copy-start.11 = (f32[192]{0:T(256)S(1)}, f32[192]{0:T(256)}, u32[]{:S(2)}) copy-start(f32[192]{0:T(256)} %param.26) | copy-start | bytes 2308
  67.5 3.3 %copy-start.6 = (f32[192]{0:T(256)S(1)}, f32[192]{0:T(256)}, u32[]{:S(2)}) copy-start(f32[192]{0:T(256)} %param.31) | copy-start | bytes 2308
  67.5 3.3 %copy-start.7 = (f32[192]{0:T(256)S(1)}, f32[192]{0:T(256)}, u32[]{:S(2)}) copy-start(f32[192]{0:T(256)} %param.30) | copy-start | bytes 2308

commit v5 on v1

--- a/solution.py
+++ b/solution.py
@@ -1,8 +1,10 @@
+import functools
 import math
 
 import jax
 import jax.numpy as jnp
 from jax import lax
+from jax.experimental import pallas as pl
 from jax.sharding import PartitionSpec as P
 
 HEADS = 6
@@ -19,28 +21,78 @@
     return centred * lax.rsqrt(variance + EPS) * norm_gain + norm_bias
 
 
+def feature_kernel(
+    feat_count,
+    cells_ref, query_w_ref, key_w_ref, value_w_ref, out_w_ref, gain_ref, bias_ref, settled_ref
+):
+    cell_count, model_width = cells_ref.shape
+    head_size = model_width // HEADS
+    row_count = cell_count // feat_count
+    cells = cells_ref[...]
+    branch = jnp.zeros((cell_count, model_width), jnp.float32)
+    for head in range(HEADS):
+        queries = jnp.dot(cells, query_w_ref[head], preferred_element_type=jnp.float32).astype(jnp.bfloat16)
+        keys = jnp.dot(cells, key_w_ref[head], preferred_element_type=jnp.float32).astype(jnp.bfloat16)
+        values = jnp.dot(cells, value_w_ref[head], preferred_element_type=jnp.float32).astype(jnp.bfloat16)
+        mixed_rows = []
+        for row in range(row_count):
+            part = slice(row * feat_count, (row + 1) * feat_count)
+            scores = lax.dot_general(
+                queries[part], keys[part], (((1,), (1,)), ((), ())),
+                preferred_element_type=jnp.float32,
+            ) / math.sqrt(head_size)
+            row_top = jnp.max(scores, axis=-1, keepdims=True)
+            weights_exp = jnp.exp(scores - row_top)
+            weights = (weights_exp / jnp.sum(weights_exp, axis=-1, keepdims=True)).astype(jnp.bfloat16)
+            mixed_rows.append(
+                jnp.dot(weights, values[part], preferred_element_type=jnp.float32).astype(jnp.bfloat16)
+            )
+        mixed = jnp.concatenate(mixed_rows, axis=0)
+        branch = branch + jnp.dot(mixed, out_w_ref[head], preferred_element_type=jnp.float32)
+    values_sum = cells.astype(jnp.float32) + branch
+    centre = jnp.mean(values_sum, axis=-1, keepdims=True)
+    centred = values_sum - centre
+    variance = jnp.mean(centred * centred, axis=-1, keepdims=True)
+    settled = centred * lax.rsqrt(variance + EPS) * gain_ref[...] + bias_ref[...]
+    settled_ref[...] = settled.astype(settled_ref.dtype)
+
+
 def feature_block(cell_rows, qkv_weight, out_weight, norm_gain, norm_bias):
     row_count, feat_count, model_width = cell_rows.shape
     head_size = model_width // HEADS
     flat_rows = cell_rows.reshape(row_count * feat_count, model_width)
-    packed = jnp.dot(flat_rows, qkv_weight, preferred_element_type=jnp.float32).astype(jnp.bfloat16)
-    packed = packed.reshape(row_count, feat_count, 3, HEADS, head_size)
-    scores = jnp.einsum(
-        "rqhd,rkhd->rhqk", packed[:, :, 0], packed[:, :, 1], preferred_element_type=jnp.float32
-    ) / math.sqrt(head_size)
-    row_top = jnp.max(scores, axis=-1, keepdims=True)
-    weights_exp = jnp.exp(scores - row_top)
-    weights = (weights_exp / jnp.sum(weights_exp, axis=-1, keepdims=True)).astype(jnp.bfloat16)
-    attended = jnp.einsum(
-        "rhqk,rkhd->rqhd", weights, packed[:, :, 2], preferred_element_type=jnp.float32
-    ).astype(jnp.bfloat16)
-    branch = jnp.dot(
-        attended.reshape(row_count * feat_count, model_width),
-        out_weight,
-        preferred_element_type=jnp.float32,
-    )
-    settled = layer_norm(flat_rows.astype(jnp.float32) + branch, norm_gain, norm_bias)
-    return settled.astype(jnp.bfloat16).reshape(row_count, feat_count, model_width)
+    head_weights = jnp.transpose(
+        qkv_weight.reshape(model_width, 3, HEADS, head_size), (1, 2, 0, 3)
+    )
+    whole = lambda shape: pl.BlockSpec(shape, lambda: (0,) * len(shape))
+    settled = pl.pallas_call(
+        functools.partial(feature_kernel, feat_count),
+        in_specs=[
+            whole((row_count * feat_count, model_width)),
+            whole((HEADS, model_width, head_size)),
+            whole((HEADS, model_width, head_size)),
+            whole((HEADS, model_width, head_size)),
+            whole((HEADS, head_size, model_width)),
+            whole((1, model_width)),
+            whole((1, model_width)),
+        ],
+        out_specs=whole((row_count * feat_count, model_width)),
+        out_shape=jax.ShapeDtypeStruct((row_count * feat_count, model_width), jnp.bfloat16),
+        cost_estimate=pl.CostEstimate(
+            flops=2 * row_count * feat_count * model_width * (4 * model_width + 2 * feat_count),
+            transcendentals=row_count * HEADS * feat_count * feat_count,
+            bytes_accessed=4 * row_count * feat_count * model_width,
+        ),
+    )(
+        flat_rows,
+        head_weights[0],
+        head_weights[1],
+        head_weights[2],
+        out_weight.reshape(HEADS, head_size, model_width),
+        norm_gain.reshape(1, model_width),
+        norm_bias.reshape(1, model_width),
+    )
+    return settled.reshape(row_count, feat_count, model_width)
 
 
 def item_attention(query_rows, key_rows, key_marks, item_qkv):

time: 89.1 us -> 99.6 us (1.12)
  Pallas kernels: 0 us -> 12 us
  matrix products: 15.6 us -> 13.2 us
    pallas_call x0 -> x1, Pallas kernels: none -> 12 us  [feature_block(): pl.pallas_call(functools.partial(feature_kernel, feat_count), in_specs=[w...]
    dot_general x3 -> x0, matrix products: 1.86 us -> none  [the longest x1 1.32 us: feature_block(): jnp.dot(flat_rows, qkv_weight, preferred_element_type=jnp.float32)]
    unnamed x25 -> x24, local copies, waits for them, and re-layouts: 1.83 us -> 2.56 us
where the time goes in v5:
time: 99.6 us; the launch traced here: 99.2 us
  blocking collectives  40.1 us (40%)
  matrix products  13.2 us (13%)
  starting transfers between devices  12.9 us (13%)
  Pallas kernels  12 us (12%)
  waiting for transfers between devices  10.1 us (10%)
  local copies, waits for them, and re-layouts  6.61 us (7%)
  other arithmetic  3.26 us (3%)
    all_gather x1, blocking collectives, per_device(): lax.all_gather(jnp.concatenate([train_rows, key_mark_row[None, :]], axis=...  22.6 us
    all_to_all x1, blocking collectives, per_device(): lax.all_to_all(result_rows, 'rows', split_axis=0, concat_axis=0, tiled=True)  17.5 us
    all_to_all x1, starting transfers between devices, per_device(): lax.all_to_all(outbound, 'rows', split_axis=0, concat_axis=0, tiled=True)  12.9 us
    pallas_call x1, Pallas kernels, feature_block(): pl.pallas_call(functools.partial(feature_kernel, feat_count), in_specs=[w...  12 us
    all_to_all x1, waiting for transfers between devices, per_device(): lax.all_to_all(outbound, 'rows', split_axis=0, concat_axis=0, tiled=True)  10.1 us
    sub x1, matrix products, item_attention(): weights_exp = jnp.where(alive_keys, jnp.exp(masked - row_top), 0.0)  5.01 us
    dot_general x1, matrix products, item_attention(): jnp.einsum('hqk,khd->hqd', weights_exp.astype(jnp.bfloat16), key_values[:...  3.89 us
    dot_general x1, matrix products, per_device(): jnp.dot(hidden_units, mlp_out, preferred_element_type=jnp.float32)  3.22 us
  transfers between devices with their start and end apart: 1, of which 1 were waited for; matrix products, arithmetic and copies ran while one was open for 0% of the time, Pallas kernels for 0%

profile of v5, /device:TPU:1, one launch (start us, length us, event | category | flops | bytes accessed | tf_op | source)
XLA Modules:
  0.0 99.2 jit_solution(8713039638387677836)
XLA Ops:
  0.6 0.7 convert.6
  1.4 0.7 convert.7
  2.1 0.1 copy.57
  2.3 1.1 %copy.54 = bf16[192,576]{0,1:T(8,128)(2,1)S(1)} copy(bf16[192,576]{1,0:T(8,128)(2,1)} %param.20) | data formatting | bytes 442368 | tf_op args[4]
  3.4 0.4 copy.55
  3.8 1.0 slice_bitcast_fusion.9
  4.8 0.7 pad_maximum_fusion.1
  5.5 12.0 %shard_map.167 = bf16[384,192]{1,0:T(8,128)(2,1)} custom-call(bf16[384,192]{1,0:T(8,128)(2,1)} %bitcast.71, bf16[6,192,32]{2,1,0:T(8,128)(2,1)} %get-tuple-element.12.query_w_ref, bf16[6,192,32]{2,1,0:T(8,128)(2,1)} %get-tuple-element.11.key_w_ref, bf16[6,192,32]{2,1,0:T(8,128)(2,1)} %get-tuple-element.10.value_w_ref, bf16[6,32,192]{2,1,0:T(8,128)(2,1)} %bitcast.74, ...), custom_call_target="tpu_custom_call" | custom-call | flops 132120576 | bytes 294912 | tf_op jit(solution)/shard_map/pallas_call | solution.py:68
  17.5 1.0 %copy.72 = bf16[6,64,192]{2,0,1:T(8,128)(2,1)S(1)} copy(bf16[6,64,192]{2,1,0:T(8,128)(2,1)} %bitcast.70) | data formatting | bytes 294912 | tf_op jit(solution)/shard_map/reshape | solution.py:95
  18.6 0.8 pad_maximum_fusion
  19.4 12.9 %all-to-all-start = ((bf16[64,7,192]{2,1,0:T(8,128)(2,1)}), bf16[64,7,192]{2,1,0:T(8,128)(2,1)S(1)}, u32[]{:S(2)}, u32[]{:S(2)}) async-start(bf16[64,7,192]{2,1,0:T(8,128)(2,1)} %pad_maximum_fusion), calls=%async_computation | async-start | bytes 524288 | tf_op jit(solution)/shard_map/all_to_all | solution.py:156
  32.4 0.1 broadcast_in_dim.55
  32.5 10.1 %all-to-all-done = bf16[64,7,192]{2,1,0:T(8,128)(2,1)S(1)} async-done(((bf16[64,7,192]{2,1,0:T(8,128)(2,1)}), bf16[64,7,192]{2,1,0:T(8,128)(2,1)S(1)}, u32[]{:S(2)}, u32[]{:S(2)}) %all-to-all-start) | async-done | bytes 172064 | tf_op jit(solution)/shard_map/all_to_all | solution.py:156
  42.6 0.1 slice_reduce_fusion
  42.8 0.1 copy.67
  42.9 0.1 copy.61
  43.0 0.2 reshape.108
  43.3 22.6 %all-gather.1 = bf16[8,129,192]{2,1,0:T(8,128)(2,1)S(1)} all-gather(bf16[1,129,192]{2,1,0:T(8,128)(2,1)S(1)} %maximum_bitcast_fusion), channel_id=2, replica_groups=mesh['rows'=64,'feat'=8] {'feat'}, dimensions={0}, use_global_device_ids=true | all-gather | bytes 445824 | tf_op jit(solution)/shard_map/all_gather | solution.py:164
  66.0 0.1 squeeze.26
  66.1 0.1 reshape.106
  66.2 0.1 copy.59
  66.4 0.3 convolution_convert_fusion.1
  66.7 0.5 convolution_convert_fusion
  67.2 5.0 %fusion.104 = (f32[6,384]{1,0:T(8,128)S(1)}, bf16[6,384,1024]{2,1,0:T(8,128)(2,1)}) fusion(pred[1024]{0:T(1024)(128)(4,1)S(1)} %compare_bitcast_fusion, bf16[384,6,32]{0,2,1:T(8,128)(2,1)S(1)} %bitcast.72, bf16[1024,2,6,32]{0,3,2,1:T(8,128)(2,1)S(1)} %bitcast.68), kind=kOutput, calls=%fused_computation.130 | convolution fusion | flops 165151744 | bytes 5270528 | tf_op jit(solution)/shard_map/sub | solution.py:116
  72.2 3.9 %fusion.26 = bf16[384,6,32]{0,2,1:T(8,128)(2,1)S(1)} fusion(bf16[6,384,1024]{2,1,0:T(8,128)(2,1)} %get-tuple-element.16, bf16[1024,2,6,32]{0,3,2,1:T(8,128)(2,1)S(1)} %bitcast.69, f32[384,6]{0,1:T(8,128)S(1)} %bitcast.79), kind=kOutput, calls=%fused_computation.35 | convolution fusion | flops 151142400 | bytes 5271552 | tf_op jit(solution)/shard_map/hqk,khd->hqd/dot_general | solution.py:118
  76.2 0.3 fusion.105
  76.6 3.2 %fusion.106 = (f32[384]{0:T(512)S(1)}, f32[384,192]{0,1:T(8,128)S(1)}) fusion(bf16[768,192]{0,1:T(8,128)(2,1)S(1)} %copy-done, bf16[192,768]{1,0:T(8,128)(2,1)S(1)} %copy-done.7, f32[384,192]{0,1:T(8,128)S(1)} %get-tuple-element.18, f32[192]{0:T(256)S(1)} %copy-done.8, f32[192]{0:T(256)S(1)} %copy-done.9, f32[384]{0:T(512)S(1)} %add_rsqrt_fusion.1, ...), kind=kOutput, calls=%fused_computation.132 | convolution fusion | flops 246619776 | bytes 1185792 | tf_op jit(solution)/shard_map/dot_general | solution.py:184
  79.9 0.1 add_convert_fusion
  80.0 0.1 copy.64
  80.2 17.5 %all_to_all.10 = bf16[64,6,192]{2,1,0:T(8,128)(2,1)S(1)} all-to-all(bf16[64,6,192]{2,1,0:T(8,128)(2,1)S(1)} %reshape.113), channel_id=1, replica_groups=mesh['rows'=64,'feat'=8] {'rows'}, dimensions={0} | all-to-all | bytes 294912 | tf_op jit(solution)/shard_map/all_to_all | solution.py:189
  97.9 0.7 copy.66
  98.6 0.6 copy.65
  (44 shorter events, 0.7 us)
Async XLA Ops:
  0.6 75.9 %copy-start = (bf16[768,192]{0,1:T(8,128)(2,1)S(1)}, bf16[768,192]{0,1:T(8,128)(2,1)}, u32[]{:S(2)}) copy-start(bf16[768,192]{0,1:T(8,128)(2,1)} %param.29) | copy-start | bytes 884740
  3.8 1.0 copy-start.2
  3.8 1.0 copy-start.4
  19.4 23.2 %all-to-all-start = ((bf16[64,7,192]{2,1,0:T(8,128)(2,1)}), bf16[64,7,192]{2,1,0:T(8,128)(2,1)S(1)}, u32[]{:S(2)}, u32[]{:S(2)}) async-start(bf16[64,7,192]{2,1,0:T(8,128)(2,1)} %pad_maximum_fusion), calls=%async_computation | async-start | bytes 524288 | tf_op jit(solution)/shard_map/all_to_all | solution.py:156
  43.3 23.1 %copy-start.1 = (bf16[192,576]{1,0:T(8,128)(2,1)S(1)}, bf16[192,576]{1,0:T(8,128)(2,1)}, u32[]{:S(2)}) copy-start(bf16[192,576]{1,0:T(8,128)(2,1)} %param.24) | copy-start | bytes 663556
  72.2 3.9 %copy-start.3 = (bf16[192,192]{1,0:T(8,128)(2,1)S(1)}, bf16[192,192]{1,0:T(8,128)(2,1)}, u32[]{:S(2)}) copy-start(bf16[192,192]{1,0:T(8,128)(2,1)} %param.25) | copy-start | bytes 221188
  72.2 4.3 %copy-start.7 = (bf16[192,768]{1,0:T(8,128)(2,1)S(1)}, bf16[192,768]{1,0:T(8,128)(2,1)}, u32[]{:S(2)}) copy-start(bf16[192,768]{1,0:T(8,128)(2,1)} %param.28) | copy-start | bytes 884740
  72.2 4.3 %copy-start.8 = (f32[192]{0:T(256)S(1)}, f32[192]{0:T(256)}, u32[]{:S(2)}) copy-start(f32[192]{0:T(256)} %param.27) | copy-start | bytes 2308
  72.2 4.3 %copy-start.9 = (f32[192]{0:T(256)S(1)}, f32[192]{0:T(256)}, u32[]{:S(2)}) copy-start(f32[192]{0:T(256)} %param.26) | copy-start | bytes 2308
  76.5 3.3 %copy-start.5 = (f32[192]{0:T(256)S(1)}, f32[192]{0:T(256)}, u32[]{:S(2)}) copy-start(f32[192]{0:T(256)} %param.31) | copy-start | bytes 2308
  76.6 3.3 %copy-start.6 = (f32[192]{0:T(256)S(1)}, f32[192]{0:T(256)}, u32[]{:S(2)}) copy-start(f32[192]{0:T(256)} %param.30) | copy-start | bytes 2308

commit v6 on v1

--- a/solution.py
+++ b/solution.py
@@ -55,22 +55,21 @@
         key_rows, item_qkv[:, model_width:], preferred_element_type=jnp.float32
     ).astype(jnp.bfloat16)
     key_values = key_values.reshape(key_count, 2, HEADS, head_size)
-    scores = jnp.einsum(
-        "qhd,khd->hqk", queries, key_values[:, 0], preferred_element_type=jnp.float32
-    ) / math.sqrt(head_size)
-    alive_keys = (key_marks > 0)[None, None, :]
-    masked = jnp.where(alive_keys, scores, NEG)
-    row_top = jnp.max(masked, axis=-1, keepdims=True)
-    weights_exp = jnp.where(alive_keys, jnp.exp(masked - row_top), 0.0)
-    totals = jnp.sum(weights_exp, axis=-1)
-    weighted = jnp.einsum(
-        "hqk,khd->hqd",
-        weights_exp.astype(jnp.bfloat16),
-        key_values[:, 1],
-        preferred_element_type=jnp.float32,
-    )
-    attended = (weighted / totals[..., None]).astype(jnp.bfloat16)
-    return jnp.transpose(attended, (1, 0, 2)).reshape(query_count, model_width)
+    alive_keys = (key_marks > 0)[None, :]
+    head_parts = []
+    for head in range(HEADS):
+        scores = jnp.dot(
+            queries[:, head], key_values[:, 0, head].T, preferred_element_type=jnp.float32
+        ) / math.sqrt(head_size)
+        masked = jnp.where(alive_keys, scores, NEG)
+        row_top = jnp.max(masked, axis=-1, keepdims=True)
+        weights_exp = jnp.where(alive_keys, jnp.exp(masked - row_top), 0.0)
+        totals = jnp.sum(weights_exp, axis=-1, keepdims=True)
+        weighted = jnp.dot(
+            weights_exp.astype(jnp.bfloat16), key_values[:, 1, head], preferred_element_type=jnp.float32
+        )
+        head_parts.append((weighted / totals).astype(jnp.bfloat16))
+    return jnp.concatenate(head_parts, axis=1)
 
 
 def per_device(

time: 89.1 us -> 99.1 us (1.11)
  other arithmetic: 2.89 us -> 7.82 us
  matrix products: 15.6 us -> 18.8 us
  local copies, waits for them, and re-layouts: 5.92 us -> 7.88 us
    dot_general x1 -> x12, matrix products: 3.89 us -> 9.78 us  [the longest x6 7.14 us: item_attention(): jnp.dot(queries[:, head], key_values[:, 0, head].T, preferred_element_typ...]
    sub x1 -> x0, matrix products: 5.01 us -> none  [item_attention(): weights_exp = jnp.where(alive_keys, jnp.exp(masked - row_top), 0.0)]
    reduce_sum x0 -> x1, other arithmetic: none -> 4.93 us  [item_attention(): totals = jnp.sum(weights_exp, axis=-1, keepdims=True)]
    unnamed x25 -> x39, local copies, waits for them, and re-layouts: 1.83 us -> 3.15 us
    dot_general x1, matrix products: 0.28 us -> 1.58 us  [feature_block(): jnp.einsum('rhqk,rkhd->rqhd', weights, packed[:, :, 2], preferred_element...]
    sub x1, matrix products: 0.61 us -> 1.6 us  [feature_block(): weights_exp = jnp.exp(scores - row_top)]
where the time goes in v6:
time: 99.1 us; the launch traced here: 98.7 us
  blocking collectives  40 us (40%)
  matrix products  18.8 us (19%)
  starting transfers between devices  12.9 us (13%)
  waiting for transfers between devices  10.1 us (10%)
  local copies, waits for them, and re-layouts  7.88 us (8%)
  other arithmetic  7.82 us (8%)
  between operations  1.08 us (1%)
    all_gather x1, blocking collectives, per_device(): lax.all_gather(jnp.concatenate([train_rows, key_mark_row[None, :]], axis=...  22.5 us
    all_to_all x1, blocking collectives, per_device(): lax.all_to_all(result_rows, 'rows', split_axis=0, concat_axis=0, tiled=True)  17.5 us
    all_to_all x1, starting transfers between devices, per_device(): lax.all_to_all(outbound, 'rows', split_axis=0, concat_axis=0, tiled=True)  12.9 us
    all_to_all x1, waiting for transfers between devices, per_device(): lax.all_to_all(outbound, 'rows', split_axis=0, concat_axis=0, tiled=True)  10.1 us
    dot_general x6, matrix products, item_attention(): jnp.dot(queries[:, head], key_values[:, 0, head].T, preferred_element_typ...  7.14 us
    reduce_sum x1, other arithmetic, item_attention(): totals = jnp.sum(weights_exp, axis=-1, keepdims=True)  4.93 us
    dot_general x1, matrix products, per_device(): jnp.dot(hidden_units, mlp_out, preferred_element_type=jnp.float32)  3.22 us
    unnamed x39, local copies, waits for them, and re-layouts  3.15 us
  transfers between devices with their start and end apart: 1, of which 1 were waited for; matrix products, arithmetic and copies ran while one was open for 0% of the time, Pallas kernels for 0%

profile of v6, /device:TPU:1, one launch (start us, length us, event | category | flops | bytes accessed | tf_op | source)
XLA Modules:
  0.0 98.7 jit_solution(14194932846194803027)
XLA Ops:
  0.6 0.7 convert.6
  1.4 0.7 convert.7
  2.2 0.9 pad_maximum_fusion.1
  3.3 1.3 %convolution_convert_fusion.1 = bf16[384,576]{0,1:T(8,128)(2,1)S(1)} fusion(bf16[384,192]{1,0:T(8,128)(2,1)S(1)} %bitcast.146, bf16[192,576]{1,0:T(8,128)(2,1)} %param.20), kind=kOutput, calls=%fused_computation.30 | convolution fusion | flops 85155840 | bytes 811008 | tf_op jit(solution)/shard_map/dot_general | solution.py:26
  4.6 0.6 reshape.118
  5.5 1.6 %fusion.133 = (f32[6,6,64]{2,1,0:T(8,128)S(1)}, f32[6,6,64,64]{2,3,1,0:T(8,128)}) fusion(bf16[6,64,1,6,32]{1,0,4,3,2:T(8,128)(2,1)S(1)} %get-tuple-element.16, bf16[6,64,1,6,32]{1,0,4,3,2:T(8,128)(2,1)S(1)} %get-tuple-element.15), kind=kOutput, calls=%fused_computation.200 | convolution fusion | flops 9879615 | bytes 893952 | tf_op jit(solution)/shard_map/sub | solution.py:32
  7.2 1.6 %fusion.26 = bf16[6,64,6,32]{1,3,2,0:T(8,128)(2,1)S(1)} fusion(f32[6,6,64,64]{2,3,1,0:T(8,128)} %get-tuple-element.20, f32[6,6,64]{2,1,0:T(8,128)S(1)} %get-tuple-element.19, bf16[6,64,1,6,32]{1,0,4,3,2:T(8,128)(2,1)S(1)} %get-tuple-element.14), kind=kOutput, calls=%fused_computation.52 | convolution fusion | flops 9805824 | bytes 893952 | tf_op jit(solution)/shard_map/rhqk,rkhd->rqhd/dot_general | solution.py:34
  9.9 0.8 copy.64
  10.8 12.9 %all-to-all-start = ((bf16[64,7,192]{2,1,0:T(8,128)(2,1)}), bf16[64,7,192]{2,1,0:T(8,128)(2,1)S(1)}, u32[]{:S(2)}, u32[]{:S(2)}) async-start(bf16[64,7,192]{2,1,0:T(8,128)(2,1)} %copy.64), calls=%async_computation | async-start | bytes 524288 | tf_op jit(solution)/shard_map/all_to_all | solution.py:103
  23.9 10.1 %all-to-all-done = bf16[64,7,192]{2,1,0:T(8,128)(2,1)S(1)} async-done(((bf16[64,7,192]{2,1,0:T(8,128)(2,1)}), bf16[64,7,192]{2,1,0:T(8,128)(2,1)S(1)}, u32[]{:S(2)}, u32[]{:S(2)}) %all-to-all-start) | async-done | bytes 172064 | tf_op jit(solution)/shard_map/all_to_all | solution.py:103
  34.7 22.5 %all-gather.1 = bf16[8,129,192]{2,1,0:T(8,128)(2,1)S(1)} all-gather(bf16[1,129,192]{2,1,0:T(8,128)(2,1)S(1)} %maximum_bitcast_fusion), channel_id=2, replica_groups=mesh['rows'=64,'feat'=8] {'feat'}, dimensions={0}, use_global_device_ids=true | all-gather | bytes 445824 | tf_op jit(solution)/shard_map/all_gather | solution.py:111
  57.3 0.8 copy.65
  58.4 0.5 convolution_convert_fusion
  58.9 0.5 fusion.136
  59.4 0.5 fusion.140
  59.9 1.5 %fusion.139 = (f32[384]{0:T(512)S(1)}, f32[384,1024]{1,0:T(8,128)}) fusion(bf16[1024,2,6,32]{0,3,2,1:T(8,128)(2,1)S(1)} %bitcast.135, bf16[384,6,32]{0,2,1:T(8,128)(2,1)S(1)} %bitcast.153, pred[1024]{0:T(1024)(128)(4,1)S(1)} %compare_bitcast_fusion), kind=kOutput, calls=%fused_computation.206 | convolution fusion | flops 26345088 | bytes 1665536 | tf_op jit(solution)/shard_map/dot_general | solution.py:61
  61.4 1.5 %fusion.138 = (f32[384]{0:T(512)S(1)}, f32[384,1024]{1,0:T(8,128)}) fusion(bf16[1024,2,6,32]{0,3,2,1:T(8,128)(2,1)S(1)} %bitcast.136, bf16[384,6,32]{0,2,1:T(8,128)(2,1)S(1)} %bitcast.154, pred[1024]{0:T(1024)(128)(4,1)S(1)} %compare_bitcast_fusion), kind=kOutput, calls=%fused_computation.205 | convolution fusion | flops 26345088 | bytes 1665536 | tf_op jit(solution)/shard_map/dot_general | solution.py:61
  63.0 1.5 %fusion.137 = (f32[384]{0:T(512)S(1)}, f32[384,1024]{1,0:T(8,128)}) fusion(bf16[1024,2,6,32]{0,3,2,1:T(8,128)(2,1)S(1)} %bitcast.137, bf16[384,6,32]{0,2,1:T(8,128)(2,1)S(1)} %bitcast.155, pred[1024]{0:T(1024)(128)(4,1)S(1)} %compare_bitcast_fusion), kind=kOutput, calls=%fused_computation.204 | convolution fusion | flops 26345088 | bytes 1665536 | tf_op jit(solution)/shard_map/dot_general | solution.py:61
  64.5 1.6 %fusion.135 = (f32[384]{0:T(512)S(1)}, f32[384,1024]{1,0:T(8,128)}) fusion(bf16[1024,2,6,32]{0,3,2,1:T(8,128)(2,1)S(1)} %bitcast.138, bf16[384,6,32]{0,2,1:T(8,128)(2,1)S(1)} %bitcast.156, pred[1024]{0:T(1024)(128)(4,1)S(1)} %compare_bitcast_fusion), kind=kOutput, calls=%fused_computation.202 | convolution fusion | flops 26345088 | bytes 1665536 | tf_op jit(solution)/shard_map/dot_general | solution.py:61
  66.2 4.9 %fusion.13 = (f32[384]{0:T(512)S(1)}, f32[384]{0:T(512)S(1)}, f32[384]{0:T(512)S(1)}, f32[384]{0:T(512)S(1)}, f32[384]{0:T(512)S(1)}, /*index=5*/f32[384]{0:T(512)S(1)}) fusion(f32[384,1024]{1,0:T(8,128)S(1)} %get-tuple-element.26, f32[384]{0:T(512)S(1)} %get-tuple-element.25, pred[1024]{0:T(1024)(128)(4,1)S(1)} %compare_bitcast_fusion, ...), kind=kLoop, calls=%fused_computation.28 | loop fusion | flops 7075584 | bytes 9456640 | tf_op jit(solution)/shard_map/reduce_sum | solution.py:67
  71.2 0.4 fusion.30
  71.7 0.9 copy-done.3
  72.6 0.4 fusion.32
  73.1 0.4 fusion.34
  73.5 0.6 copy-done.1
  74.1 0.4 fusion.36
  74.6 0.4 fusion.38
  75.1 0.4 fusion.40
  76.0 3.2 %fusion.142 = (f32[384]{0:T(512)S(1)}, f32[384,192]{0,1:T(8,128)S(1)}) fusion(bf16[768,192]{0,1:T(8,128)(2,1)S(1)} %copy-done, bf16[192,768]{1,0:T(8,128)(2,1)S(1)} %copy-done.15, f32[384,192]{0,1:T(8,128)S(1)} %get-tuple-element.36, f32[192]{0:T(256)S(1)} %copy-done.16, f32[192]{0:T(256)S(1)} %copy-done.17, f32[384]{0:T(512)S(1)} %add_rsqrt_fusion.1, ...), kind=kOutput, calls=%fused_computation.209 | convolution fusion | flops 246619776 | bytes 1185792 | tf_op jit(solution)/shard_map/dot_general | solution.py:131
  79.7 17.5 %all_to_all.10 = bf16[64,6,192]{2,1,0:T(8,128)(2,1)S(1)} all-to-all(bf16[64,6,192]{2,1,0:T(8,128)(2,1)S(1)} %reshape.127), channel_id=1, replica_groups=mesh['rows'=64,'feat'=8] {'rows'}, dimensions={0} | all-to-all | bytes 294912 | tf_op jit(solution)/shard_map/all_to_all | solution.py:136
  97.3 0.7 copy.72
  98.0 0.6 copy.71
  (80 shorter events, 4.1 us)
Async XLA Ops:
  0.6 75.2 %copy-start = (bf16[768,192]{0,1:T(8,128)(2,1)S(1)}, bf16[768,192]{0,1:T(8,128)(2,1)}, u32[]{:S(2)}) copy-start(bf16[768,192]{0,1:T(8,128)(2,1)} %param.29) | copy-start | bytes 884740
  7.2 2.1 %copy-start.9 = (bf16[192,192]{1,0:T(8,128)(2,1)S(1)}, bf16[192,192]{1,0:T(8,128)(2,1)}, u32[]{:S(2)}) copy-start(bf16[192,192]{1,0:T(8,128)(2,1)} %param.21) | copy-start | bytes 221188
  8.7 0.9 copy-start.11
  8.8 0.9 copy-start.12
  10.8 23.3 %all-to-all-start = ((bf16[64,7,192]{2,1,0:T(8,128)(2,1)}), bf16[64,7,192]{2,1,0:T(8,128)(2,1)S(1)}, u32[]{:S(2)}, u32[]{:S(2)}) async-start(bf16[64,7,192]{2,1,0:T(8,128)(2,1)} %copy.64), calls=%async_computation | async-start | bytes 524288 | tf_op jit(solution)/shard_map/all_to_all | solution.py:103
  23.7 34.4 %copy-start.8 = (bf16[192,576]{1,0:T(8,128)(2,1)S(1)}, bf16[192,576]{1,0:T(8,128)(2,1)}, u32[]{:S(2)}) copy-start(bf16[192,576]{1,0:T(8,128)(2,1)} %param.24) | copy-start | bytes 663556
  58.9 5.6 %copy-start.5 = (bf16[1024,384]{0,1:T(8,128)(2,1)}, bf16[1024,384]{0,1:T(8,128)(2,1)S(1)}, u32[]{:S(2)}) copy-start(bf16[1024,384]{0,1:T(8,128)(2,1)S(1)} %convolution_convert_fusion) | copy-start | bytes 2359300
  66.2 5.0 %copy-start.4 = (f32[384,1024]{1,0:T(8,128)S(1)}, f32[384,1024]{1,0:T(8,128)}, u32[]{:S(2)}) copy-start(f32[384,1024]{1,0:T(8,128)} %get-tuple-element.24) | copy-start | bytes 4718596
  66.2 5.0 %copy-start.6 = (bf16[1024,384]{0,1:T(8,128)(2,1)S(1)}, bf16[1024,384]{0,1:T(8,128)(2,1)}, u32[]{:S(2)}) copy-start(bf16[1024,384]{0,1:T(8,128)(2,1)} %copy-done.5) | copy-start | bytes 2359300
  71.2 1.4 %copy-start.3 = (f32[384,1024]{1,0:T(8,128)S(1)}, f32[384,1024]{1,0:T(8,128)}, u32[]{:S(2)}) copy-start(f32[384,1024]{1,0:T(8,128)} %get-tuple-element.28) | copy-start | bytes 4718596
  71.2 1.9 %copy-start.2 = (f32[384,1024]{1,0:T(8,128)S(1)}, f32[384,1024]{1,0:T(8,128)}, u32[]{:S(2)}) copy-start(f32[384,1024]{1,0:T(8,128)} %get-tuple-element.30) | copy-start | bytes 4718596
  72.6 1.5 %copy-start.1 = (f32[384,1024]{1,0:T(8,128)S(1)}, f32[384,1024]{1,0:T(8,128)}, u32[]{:S(2)}) copy-start(f32[384,1024]{1,0:T(8,128)} %get-tuple-element.32) | copy-start | bytes 4718596
  74.6 0.9 copy-start.7
  74.6 1.0 copy-start.10
  75.0 1.0 copy-start.15
  75.0 1.0 copy-start.16
  75.0 0.9 copy-start.17
  76.0 3.3 %copy-start.13 = (f32[192]{0:T(256)S(1)}, f32[192]{0:T(256)}, u32[]{:S(2)}) copy-start(f32[192]{0:T(256)} %param.31) | copy-start | bytes 2308
  76.0 3.3 %copy-start.14 = (f32[192]{0:T(256)S(1)}, f32[192]{0:T(256)}, u32[]{:S(2)}) copy-start(f32[192]{0:T(256)} %param.30) | copy-start | bytes 2308

commit v7 on v1

--- a/solution.py
+++ b/solution.py
@@ -3,6 +3,7 @@
 import jax
 import jax.numpy as jnp
 from jax import lax
+from jax.experimental import pallas as pl
 from jax.sharding import PartitionSpec as P
 
 HEADS = 6
@@ -10,6 +11,7 @@
 
 EPS = 1e-05
 NEG = -1e30
+SQRT_HALF = math.sqrt(0.5)
 
 
 def layer_norm(values, norm_gain, norm_bias):
@@ -73,6 +75,44 @@
     return jnp.transpose(attended, (1, 0, 2)).reshape(query_count, model_width)
 
 
+def tail_kernel(
+    mixed_ref, rows_ref, item_out_ref, item_gain_ref, item_bias_ref,
+    mlp_in_ref, mlp_out_ref, mlp_gain_ref, mlp_bias_ref, out_ref,
+):
+    branch = jnp.dot(mixed_ref[...], item_out_ref[...], preferred_element_type=jnp.float32)
+    settled = layer_norm(
+        rows_ref[...].astype(jnp.float32) + branch, item_gain_ref[...], item_bias_ref[...]
+    ).astype(jnp.bfloat16)
+    pre = jnp.dot(settled, mlp_in_ref[...], preferred_element_type=jnp.float32)
+    inner = (0.5 * pre * (1.0 + lax.erf(pre * SQRT_HALF))).astype(jnp.bfloat16)
+    result = layer_norm(
+        settled.astype(jnp.float32)
+        + jnp.dot(inner, mlp_out_ref[...], preferred_element_type=jnp.float32),
+        mlp_gain_ref[...],
+        mlp_bias_ref[...],
+    )
+    out_ref[...] = result.astype(out_ref.dtype)
+
+
+def item_tail(mixed, rows, item_out, item_gain, item_bias, mlp_in, mlp_out, mlp_gain, mlp_bias):
+    cell_count, model_width = rows.shape
+    hidden_width = mlp_in.shape[1]
+    as_row = lambda vector: vector.reshape(1, model_width)
+    return pl.pallas_call(
+        tail_kernel,
+        out_shape=jax.ShapeDtypeStruct((cell_count, model_width), jnp.bfloat16),
+        cost_estimate=pl.CostEstimate(
+            flops=2 * cell_count * model_width * (model_width + 2 * hidden_width),
+            transcendentals=cell_count * hidden_width,
+            bytes_accessed=2 * (3 * cell_count * model_width
+                                + model_width * (model_width + 2 * hidden_width)),
+        ),
+    )(
+        mixed, rows, item_out, as_row(item_gain), as_row(item_bias),
+        mlp_in, mlp_out, as_row(mlp_gain), as_row(mlp_bias),
+    )
+
+
 def per_device(
     train_cells,
     test_cells,
@@ -117,22 +157,12 @@
 
     query_rows = col_rows.reshape(source_count * row_count, model_width)
     attended = item_attention(query_rows, key_rows, key_marks, item_qkv)
-    branch = jnp.dot(attended, item_out, preferred_element_type=jnp.float32)
     is_train = (jnp.arange(row_count) < train_count)[None, :]
-    keep_gate = jnp.where(is_train, jnp.ones_like(col_marks), col_marks).astype(jnp.float32)
-    branch = branch * keep_gate.reshape(-1, 1)
-    settled_item = layer_norm(
-        query_rows.astype(jnp.float32) + branch, item_gain, item_bias
-    ).astype(jnp.bfloat16)
-    hidden_units = jax.nn.gelu(
-        jnp.dot(settled_item, mlp_in, preferred_element_type=jnp.float32), approximate=False
-    ).astype(jnp.bfloat16)
-    result_rows = layer_norm(
-        settled_item.astype(jnp.float32)
-        + jnp.dot(hidden_units, mlp_out, preferred_element_type=jnp.float32),
-        mlp_gain,
-        mlp_bias,
-    ).astype(jnp.bfloat16)
+    keep_gate = jnp.where(is_train, jnp.ones_like(col_marks), col_marks)
+    gated = attended * keep_gate.reshape(-1, 1)
+    result_rows = item_tail(
+        gated, query_rows, item_out, item_gain, item_bias, mlp_in, mlp_out, mlp_gain, mlp_bias
+    )
     result_rows = result_rows.reshape(source_count, row_count, model_width)
     returned = lax.all_to_all(result_rows, "rows", split_axis=0, concat_axis=0, tiled=True)
     final = jnp.swapaxes(returned, 0, 1)

time: 89.1 us -> 87.1 us (0.978)
  matrix products: 15.6 us -> 11.1 us
  Pallas kernels: 0 us -> 3.2 us
  local copies, waits for them, and re-layouts: 5.92 us -> 7.31 us
  waiting for transfers between devices: 10.1 us -> 9.2 us
    dot_general x2 -> x0, matrix products: 3.49 us -> none  [the longest x1 3.22 us: per_device(): jnp.dot(hidden_units, mlp_out, preferred_element_type=jnp.float32)]
    pallas_call x0 -> x1, Pallas kernels: none -> 3.2 us  [item_tail(): pl.pallas_call(tail_kernel, out_shape=jax.ShapeDtypeStruct((cell_count, m...]
    another operation x2, other arithmetic: 1.41 us -> 0.01 us
    dot_general x1, matrix products: 1.32 us -> 0.36 us  [feature_block(): jnp.dot(flat_rows, qkv_weight, preferred_element_type=jnp.float32)]
    all_to_all x1, waiting for transfers between devices: 10.1 us -> 9.2 us  [per_device(): lax.all_to_all(outbound, 'rows', split_axis=0, concat_axis=0, tiled=True)]
    reshape x1, local copies, waits for them, and re-layouts: 0.08 us -> 1.01 us  [per_device(): result_rows = result_rows.reshape(source_count, row_count, model_width)]
    unnamed x25 -> x22, local copies, waits for them, and re-layouts: 1.83 us -> 2.43 us
  transfers between devices with their start and end apart: 1 -> 1, of which waited for: 1 -> 1; matrix products, arithmetic and copies ran while one was open for 0% -> 1% of each run, Pallas kernels for 0% -> 0%
where the time goes in v7:
time: 87.1 us; the launch traced here: 86.6 us
  blocking collectives  39.8 us (46%)
  starting transfers between devices  12.9 us (15%)
  matrix products  11.1 us (13%)
  waiting for transfers between devices  9.2 us (11%)
  local copies, waits for them, and re-layouts  7.31 us (8%)
  Pallas kernels  3.2 us (4%)
  other arithmetic  2.06 us (2%)
  between operations  0.99 us (1%)
    all_gather x1, blocking collectives, per_device(): lax.all_gather(jnp.concatenate([train_rows, key_mark_row[None, :]], axis=...  22.3 us
    all_to_all x1, blocking collectives, per_device(): lax.all_to_all(result_rows, 'rows', split_axis=0, concat_axis=0, tiled=True)  17.5 us
    all_to_all x1, starting transfers between devices, per_device(): lax.all_to_all(outbound, 'rows', split_axis=0, concat_axis=0, tiled=True)  12.9 us
    all_to_all x1, waiting for transfers between devices, per_device(): lax.all_to_all(outbound, 'rows', split_axis=0, concat_axis=0, tiled=True)  9.2 us
    sub x1, matrix products, item_attention(): weights_exp = jnp.where(alive_keys, jnp.exp(masked - row_top), 0.0)  5.01 us
    dot_general x1, matrix products, item_attention(): jnp.einsum('hqk,khd->hqd', weights_exp.astype(jnp.bfloat16), key_values[:...  3.84 us
    pallas_call x1, Pallas kernels, item_tail(): pl.pallas_call(tail_kernel, out_shape=jax.ShapeDtypeStruct((cell_count, m...  3.2 us
    unnamed x22, local copies, waits for them, and re-layouts  2.43 us
  transfers between devices with their start and end apart: 1, of which 1 were waited for; matrix products, arithmetic and copies ran while one was open for 1% of the time, Pallas kernels for 0%

profile of v7, /device:TPU:1, one launch (start us, length us, event | category | flops | bytes accessed | tf_op | source)
XLA Modules:
  0.0 86.6 jit_solution(5578517039297763773)
XLA Ops:
  0.6 1.0 %pad_maximum_fusion.1 = bf16[6,64,192]{2,1,0:T(8,128)(2,1)S(1)} fusion(bf16[4,64,192]{2,1,0:T(8,128)(2,1)} %param.17, bf16[2,64,192]{2,1,0:T(8,128)(2,1)} %param.16), kind=kLoop, calls=%fused_computation.33 | loop fusion | flops 73728 | bytes 294912 | tf_op jit(solution)/shard_map/concatenate | solution.py:137
  1.6 0.1 copy.75
  1.8 0.4 convolution_convert_fusion.1
  2.1 0.6 reshape.94
  2.8 0.3 fusion.29
  3.1 0.6 fusion.30
  3.7 0.3 fusion.10
  4.0 0.2 copy.80
  4.3 0.3 reshape.95
  4.6 0.3 fusion.31
  5.0 0.1 add_convert_fusion
  5.1 0.1 copy.81
  5.5 0.8 copy.83
  6.3 12.9 %all-to-all-start = ((bf16[64,7,192]{2,1,0:T(8,128)(2,1)}), bf16[64,7,192]{2,1,0:T(8,128)(2,1)S(1)}, u32[]{:S(2)}, u32[]{:S(2)}) async-start(bf16[64,7,192]{2,1,0:T(8,128)(2,1)} %copy.83), calls=%async_computation | async-start | bytes 524288 | tf_op jit(solution)/shard_map/all_to_all | solution.py:144
  19.3 0.1 broadcast_in_dim.53
  19.4 0.9 %copy.90.mlp_out_ref = bf16[768,192]{1,0:T(8,128)(2,1)} copy(bf16[768,192]{0,1:T(8,128)(2,1)S(1)} %copy-done.2) | data formatting | bytes 589824 | tf_op args[13]
  20.4 9.2 %all-to-all-done = bf16[64,7,192]{2,1,0:T(8,128)(2,1)S(1)} async-done(((bf16[64,7,192]{2,1,0:T(8,128)(2,1)}), bf16[64,7,192]{2,1,0:T(8,128)(2,1)S(1)}, u32[]{:S(2)}, u32[]{:S(2)}) %all-to-all-start) | async-done | bytes 172064 | tf_op jit(solution)/shard_map/all_to_all | solution.py:144
  29.6 0.1 slice_reduce_fusion
  29.9 0.2 reshape.98
  30.2 22.3 %all-gather.1 = bf16[8,129,192]{2,1,0:T(8,128)(2,1)S(1)} all-gather(bf16[1,129,192]{2,1,0:T(8,128)(2,1)S(1)} %maximum_bitcast_fusion), channel_id=2, replica_groups=mesh['rows'=64,'feat'=8] {'feat'}, dimensions={0}, use_global_device_ids=true | all-gather | bytes 445824 | tf_op jit(solution)/shard_map/all_gather | solution.py:152
  52.7 0.5 convolution_convert_fusion
  53.3 0.3 convolution_convert_fusion.3
  53.5 5.0 %fusion.32 = (f32[6,384]{1,0:T(8,128)S(1)}, bf16[6,384,1024]{2,1,0:T(8,128)(2,1)}) fusion(pred[1024]{0:T(1024)(128)(4,1)S(1)} %compare_bitcast_fusion, bf16[384,6,32]{0,2,1:T(8,128)(2,1)S(1)} %bitcast.89, bf16[1024,2,6,32]{0,3,2,1:T(8,128)(2,1)S(1)} %bitcast.86), kind=kOutput, calls=%fused_computation.53 | convolution fusion | flops 165151744 | bytes 5270528 | tf_op jit(solution)/shard_map/sub | solution.py:66
  58.5 3.8 %fusion.17 = bf16[384,6,32]{0,2,1:T(8,128)(2,1)S(1)} fusion(bf16[6,384,1024]{2,1,0:T(8,128)(2,1)} %get-tuple-element.20, bf16[1024,2,6,32]{0,3,2,1:T(8,128)(2,1)S(1)} %bitcast.87, f32[384,6]{0,1:T(8,128)S(1)} %bitcast.97), kind=kOutput, calls=%fused_computation.21 | convolution fusion | flops 151142400 | bytes 5271552 | tf_op jit(solution)/shard_map/hqk,khd->hqd/dot_general | solution.py:68
  62.4 0.1 copy.88
  62.5 0.1 squeeze.26
  62.7 0.8 broadcast_multiply_fusion.mixed_ref
  63.5 3.2 %shard_map.167 = bf16[384,192]{1,0:T(8,128)(2,1)} custom-call(bf16[384,192]{1,0:T(8,128)(2,1)} %broadcast_multiply_fusion.mixed_ref, bf16[384,192]{1,0:T(8,128)(2,1)} %copy-done.1, bf16[192,192]{1,0:T(8,128)(2,1)} %item_out_ref.1, f32[1,192]{1,0:T(1,128)} %bitcast.93, f32[1,192]{1,0:T(1,128)} %bitcast.94, bf16[192,768]{1,0:T(8,128)(2,1)} %mlp_in_ref.1, ...), custom_call_target="tpu_custom_call" | custom-call | flops 254803968 | bytes 1105920 | tf_op jit(solution)/shard_map/pallas_call | solution.py:101
  66.7 1.0 %reshape.108 = bf16[64,6,192]{2,1,0:T(8,128)(2,1)S(1)} reshape(bf16[384,192]{1,0:T(8,128)(2,1)} %shard_map.167) | data formatting | bytes 294912 | tf_op jit(solution)/shard_map/reshape | solution.py:166
  67.7 17.5 %all_to_all.10 = bf16[64,6,192]{2,1,0:T(8,128)(2,1)S(1)} all-to-all(bf16[64,6,192]{2,1,0:T(8,128)(2,1)S(1)} %reshape.108), channel_id=1, replica_groups=mesh['rows'=64,'feat'=8] {'rows'}, dimensions={0} | all-to-all | bytes 294912 | tf_op jit(solution)/shard_map/all_to_all | solution.py:167
  85.3 0.7 copy.92
  86.0 0.6 copy.91
  (44 shorter events, 1.0 us)
Async XLA Ops:
  0.6 1.1 %copy-start = (bf16[192,576]{1,0:T(8,128)(2,1)S(1)}, bf16[192,576]{1,0:T(8,128)(2,1)}, u32[]{:S(2)}) copy-start(bf16[192,576]{1,0:T(8,128)(2,1)} %param.20) | copy-start | bytes 663556
  3.7 0.9 %copy-start.4 = (bf16[192,192]{1,0:T(8,128)(2,1)S(1)}, bf16[192,192]{1,0:T(8,128)(2,1)}, u32[]{:S(2)}) copy-start(bf16[192,192]{1,0:T(8,128)(2,1)} %param.21) | copy-start | bytes 221188
  3.7 1.2 %copy-start.6 = (f32[192]{0:T(256)S(1)}, f32[192]{0:T(256)}, u32[]{:S(2)}) copy-start(f32[192]{0:T(256)} %param.23) | copy-start | bytes 2308
  3.7 1.2 %copy-start.7 = (f32[192]{0:T(256)S(1)}, f32[192]{0:T(256)}, u32[]{:S(2)}) copy-start(f32[192]{0:T(256)} %param.22) | copy-start | bytes 2308
  4.0 1.2 %copy-start.5 = (s32[4,64]{1,0:T(4,128)S(1)}, s32[4,64]{1,0:T(4,128)}, u32[]{:S(2)}) copy-start(s32[4,64]{1,0:T(4,128)} %param.19) | copy-start | bytes 3076
  4.0 1.2 %copy-start.8 = (s32[2,64]{1,0:T(2,128)S(1)}, s32[2,64]{1,0:T(2,128)}, u32[]{:S(2)}) copy-start(s32[2,64]{1,0:T(2,128)} %param.18) | copy-start | bytes 1540
  4.0 15.4 %copy-start.2 = (bf16[768,192]{0,1:T(8,128)(2,1)S(1)}, bf16[768,192]{0,1:T(8,128)(2,1)}, u32[]{:S(2)}) copy-start(bf16[768,192]{0,1:T(8,128)(2,1)} %param.29) | copy-start | bytes 884740
  5.4 47.3 %copy-start.3 = (bf16[192,576]{1,0:T(8,128)(2,1)S(1)}, bf16[192,576]{1,0:T(8,128)(2,1)}, u32[]{:S(2)}) copy-start(bf16[192,576]{1,0:T(8,128)(2,1)} %param.24) | copy-start | bytes 663556
  6.3 23.3 %all-to-all-start = ((bf16[64,7,192]{2,1,0:T(8,128)(2,1)}), bf16[64,7,192]{2,1,0:T(8,128)(2,1)S(1)}, u32[]{:S(2)}, u32[]{:S(2)}) async-start(bf16[64,7,192]{2,1,0:T(8,128)(2,1)} %copy.83), calls=%async_computation | async-start | bytes 524288 | tf_op jit(solution)/shard_map/all_to_all | solution.py:144
  52.7 5.8 %copy-start.1 = (bf16[384,192]{1,0:T(8,128)(2,1)}, bf16[384,192]{1,0:T(8,128)(2,1)S(1)}, u32[]{:S(2)}) copy-start(bf16[384,192]{1,0:T(8,128)(2,1)S(1)} %reshape.99.rows_ref) | copy-start | bytes 442372

commit v8 on v7

--- a/solution.py
+++ b/solution.py
@@ -45,7 +45,7 @@
     return settled.astype(jnp.bfloat16).reshape(row_count, feat_count, model_width)
 
 
-def item_attention(query_rows, key_rows, key_marks, item_qkv):
+def item_attention(query_rows, key_rows, key_marks, row_gate, item_qkv):
     query_count, model_width = query_rows.shape
     key_count = key_rows.shape[0]
     head_size = model_width // HEADS
@@ -71,7 +71,7 @@
         key_values[:, 1],
         preferred_element_type=jnp.float32,
     )
-    attended = (weighted / totals[..., None]).astype(jnp.bfloat16)
+    attended = ((weighted * row_gate[None, :, None]) / totals[..., None]).astype(jnp.bfloat16)
     return jnp.transpose(attended, (1, 0, 2)).reshape(query_count, model_width)
 
 
@@ -156,10 +156,9 @@
     key_marks = gathered[:, local_keys, :local_keys].reshape(-1)
 
     query_rows = col_rows.reshape(source_count * row_count, model_width)
-    attended = item_attention(query_rows, key_rows, key_marks, item_qkv)
     is_train = (jnp.arange(row_count) < train_count)[None, :]
-    keep_gate = jnp.where(is_train, jnp.ones_like(col_marks), col_marks)
-    gated = attended * keep_gate.reshape(-1, 1)
+    keep_gate = jnp.where(is_train, jnp.ones_like(col_marks), col_marks).astype(jnp.float32)
+    gated = item_attention(query_rows, key_rows, key_marks, keep_gate.reshape(-1), item_qkv)
     result_rows = item_tail(
         gated, query_rows, item_out, item_gain, item_bias, mlp_in, mlp_out, mlp_gain, mlp_bias
     )

time: 87.1 us -> 87 us (level)
  no operation moved by 1% of the time
where the time goes in v8:
time: 87 us; the launch traced here: 86.5 us
  blocking collectives  39.8 us (46%)
  starting transfers between devices  12.9 us (15%)
  matrix products  11.1 us (13%)
  waiting for transfers between devices  9.2 us (11%)
  local copies, waits for them, and re-layouts  7.99 us (9%)
  Pallas kernels  3.21 us (4%)
  other arithmetic  1.27 us (1%)
  between operations  0.99 us (1%)
    all_gather x1, blocking collectives, per_device(): lax.all_gather(jnp.concatenate([train_rows, key_mark_row[None, :]], axis=...  22.3 us
    all_to_all x1, blocking collectives, per_device(): lax.all_to_all(result_rows, 'rows', split_axis=0, concat_axis=0, tiled=True)  17.5 us
    all_to_all x1, starting transfers between devices, per_device(): lax.all_to_all(outbound, 'rows', split_axis=0, concat_axis=0, tiled=True)  12.9 us
    all_to_all x1, waiting for transfers between devices, per_device(): lax.all_to_all(outbound, 'rows', split_axis=0, concat_axis=0, tiled=True)  9.2 us
    sub x1, matrix products, item_attention(): weights_exp = jnp.where(alive_keys, jnp.exp(masked - row_top), 0.0)  5 us
    dot_general x1, matrix products, item_attention(): jnp.einsum('hqk,khd->hqd', weights_exp.astype(jnp.bfloat16), key_values[:...  3.84 us
    pallas_call x1, Pallas kernels, item_tail(): pl.pallas_call(tail_kernel, out_shape=jax.ShapeDtypeStruct((cell_count, m...  3.21 us
    unnamed x22, local copies, waits for them, and re-layouts  2.44 us
  transfers between devices with their start and end apart: 1, of which 1 were waited for; matrix products, arithmetic and copies ran while one was open for 1% of the time, Pallas kernels for 0%

profile of v8, /device:TPU:1, one launch (start us, length us, event | category | flops | bytes accessed | tf_op | source)
XLA Modules:
  0.0 86.5 jit_solution(10931061653432044354)
XLA Ops:
  0.6 1.0 %pad_maximum_fusion.1 = bf16[6,64,192]{2,1,0:T(8,128)(2,1)S(1)} fusion(bf16[4,64,192]{2,1,0:T(8,128)(2,1)} %param.17, bf16[2,64,192]{2,1,0:T(8,128)(2,1)} %param.16), kind=kLoop, calls=%fused_computation.34 | loop fusion | flops 73728 | bytes 294912 | tf_op jit(solution)/shard_map/concatenate | solution.py:137
  1.6 0.1 copy.58
  1.8 0.4 convolution_convert_fusion.1
  2.1 0.6 reshape.94
  2.8 0.3 fusion.32
  3.1 0.6 fusion.33
  3.7 0.3 fusion.10
  4.0 0.2 copy.63
  4.3 0.3 reshape.95
  4.6 0.3 fusion.34
  5.0 0.1 add_convert_fusion
  5.1 0.1 copy.64
  5.5 0.8 copy.66
  6.3 12.9 %all-to-all-start = ((bf16[64,7,192]{2,1,0:T(8,128)(2,1)}), bf16[64,7,192]{2,1,0:T(8,128)(2,1)S(1)}, u32[]{:S(2)}, u32[]{:S(2)}) async-start(bf16[64,7,192]{2,1,0:T(8,128)(2,1)} %copy.66), calls=%async_computation | async-start | bytes 524288 | tf_op jit(solution)/shard_map/all_to_all | solution.py:144
  19.3 0.1 broadcast_in_dim.53
  19.4 0.9 %copy.72.mlp_out_ref = bf16[768,192]{1,0:T(8,128)(2,1)} copy(bf16[768,192]{0,1:T(8,128)(2,1)S(1)} %copy-done.2) | data formatting | bytes 589824 | tf_op args[13]
  20.4 9.2 %all-to-all-done = bf16[64,7,192]{2,1,0:T(8,128)(2,1)S(1)} async-done(((bf16[64,7,192]{2,1,0:T(8,128)(2,1)}), bf16[64,7,192]{2,1,0:T(8,128)(2,1)S(1)}, u32[]{:S(2)}, u32[]{:S(2)}) %all-to-all-start) | async-done | bytes 172064 | tf_op jit(solution)/shard_map/all_to_all | solution.py:144
  29.6 0.1 slice_reduce_fusion
  29.9 0.2 reshape.98
  30.2 22.3 %all-gather.1 = bf16[8,129,192]{2,1,0:T(8,128)(2,1)S(1)} all-gather(bf16[1,129,192]{2,1,0:T(8,128)(2,1)S(1)} %maximum_bitcast_fusion), channel_id=2, replica_groups=mesh['rows'=64,'feat'=8] {'feat'}, dimensions={0}, use_global_device_ids=true | all-gather | bytes 445824 | tf_op jit(solution)/shard_map/all_gather | solution.py:152
  52.6 0.1 reshape.99.rows_ref
  52.7 0.5 convolution_convert_fusion
  53.3 0.3 convolution_convert_fusion.3
  53.5 0.1 squeeze.26
  53.7 5.0 %fusion.35 = (f32[6,384]{1,0:T(8,128)S(1)}, bf16[6,384,1024]{2,1,0:T(8,128)(2,1)}) fusion(pred[1024]{0:T(1024)(128)(4,1)S(1)} %compare_bitcast_fusion, bf16[384,6,32]{0,2,1:T(8,128)(2,1)S(1)} %bitcast.89, bf16[1024,2,6,32]{0,3,2,1:T(8,128)(2,1)S(1)} %bitcast.86), kind=kOutput, calls=%fused_computation.53 | convolution fusion | flops 165151744 | bytes 5270528 | tf_op jit(solution)/shard_map/sub | solution.py:66
  58.7 3.8 %fusion.20 = bf16[384,6,32]{0,2,1:T(8,128)(2,1)S(1)} fusion(bf16[6,384,1024]{2,1,0:T(8,128)(2,1)} %get-tuple-element.18, bf16[1024,2,6,32]{0,3,2,1:T(8,128)(2,1)S(1)} %bitcast.87, f32[384,6]{0,1:T(8,128)S(1)} %bitcast.97, f32[384]{0:T(512)S(1)} %select_convert_fusion), kind=kOutput, calls=%fused_computation.23 | convolution fusion | flops 151216128 | bytes 5273600 | tf_op jit(solution)/shard_map/hqk,khd->hqd/dot_general | solution.py:68
  62.5 0.8 copy.71.mixed_ref
  63.3 3.2 %shard_map.167 = bf16[384,192]{1,0:T(8,128)(2,1)} custom-call(bf16[384,192]{1,0:T(8,128)(2,1)} %copy.71.mixed_ref, bf16[384,192]{1,0:T(8,128)(2,1)} %copy-done.1, bf16[192,192]{1,0:T(8,128)(2,1)} %item_out_ref.1, f32[1,192]{1,0:T(1,128)} %bitcast.93, f32[1,192]{1,0:T(1,128)} %bitcast.94, bf16[192,768]{1,0:T(8,128)(2,1)} %mlp_in_ref.1, ...), custom_call_target="tpu_custom_call" | custom-call | flops 254803968 | bytes 1105920 | tf_op jit(solution)/shard_map/pallas_call | solution.py:101
  66.6 1.0 %reshape.108 = bf16[64,6,192]{2,1,0:T(8,128)(2,1)S(1)} reshape(bf16[384,192]{1,0:T(8,128)(2,1)} %shard_map.167) | data formatting | bytes 294912 | tf_op jit(solution)/shard_map/reshape | solution.py:165
  67.6 17.5 %all_to_all.10 = bf16[64,6,192]{2,1,0:T(8,128)(2,1)S(1)} all-to-all(bf16[64,6,192]{2,1,0:T(8,128)(2,1)S(1)} %reshape.108), channel_id=1, replica_groups=mesh['rows'=64,'feat'=8] {'rows'}, dimensions={0} | all-to-all | bytes 294912 | tf_op jit(solution)/shard_map/all_to_all | solution.py:166
  85.2 0.7 copy.74
  85.9 0.6 copy.73
  (43 shorter events, 0.9 us)
Async XLA Ops:
  0.6 1.1 %copy-start = (bf16[192,576]{1,0:T(8,128)(2,1)S(1)}, bf16[192,576]{1,0:T(8,128)(2,1)}, u32[]{:S(2)}) copy-start(bf16[192,576]{1,0:T(8,128)(2,1)} %param.20) | copy-start | bytes 663556
  3.7 0.9 %copy-start.4 = (bf16[192,192]{1,0:T(8,128)(2,1)S(1)}, bf16[192,192]{1,0:T(8,128)(2,1)}, u32[]{:S(2)}) copy-start(bf16[192,192]{1,0:T(8,128)(2,1)} %param.21) | copy-start | bytes 221188
  3.7 1.2 %copy-start.6 = (f32[192]{0:T(256)S(1)}, f32[192]{0:T(256)}, u32[]{:S(2)}) copy-start(f32[192]{0:T(256)} %param.23) | copy-start | bytes 2308
  3.7 1.2 %copy-start.7 = (f32[192]{0:T(256)S(1)}, f32[192]{0:T(256)}, u32[]{:S(2)}) copy-start(f32[192]{0:T(256)} %param.22) | copy-start | bytes 2308
  4.0 1.2 %copy-start.5 = (s32[4,64]{1,0:T(4,128)S(1)}, s32[4,64]{1,0:T(4,128)}, u32[]{:S(2)}) copy-start(s32[4,64]{1,0:T(4,128)} %param.19) | copy-start | bytes 3076
  4.0 1.2 %copy-start.8 = (s32[2,64]{1,0:T(2,128)S(1)}, s32[2,64]{1,0:T(2,128)}, u32[]{:S(2)}) copy-start(s32[2,64]{1,0:T(2,128)} %param.18) | copy-start | bytes 1540
  4.0 15.4 %copy-start.2 = (bf16[768,192]{0,1:T(8,128)(2,1)S(1)}, bf16[768,192]{0,1:T(8,128)(2,1)}, u32[]{:S(2)}) copy-start(bf16[768,192]{0,1:T(8,128)(2,1)} %param.29) | copy-start | bytes 884740
  5.4 47.3 %copy-start.3 = (bf16[192,576]{1,0:T(8,128)(2,1)S(1)}, bf16[192,576]{1,0:T(8,128)(2,1)}, u32[]{:S(2)}) copy-start(bf16[192,576]{1,0:T(8,128)(2,1)} %param.24) | copy-start | bytes 663556
  6.3 23.3 %all-to-all-start = ((bf16[64,7,192]{2,1,0:T(8,128)(2,1)}), bf16[64,7,192]{2,1,0:T(8,128)(2,1)S(1)}, u32[]{:S(2)}, u32[]{:S(2)}) async-start(bf16[64,7,192]{2,1,0:T(8,128)(2,1)} %copy.66), calls=%async_computation | async-start | bytes 524288 | tf_op jit(solution)/shard_map/all_to_all | solution.py:144
  52.7 6.0 %copy-start.1 = (bf16[384,192]{1,0:T(8,128)(2,1)}, bf16[384,192]{1,0:T(8,128)(2,1)S(1)}, u32[]{:S(2)}) copy-start(bf16[384,192]{1,0:T(8,128)(2,1)S(1)} %reshape.99.rows_ref) | copy-start | bytes 442372

commit v9 on v8

--- a/solution.py
+++ b/solution.py
@@ -72,14 +72,17 @@
         preferred_element_type=jnp.float32,
     )
     attended = ((weighted * row_gate[None, :, None]) / totals[..., None]).astype(jnp.bfloat16)
-    return jnp.transpose(attended, (1, 0, 2)).reshape(query_count, model_width)
+    return jnp.transpose(attended, (0, 2, 1)).reshape(model_width, query_count)
 
 
 def tail_kernel(
     mixed_ref, rows_ref, item_out_ref, item_gain_ref, item_bias_ref,
     mlp_in_ref, mlp_out_ref, mlp_gain_ref, mlp_bias_ref, out_ref,
 ):
-    branch = jnp.dot(mixed_ref[...], item_out_ref[...], preferred_element_type=jnp.float32)
+    branch = lax.dot_general(
+        mixed_ref[...], item_out_ref[...], (((0,), (0,)), ((), ())),
+        preferred_element_type=jnp.float32,
+    )
     settled = layer_norm(
         rows_ref[...].astype(jnp.float32) + branch, item_gain_ref[...], item_bias_ref[...]
     ).astype(jnp.bfloat16)

time: 87 us -> 86.8 us (level)
  no operation moved by 1% of the time
where the time goes in v9:
time: 86.8 us; the launch traced here: 86.3 us
  blocking collectives  39.8 us (46%)
  starting transfers between devices  12.9 us (15%)
  matrix products  11.8 us (14%)
  waiting for transfers between devices  9.2 us (11%)
  local copies, waits for them, and re-layouts  7.17 us (8%)
  Pallas kernels  3.2 us (4%)
  other arithmetic  1.27 us (1%)
  between operations  0.98 us (1%)
    all_gather x1, blocking collectives, per_device(): lax.all_gather(jnp.concatenate([train_rows, key_mark_row[None, :]], axis=...  22.3 us
    all_to_all x1, blocking collectives, per_device(): lax.all_to_all(result_rows, 'rows', split_axis=0, concat_axis=0, tiled=True)  17.5 us
    all_to_all x1, starting transfers between devices, per_device(): lax.all_to_all(outbound, 'rows', split_axis=0, concat_axis=0, tiled=True)  12.9 us
    all_to_all x1, waiting for transfers between devices, per_device(): lax.all_to_all(outbound, 'rows', split_axis=0, concat_axis=0, tiled=True)  9.2 us
    sub x1, matrix products, item_attention(): weights_exp = jnp.where(alive_keys, jnp.exp(masked - row_top), 0.0)  5.01 us
    dot_general x1, matrix products, item_attention(): jnp.einsum('hqk,khd->hqd', weights_exp.astype(jnp.bfloat16), key_values[:...  4.49 us
    pallas_call x1, Pallas kernels, item_tail(): pl.pallas_call(tail_kernel, out_shape=jax.ShapeDtypeStruct((cell_count, m...  3.2 us
    unnamed x22, local copies, waits for them, and re-layouts  2.44 us
  transfers between devices with their start and end apart: 1, of which 1 were waited for; matrix products, arithmetic and copies ran while one was open for 1% of the time, Pallas kernels for 0%

profile of v9, /device:TPU:1, one launch (start us, length us, event | category | flops | bytes accessed | tf_op | source)
XLA Modules:
  0.0 86.3 jit_solution(16830510061156760926)
XLA Ops:
  0.6 1.0 %pad_maximum_fusion.1 = bf16[6,64,192]{2,1,0:T(8,128)(2,1)S(1)} fusion(bf16[4,64,192]{2,1,0:T(8,128)(2,1)} %param.17, bf16[2,64,192]{2,1,0:T(8,128)(2,1)} %param.16), kind=kLoop, calls=%fused_computation.33 | loop fusion | flops 73728 | bytes 294912 | tf_op jit(solution)/shard_map/concatenate | solution.py:140
  1.6 0.1 copy.55
  1.8 0.4 convolution_convert_fusion.1
  2.1 0.6 reshape.94
  2.8 0.3 fusion.29
  3.1 0.6 fusion.30
  3.7 0.3 fusion.10
  4.0 0.2 copy.60
  4.3 0.3 reshape.95
  4.6 0.3 fusion.31
  5.0 0.1 add_convert_fusion
  5.1 0.1 copy.61
  5.5 0.8 copy.63
  6.3 12.9 %all-to-all-start = ((bf16[64,7,192]{2,1,0:T(8,128)(2,1)}), bf16[64,7,192]{2,1,0:T(8,128)(2,1)S(1)}, u32[]{:S(2)}, u32[]{:S(2)}) async-start(bf16[64,7,192]{2,1,0:T(8,128)(2,1)} %copy.63), calls=%async_computation | async-start | bytes 524288 | tf_op jit(solution)/shard_map/all_to_all | solution.py:147
  19.3 0.1 broadcast_in_dim.53
  19.4 0.9 %copy.68.mlp_out_ref = bf16[768,192]{1,0:T(8,128)(2,1)} copy(bf16[768,192]{0,1:T(8,128)(2,1)S(1)} %copy-done.2) | data formatting | bytes 589824 | tf_op args[13]
  20.4 9.2 %all-to-all-done = bf16[64,7,192]{2,1,0:T(8,128)(2,1)S(1)} async-done(((bf16[64,7,192]{2,1,0:T(8,128)(2,1)}), bf16[64,7,192]{2,1,0:T(8,128)(2,1)S(1)}, u32[]{:S(2)}, u32[]{:S(2)}) %all-to-all-start) | async-done | bytes 172064 | tf_op jit(solution)/shard_map/all_to_all | solution.py:147
  29.6 0.1 slice_reduce_fusion
  29.8 0.1 copy.65
  29.9 0.2 reshape.98
  30.2 22.3 %all-gather.1 = bf16[8,129,192]{2,1,0:T(8,128)(2,1)S(1)} all-gather(bf16[1,129,192]{2,1,0:T(8,128)(2,1)S(1)} %maximum_bitcast_fusion), channel_id=2, replica_groups=mesh['rows'=64,'feat'=8] {'feat'}, dimensions={0}, use_global_device_ids=true | all-gather | bytes 445824 | tf_op jit(solution)/shard_map/all_gather | solution.py:155
  52.6 0.1 reshape.101.rows_ref
  52.7 0.5 convolution_convert_fusion
  53.3 0.3 convolution_convert_fusion.3
  53.5 0.1 squeeze.26
  53.7 5.0 %fusion.32 = (f32[6,384]{1,0:T(8,128)S(1)}, bf16[6,384,1024]{2,1,0:T(8,128)(2,1)}) fusion(pred[1024]{0:T(1024)(128)(4,1)S(1)} %compare_bitcast_fusion, bf16[384,6,32]{0,2,1:T(8,128)(2,1)S(1)} %bitcast.83, bf16[1024,2,6,32]{0,3,2,1:T(8,128)(2,1)S(1)} %bitcast.76), kind=kOutput, calls=%fused_computation.52 | convolution fusion | flops 165151744 | bytes 5270528 | tf_op jit(solution)/shard_map/sub | solution.py:66
  58.7 4.5 %fusion.17 = bf16[6,32,384]{2,1,0:T(8,128)(2,1)} fusion(bf16[6,384,1024]{2,1,0:T(8,128)(2,1)} %get-tuple-element.18, bf16[1024,2,6,32]{0,3,2,1:T(8,128)(2,1)S(1)} %bitcast.77, f32[6,384]{1,0:T(8,128)S(1)} %get-tuple-element.17, f32[384]{0:T(512)S(1)} %select_convert_fusion), kind=kOutput, calls=%fused_computation.22 | convolution fusion | flops 151216128 | bytes 5273600 | tf_op jit(solution)/shard_map/hqk,khd->hqd/dot_general | solution.py:68
  63.2 3.2 %shard_map.167 = bf16[384,192]{1,0:T(8,128)(2,1)} custom-call(bf16[192,384]{1,0:T(8,128)(2,1)} %bitcast.82, bf16[384,192]{1,0:T(8,128)(2,1)} %copy-done.1, bf16[192,192]{1,0:T(8,128)(2,1)} %item_out_ref.1, f32[1,192]{1,0:T(1,128)} %bitcast.86, f32[1,192]{1,0:T(1,128)} %bitcast.87, bf16[192,768]{1,0:T(8,128)(2,1)} %mlp_in_ref.1, ...), custom_call_target="tpu_custom_call" | custom-call | flops 254803968 | bytes 1105920 | tf_op jit(solution)/shard_map/pallas_call | solution.py:104
  66.4 1.0 %reshape.108 = bf16[64,6,192]{2,1,0:T(8,128)(2,1)S(1)} reshape(bf16[384,192]{1,0:T(8,128)(2,1)} %shard_map.167) | data formatting | bytes 294912 | tf_op jit(solution)/shard_map/reshape | solution.py:168
  67.4 17.5 %all_to_all.10 = bf16[64,6,192]{2,1,0:T(8,128)(2,1)S(1)} all-to-all(bf16[64,6,192]{2,1,0:T(8,128)(2,1)S(1)} %reshape.108), channel_id=1, replica_groups=mesh['rows'=64,'feat'=8] {'rows'}, dimensions={0} | all-to-all | bytes 294912 | tf_op jit(solution)/shard_map/all_to_all | solution.py:169
  85.0 0.7 copy.70
  85.7 0.6 copy.69
  (42 shorter events, 0.8 us)
Async XLA Ops:
  0.6 1.1 %copy-start = (bf16[192,576]{1,0:T(8,128)(2,1)S(1)}, bf16[192,576]{1,0:T(8,128)(2,1)}, u32[]{:S(2)}) copy-start(bf16[192,576]{1,0:T(8,128)(2,1)} %param.20) | copy-start | bytes 663556
  3.7 0.9 %copy-start.4 = (bf16[192,192]{1,0:T(8,128)(2,1)S(1)}, bf16[192,192]{1,0:T(8,128)(2,1)}, u32[]{:S(2)}) copy-start(bf16[192,192]{1,0:T(8,128)(2,1)} %param.21) | copy-start | bytes 221188
  3.7 1.2 %copy-start.6 = (f32[192]{0:T(256)S(1)}, f32[192]{0:T(256)}, u32[]{:S(2)}) copy-start(f32[192]{0:T(256)} %param.23) | copy-start | bytes 2308
  3.7 1.2 %copy-start.7 = (f32[192]{0:T(256)S(1)}, f32[192]{0:T(256)}, u32[]{:S(2)}) copy-start(f32[192]{0:T(256)} %param.22) | copy-start | bytes 2308
  4.0 1.2 %copy-start.5 = (s32[4,64]{1,0:T(4,128)S(1)}, s32[4,64]{1,0:T(4,128)}, u32[]{:S(2)}) copy-start(s32[4,64]{1,0:T(4,128)} %param.19) | copy-start | bytes 3076
  4.0 1.2 %copy-start.8 = (s32[2,64]{1,0:T(2,128)S(1)}, s32[2,64]{1,0:T(2,128)}, u32[]{:S(2)}) copy-start(s32[2,64]{1,0:T(2,128)} %param.18) | copy-start | bytes 1540
  4.0 15.4 %copy-start.2 = (bf16[768,192]{0,1:T(8,128)(2,1)S(1)}, bf16[768,192]{0,1:T(8,128)(2,1)}, u32[]{:S(2)}) copy-start(bf16[768,192]{0,1:T(8,128)(2,1)} %param.29) | copy-start | bytes 884740
  5.4 47.3 %copy-start.3 = (bf16[192,576]{1,0:T(8,128)(2,1)S(1)}, bf16[192,576]{1,0:T(8,128)(2,1)}, u32[]{:S(2)}) copy-start(bf16[192,576]{1,0:T(8,128)(2,1)} %param.24) | copy-start | bytes 663556
  6.3 23.3 %all-to-all-start = ((bf16[64,7,192]{2,1,0:T(8,128)(2,1)}), bf16[64,7,192]{2,1,0:T(8,128)(2,1)S(1)}, u32[]{:S(2)}, u32[]{:S(2)}) async-start(bf16[64,7,192]{2,1,0:T(8,128)(2,1)} %copy.63), calls=%async_computation | async-start | bytes 524288 | tf_op jit(solution)/shard_map/all_to_all | solution.py:147
  52.7 6.0 %copy-start.1 = (bf16[384,192]{1,0:T(8,128)(2,1)}, bf16[384,192]{1,0:T(8,128)(2,1)S(1)}, u32[]{:S(2)}) copy-start(bf16[384,192]{1,0:T(8,128)(2,1)S(1)} %reshape.101.rows_ref) | copy-start | bytes 442372

commit v10 on v9

--- a/solution.py
+++ b/solution.py
@@ -94,16 +94,22 @@
         mlp_gain_ref[...],
         mlp_bias_ref[...],
     )
-    out_ref[...] = result.astype(out_ref.dtype)
-
-
-def item_tail(mixed, rows, item_out, item_gain, item_bias, mlp_in, mlp_out, mlp_gain, mlp_bias):
+    source_count, row_count = out_ref.shape[0], out_ref.shape[1]
+    for source in range(source_count):
+        out_ref[source] = result[source * row_count:(source + 1) * row_count].astype(out_ref.dtype)
+
+
+def item_tail(
+    mixed, rows, item_out, item_gain, item_bias, mlp_in, mlp_out, mlp_gain, mlp_bias, source_count
+):
     cell_count, model_width = rows.shape
     hidden_width = mlp_in.shape[1]
     as_row = lambda vector: vector.reshape(1, model_width)
     return pl.pallas_call(
         tail_kernel,
-        out_shape=jax.ShapeDtypeStruct((cell_count, model_width), jnp.bfloat16),
+        out_shape=jax.ShapeDtypeStruct(
+            (source_count, cell_count // source_count, model_width), jnp.bfloat16
+        ),
         cost_estimate=pl.CostEstimate(
             flops=2 * cell_count * model_width * (model_width + 2 * hidden_width),
             transcendentals=cell_count * hidden_width,
@@ -163,9 +169,9 @@
     keep_gate = jnp.where(is_train, jnp.ones_like(col_marks), col_marks).astype(jnp.float32)
     gated = item_attention(query_rows, key_rows, key_marks, keep_gate.reshape(-1), item_qkv)
     result_rows = item_tail(
-        gated, query_rows, item_out, item_gain, item_bias, mlp_in, mlp_out, mlp_gain, mlp_bias
-    )
-    result_rows = result_rows.reshape(source_count, row_count, model_width)
+        gated, query_rows, item_out, item_gain, item_bias, mlp_in, mlp_out, mlp_gain, mlp_bias,
+        source_count,
+    )
     returned = lax.all_to_all(result_rows, "rows", split_axis=0, concat_axis=0, tiled=True)
     final = jnp.swapaxes(returned, 0, 1)
     return (final[:train_count], final[train_count:])

time: 86.8 us -> 86 us (level)
  local copies, waits for them, and re-layouts: 7.17 us -> 6.16 us
    reshape x1 -> x0, local copies, waits for them, and re-layouts: 1.01 us -> none  [per_device(): result_rows = result_rows.reshape(source_count, row_count, model_width)]
where the time goes in v10:
time: 86 us; the launch traced here: 85.5 us
  blocking collectives  40 us (47%)
  starting transfers between devices  12.9 us (15%)
  matrix products  11.8 us (14%)
  waiting for transfers between devices  9.2 us (11%)
  local copies, waits for them, and re-layouts  6.16 us (7%)
  Pallas kernels  3.23 us (4%)
  other arithmetic  1.27 us (1%)
  between operations  0.97 us (1%)
    all_gather x1, blocking collectives, per_device(): lax.all_gather(jnp.concatenate([train_rows, key_mark_row[None, :]], axis=...  22.3 us
    all_to_all x1, blocking collectives, per_device(): lax.all_to_all(result_rows, 'rows', split_axis=0, concat_axis=0, tiled=True)  17.7 us
    all_to_all x1, starting transfers between devices, per_device(): lax.all_to_all(outbound, 'rows', split_axis=0, concat_axis=0, tiled=True)  12.9 us
    all_to_all x1, waiting for transfers between devices, per_device(): lax.all_to_all(outbound, 'rows', split_axis=0, concat_axis=0, tiled=True)  9.2 us
    sub x1, matrix products, item_attention(): weights_exp = jnp.where(alive_keys, jnp.exp(masked - row_top), 0.0)  5.01 us
    dot_general x1, matrix products, item_attention(): jnp.einsum('hqk,khd->hqd', weights_exp.astype(jnp.bfloat16), key_values[:...  4.49 us
    pallas_call x1, Pallas kernels, item_tail(): pl.pallas_call(tail_kernel, out_shape=jax.ShapeDtypeStruct((source_count,...  3.23 us
    unnamed x22, local copies, waits for them, and re-layouts  2.44 us
  transfers between devices with their start and end apart: 1, of which 1 were waited for; matrix products, arithmetic and copies ran while one was open for 1% of the time, Pallas kernels for 0%

profile of v10, /device:TPU:1, one launch (start us, length us, event | category | flops | bytes accessed | tf_op | source)
XLA Modules:
  0.0 85.5 jit_solution(5297966222821562975)
XLA Ops:
  0.6 1.0 %pad_maximum_fusion.1 = bf16[6,64,192]{2,1,0:T(8,128)(2,1)S(1)} fusion(bf16[4,64,192]{2,1,0:T(8,128)(2,1)} %param.17, bf16[2,64,192]{2,1,0:T(8,128)(2,1)} %param.16), kind=kLoop, calls=%fused_computation.33 | loop fusion | flops 73728 | bytes 294912 | tf_op jit(solution)/shard_map/concatenate | solution.py:146
  1.6 0.1 copy.56
  1.8 0.4 convolution_convert_fusion.1
  2.1 0.6 reshape.91
  2.8 0.3 fusion.29
  3.1 0.6 fusion.30
  3.7 0.3 fusion.10
  4.0 0.2 copy.61
  4.3 0.3 reshape.92
  4.6 0.3 fusion.31
  5.0 0.1 add_convert_fusion
  5.1 0.1 copy.62
  5.3 0.1 copy.63
  5.5 0.8 copy.64
  6.3 12.9 %all-to-all-start = ((bf16[64,7,192]{2,1,0:T(8,128)(2,1)}), bf16[64,7,192]{2,1,0:T(8,128)(2,1)S(1)}, u32[]{:S(2)}, u32[]{:S(2)}) async-start(bf16[64,7,192]{2,1,0:T(8,128)(2,1)} %copy.64), calls=%async_computation | async-start | bytes 524288 | tf_op jit(solution)/shard_map/all_to_all | solution.py:153
  19.3 0.1 broadcast_in_dim.53
  19.4 0.9 %copy.69.mlp_out_ref = bf16[768,192]{1,0:T(8,128)(2,1)} copy(bf16[768,192]{0,1:T(8,128)(2,1)S(1)} %copy-done.2) | data formatting | bytes 589824 | tf_op args[13]
  20.4 9.2 %all-to-all-done = bf16[64,7,192]{2,1,0:T(8,128)(2,1)S(1)} async-done(((bf16[64,7,192]{2,1,0:T(8,128)(2,1)}), bf16[64,7,192]{2,1,0:T(8,128)(2,1)S(1)}, u32[]{:S(2)}, u32[]{:S(2)}) %all-to-all-start) | async-done | bytes 172064 | tf_op jit(solution)/shard_map/all_to_all | solution.py:153
  29.6 0.1 slice_reduce_fusion
  29.8 0.1 copy.66
  29.9 0.2 reshape.95
  30.2 22.3 %all-gather.1 = bf16[8,129,192]{2,1,0:T(8,128)(2,1)S(1)} all-gather(bf16[1,129,192]{2,1,0:T(8,128)(2,1)S(1)} %maximum_bitcast_fusion), channel_id=2, replica_groups=mesh['rows'=64,'feat'=8] {'feat'}, dimensions={0}, use_global_device_ids=true | all-gather | bytes 445824 | tf_op jit(solution)/shard_map/all_gather | solution.py:161
  52.6 0.1 reshape.98.rows_ref
  52.7 0.5 convolution_convert_fusion
  53.3 0.3 convolution_convert_fusion.3
  53.5 0.1 squeeze.26
  53.7 5.0 %fusion.32 = (f32[6,384]{1,0:T(8,128)S(1)}, bf16[6,384,1024]{2,1,0:T(8,128)(2,1)}) fusion(pred[1024]{0:T(1024)(128)(4,1)S(1)} %compare_bitcast_fusion, bf16[384,6,32]{0,2,1:T(8,128)(2,1)S(1)} %bitcast.83, bf16[1024,2,6,32]{0,3,2,1:T(8,128)(2,1)S(1)} %bitcast.76), kind=kOutput, calls=%fused_computation.52 | convolution fusion | flops 165151744 | bytes 5270528 | tf_op jit(solution)/shard_map/sub | solution.py:66
  58.7 4.5 %fusion.17 = bf16[6,32,384]{2,1,0:T(8,128)(2,1)} fusion(bf16[6,384,1024]{2,1,0:T(8,128)(2,1)} %get-tuple-element.20, bf16[1024,2,6,32]{0,3,2,1:T(8,128)(2,1)S(1)} %bitcast.77, f32[6,384]{1,0:T(8,128)S(1)} %get-tuple-element.19, f32[384]{0:T(512)S(1)} %select_convert_fusion), kind=kOutput, calls=%fused_computation.22 | convolution fusion | flops 151216128 | bytes 5273600 | tf_op jit(solution)/shard_map/hqk,khd->hqd/dot_general | solution.py:68
  63.2 3.2 %shard_map.167 = bf16[64,6,192]{2,1,0:T(8,128)(2,1)} custom-call(bf16[192,384]{1,0:T(8,128)(2,1)} %bitcast.82, bf16[384,192]{1,0:T(8,128)(2,1)} %copy-done.1, bf16[192,192]{1,0:T(8,128)(2,1)} %item_out_ref.1, f32[1,192]{1,0:T(1,128)} %bitcast.86, f32[1,192]{1,0:T(1,128)} %bitcast.87, bf16[192,768]{1,0:T(8,128)(2,1)} %mlp_in_ref.1, ...), custom_call_target="tpu_custom_call" | custom-call | flops 254803968 | bytes 1105920 | tf_op jit(solution)/shard_map/pallas_call | solution.py:108
  66.4 17.7 %all_to_all.10 = bf16[64,6,192]{2,1,0:T(8,128)(2,1)S(1)} all-to-all(bf16[64,6,192]{2,1,0:T(8,128)(2,1)} %shard_map.167), channel_id=1, replica_groups=mesh['rows'=64,'feat'=8] {'rows'}, dimensions={0} | all-to-all | bytes 294912 | tf_op jit(solution)/shard_map/all_to_all | solution.py:175
  84.2 0.7 copy.71
  84.9 0.6 copy.70
  (41 shorter events, 0.7 us)
Async XLA Ops:
  0.6 1.1 %copy-start = (bf16[192,576]{1,0:T(8,128)(2,1)S(1)}, bf16[192,576]{1,0:T(8,128)(2,1)}, u32[]{:S(2)}) copy-start(bf16[192,576]{1,0:T(8,128)(2,1)} %param.20) | copy-start | bytes 663556
  3.7 0.9 %copy-start.4 = (bf16[192,192]{1,0:T(8,128)(2,1)S(1)}, bf16[192,192]{1,0:T(8,128)(2,1)}, u32[]{:S(2)}) copy-start(bf16[192,192]{1,0:T(8,128)(2,1)} %param.21) | copy-start | bytes 221188
  3.7 1.2 %copy-start.6 = (f32[192]{0:T(256)S(1)}, f32[192]{0:T(256)}, u32[]{:S(2)}) copy-start(f32[192]{0:T(256)} %param.23) | copy-start | bytes 2308
  3.7 1.2 %copy-start.7 = (f32[192]{0:T(256)S(1)}, f32[192]{0:T(256)}, u32[]{:S(2)}) copy-start(f32[192]{0:T(256)} %param.22) | copy-start | bytes 2308
  4.0 1.2 %copy-start.5 = (s32[4,64]{1,0:T(4,128)S(1)}, s32[4,64]{1,0:T(4,128)}, u32[]{:S(2)}) copy-start(s32[4,64]{1,0:T(4,128)} %param.19) | copy-start | bytes 3076
  4.0 1.2 %copy-start.8 = (s32[2,64]{1,0:T(2,128)S(1)}, s32[2,64]{1,0:T(2,128)}, u32[]{:S(2)}) copy-start(s32[2,64]{1,0:T(2,128)} %param.18) | copy-start | bytes 1540
  4.0 15.4 %copy-start.2 = (bf16[768,192]{0,1:T(8,128)(2,1)S(1)}, bf16[768,192]{0,1:T(8,128)(2,1)}, u32[]{:S(2)}) copy-start(bf16[768,192]{0,1:T(8,128)(2,1)} %param.29) | copy-start | bytes 884740
  5.4 47.3 %copy-start.3 = (bf16[192,576]{1,0:T(8,128)(2,1)S(1)}, bf16[192,576]{1,0:T(8,128)(2,1)}, u32[]{:S(2)}) copy-start(bf16[192,576]{1,0:T(8,128)(2,1)} %param.24) | copy-start | bytes 663556
  6.3 23.3 %all-to-all-start = ((bf16[64,7,192]{2,1,0:T(8,128)(2,1)}), bf16[64,7,192]{2,1,0:T(8,128)(2,1)S(1)}, u32[]{:S(2)}, u32[]{:S(2)}) async-start(bf16[64,7,192]{2,1,0:T(8,128)(2,1)} %copy.64), calls=%async_computation | async-start | bytes 524288 | tf_op jit(solution)/shard_map/all_to_all | solution.py:153
  52.7 6.0 %copy-start.1 = (bf16[384,192]{1,0:T(8,128)(2,1)}, bf16[384,192]{1,0:T(8,128)(2,1)S(1)}, u32[]{:S(2)}) copy-start(bf16[384,192]{1,0:T(8,128)(2,1)S(1)} %reshape.98.rows_ref) | copy-start | bytes 442372

commit v11 on v10

--- a/solution.py
+++ b/solution.py
@@ -145,8 +145,10 @@
     feat_count, model_width = train_cells.shape[1], train_cells.shape[2]
     both_rows = jnp.concatenate([train_cells, test_cells], axis=0)
     settled = feature_block(both_rows, feat_qkv, feat_out, feat_gain, feat_bias)
-    marks = jnp.concatenate([train_mask, test_mask], axis=0).astype(jnp.bfloat16)
-    mark_row = jnp.pad(jnp.transpose(marks), ((0, 0), (0, model_width - row_count)))
+    live = jnp.transpose(jnp.concatenate([train_mask, test_mask], axis=0)) > 0
+    mark_row = jnp.pad(
+        jnp.where(live, 1.0, 0.0).astype(jnp.bfloat16), ((0, 0), (0, model_width - row_count))
+    )
     outbound = jnp.concatenate(
         [jnp.swapaxes(settled, 0, 1), mark_row[:, None, :]], axis=1
     )

time: 86 us -> 86 us (level)
  no operation moved by 1% of the time
where the time goes in v11:
time: 86 us; the launch traced here: 85.5 us
  blocking collectives  40 us (47%)
  starting transfers between devices  12.9 us (15%)
  matrix products  11.8 us (14%)
  waiting for transfers between devices  9.2 us (11%)
  local copies, waits for them, and re-layouts  6.14 us (7%)
  Pallas kernels  3.23 us (4%)
  other arithmetic  1.26 us (1%)
  between operations  0.97 us (1%)
    all_gather x1, blocking collectives, per_device(): lax.all_gather(jnp.concatenate([train_rows, key_mark_row[None, :]], axis=...  22.3 us
    all_to_all x1, blocking collectives, per_device(): lax.all_to_all(result_rows, 'rows', split_axis=0, concat_axis=0, tiled=True)  17.7 us
    all_to_all x1, starting transfers between devices, per_device(): lax.all_to_all(outbound, 'rows', split_axis=0, concat_axis=0, tiled=True)  12.9 us
    all_to_all x1, waiting for transfers between devices, per_device(): lax.all_to_all(outbound, 'rows', split_axis=0, concat_axis=0, tiled=True)  9.2 us
    sub x1, matrix products, item_attention(): weights_exp = jnp.where(alive_keys, jnp.exp(masked - row_top), 0.0)  5.01 us
    dot_general x1, matrix products, item_attention(): jnp.einsum('hqk,khd->hqd', weights_exp.astype(jnp.bfloat16), key_values[:...  4.49 us
    pallas_call x1, Pallas kernels, item_tail(): pl.pallas_call(tail_kernel, out_shape=jax.ShapeDtypeStruct((source_count,...  3.23 us
    unnamed x22, local copies, waits for them, and re-layouts  2.43 us
  transfers between devices with their start and end apart: 1, of which 1 were waited for; matrix products, arithmetic and copies ran while one was open for 1% of the time, Pallas kernels for 0%

profile of v11, /device:TPU:1, one launch (start us, length us, event | category | flops | bytes accessed | tf_op | source)
XLA Modules:
  0.0 85.5 jit_solution(17701567696221489002)
XLA Ops:
  0.6 1.0 %pad_maximum_fusion.1 = bf16[6,64,192]{2,1,0:T(8,128)(2,1)S(1)} fusion(bf16[4,64,192]{2,1,0:T(8,128)(2,1)} %param.17, bf16[2,64,192]{2,1,0:T(8,128)(2,1)} %param.16), kind=kLoop, calls=%fused_computation.33 | loop fusion | flops 73728 | bytes 294912 | tf_op jit(solution)/shard_map/concatenate | solution.py:146
  1.6 0.1 copy.78
  1.8 0.4 convolution_convert_fusion.1
  2.1 0.6 reshape.91
  2.8 0.3 fusion.30
  3.1 0.6 fusion.31
  3.7 0.3 fusion.10
  4.0 0.2 copy.83
  4.3 0.3 reshape.92
  4.6 0.3 fusion.32
  5.0 0.1 add_convert_fusion
  5.1 0.1 copy.84
  5.3 0.1 copy.85
  5.4 0.8 copy.86
  6.3 12.9 %all-to-all-start = ((bf16[64,7,192]{2,1,0:T(8,128)(2,1)}), bf16[64,7,192]{2,1,0:T(8,128)(2,1)S(1)}, u32[]{:S(2)}, u32[]{:S(2)}) async-start(bf16[64,7,192]{2,1,0:T(8,128)(2,1)} %copy.86), calls=%async_computation | async-start | bytes 524288 | tf_op jit(solution)/shard_map/all_to_all | solution.py:155
  19.2 0.1 broadcast_in_dim.63
  19.4 0.9 %copy.91.mlp_out_ref = bf16[768,192]{1,0:T(8,128)(2,1)} copy(bf16[768,192]{0,1:T(8,128)(2,1)S(1)} %copy-done.2) | data formatting | bytes 589824 | tf_op args[13]
  20.3 9.2 %all-to-all-done = bf16[64,7,192]{2,1,0:T(8,128)(2,1)S(1)} async-done(((bf16[64,7,192]{2,1,0:T(8,128)(2,1)}), bf16[64,7,192]{2,1,0:T(8,128)(2,1)S(1)}, u32[]{:S(2)}, u32[]{:S(2)}) %all-to-all-start) | async-done | bytes 172064 | tf_op jit(solution)/shard_map/all_to_all | solution.py:155
  29.5 0.1 slice_reduce_fusion
  29.7 0.1 copy.88
  29.9 0.2 reshape.95
  30.2 22.3 %all-gather.1 = bf16[8,129,192]{2,1,0:T(8,128)(2,1)S(1)} all-gather(bf16[1,129,192]{2,1,0:T(8,128)(2,1)S(1)} %maximum_bitcast_fusion), channel_id=2, replica_groups=mesh['rows'=64,'feat'=8] {'feat'}, dimensions={0}, use_global_device_ids=true | all-gather | bytes 445824 | tf_op jit(solution)/shard_map/all_gather | solution.py:163
  52.5 0.1 reshape.98.rows_ref
  52.7 0.6 convolution_convert_fusion
  53.2 0.3 convolution_convert_fusion.3
  53.5 0.1 squeeze.26
  53.7 5.0 %fusion.33 = (f32[6,384]{1,0:T(8,128)S(1)}, bf16[6,384,1024]{2,1,0:T(8,128)(2,1)}) fusion(pred[1024]{0:T(1024)(128)(4,1)S(1)} %compare_bitcast_fusion, bf16[384,6,32]{0,2,1:T(8,128)(2,1)S(1)} %bitcast.84, bf16[1024,2,6,32]{0,3,2,1:T(8,128)(2,1)S(1)} %bitcast.77), kind=kOutput, calls=%fused_computation.54 | convolution fusion | flops 165151744 | bytes 5270528 | tf_op jit(solution)/shard_map/sub | solution.py:66
  58.7 4.5 %fusion.17 = bf16[6,32,384]{2,1,0:T(8,128)(2,1)} fusion(bf16[6,384,1024]{2,1,0:T(8,128)(2,1)} %get-tuple-element.22, bf16[1024,2,6,32]{0,3,2,1:T(8,128)(2,1)S(1)} %bitcast.78, f32[6,384]{1,0:T(8,128)S(1)} %get-tuple-element.21, f32[384]{0:T(512)S(1)} %select_convert_fusion.1), kind=kOutput, calls=%fused_computation.22 | convolution fusion | flops 151216128 | bytes 5273600 | tf_op jit(solution)/shard_map/hqk,khd->hqd/dot_general | solution.py:68
  63.2 3.2 %shard_map.167 = bf16[64,6,192]{2,1,0:T(8,128)(2,1)} custom-call(bf16[192,384]{1,0:T(8,128)(2,1)} %bitcast.83, bf16[384,192]{1,0:T(8,128)(2,1)} %copy-done.1, bf16[192,192]{1,0:T(8,128)(2,1)} %item_out_ref.1, f32[1,192]{1,0:T(1,128)} %bitcast.86, f32[1,192]{1,0:T(1,128)} %bitcast.87, bf16[192,768]{1,0:T(8,128)(2,1)} %mlp_in_ref.1, ...), custom_call_target="tpu_custom_call" | custom-call | flops 254803968 | bytes 1105920 | tf_op jit(solution)/shard_map/pallas_call | solution.py:108
  66.4 17.7 %all_to_all.10 = bf16[64,6,192]{2,1,0:T(8,128)(2,1)S(1)} all-to-all(bf16[64,6,192]{2,1,0:T(8,128)(2,1)} %shard_map.167), channel_id=1, replica_groups=mesh['rows'=64,'feat'=8] {'rows'}, dimensions={0} | all-to-all | bytes 294912 | tf_op jit(solution)/shard_map/all_to_all | solution.py:177
  84.2 0.7 copy.93
  84.9 0.6 copy.92
  (39 shorter events, 0.6 us)
Async XLA Ops:
  0.6 1.1 %copy-start = (bf16[192,576]{1,0:T(8,128)(2,1)S(1)}, bf16[192,576]{1,0:T(8,128)(2,1)}, u32[]{:S(2)}) copy-start(bf16[192,576]{1,0:T(8,128)(2,1)} %param.20) | copy-start | bytes 663556
  3.7 0.9 %copy-start.4 = (bf16[192,192]{1,0:T(8,128)(2,1)S(1)}, bf16[192,192]{1,0:T(8,128)(2,1)}, u32[]{:S(2)}) copy-start(bf16[192,192]{1,0:T(8,128)(2,1)} %param.21) | copy-start | bytes 221188
  3.7 1.2 %copy-start.6 = (f32[192]{0:T(256)S(1)}, f32[192]{0:T(256)}, u32[]{:S(2)}) copy-start(f32[192]{0:T(256)} %param.23) | copy-start | bytes 2308
  3.7 1.2 %copy-start.7 = (f32[192]{0:T(256)S(1)}, f32[192]{0:T(256)}, u32[]{:S(2)}) copy-start(f32[192]{0:T(256)} %param.22) | copy-start | bytes 2308
  4.0 1.2 %copy-start.5 = (s32[4,64]{1,0:T(4,128)S(1)}, s32[4,64]{1,0:T(4,128)}, u32[]{:S(2)}) copy-start(s32[4,64]{1,0:T(4,128)} %param.19) | copy-start | bytes 3076
  4.0 1.2 %copy-start.8 = (s32[2,64]{1,0:T(2,128)S(1)}, s32[2,64]{1,0:T(2,128)}, u32[]{:S(2)}) copy-start(s32[2,64]{1,0:T(2,128)} %param.18) | copy-start | bytes 1540
  4.0 15.3 %copy-start.2 = (bf16[768,192]{0,1:T(8,128)(2,1)S(1)}, bf16[768,192]{0,1:T(8,128)(2,1)}, u32[]{:S(2)}) copy-start(bf16[768,192]{0,1:T(8,128)(2,1)} %param.29) | copy-start | bytes 884740
  5.4 47.3 %copy-start.3 = (bf16[192,576]{1,0:T(8,128)(2,1)S(1)}, bf16[192,576]{1,0:T(8,128)(2,1)}, u32[]{:S(2)}) copy-start(bf16[192,576]{1,0:T(8,128)(2,1)} %param.24) | copy-start | bytes 663556
  6.3 23.3 %all-to-all-start = ((bf16[64,7,192]{2,1,0:T(8,128)(2,1)}), bf16[64,7,192]{2,1,0:T(8,128)(2,1)S(1)}, u32[]{:S(2)}, u32[]{:S(2)}) async-start(bf16[64,7,192]{2,1,0:T(8,128)(2,1)} %copy.86), calls=%async_computation | async-start | bytes 524288 | tf_op jit(solution)/shard_map/all_to_all | solution.py:155
  52.7 6.0 %copy-start.1 = (bf16[384,192]{1,0:T(8,128)(2,1)}, bf16[384,192]{1,0:T(8,128)(2,1)S(1)}, u32[]{:S(2)}) copy-start(bf16[384,192]{1,0:T(8,128)(2,1)S(1)} %reshape.98.rows_ref) | copy-start | bytes 442372

commit v12 on v10

--- a/solution.py
+++ b/solution.py
@@ -63,7 +63,7 @@
     alive_keys = (key_marks > 0)[None, None, :]
     masked = jnp.where(alive_keys, scores, NEG)
     row_top = jnp.max(masked, axis=-1, keepdims=True)
-    weights_exp = jnp.where(alive_keys, jnp.exp(masked - row_top), 0.0)
+    weights_exp = jnp.exp(masked - row_top)
     totals = jnp.sum(weights_exp, axis=-1)
     weighted = jnp.einsum(
         "hqk,khd->hqd",

time: 86 us -> 83.3 us (0.969)
  matrix products: 11.8 us -> 6.76 us
  other arithmetic: 1.27 us -> 3.72 us
    sub x1 -> x0, matrix products: 5.01 us -> none  [item_attention(): weights_exp = jnp.where(alive_keys, jnp.exp(masked - row_top), 0.0)]
    reduce_sum x0 -> x1, other arithmetic: none -> 2.34 us  [item_attention(): totals = jnp.sum(weights_exp, axis=-1)]
    dot_general x1, matrix products: 4.49 us -> 2.85 us  [item_attention(): jnp.einsum('hqk,khd->hqd', weights_exp.astype(jnp.bfloat16), key_values[:...]
    dot_general x0 -> x1, matrix products: none -> 1.61 us  [item_attention(): jnp.einsum('qhd,khd->hqk', queries, key_values[:, 0], preferred_element_t...]
where the time goes in v12:
time: 83.3 us; the launch traced here: 82.9 us
  blocking collectives  40 us (48%)
  starting transfers between devices  12.9 us (15%)
  waiting for transfers between devices  9.22 us (11%)
  matrix products  6.76 us (8%)
  local copies, waits for them, and re-layouts  6.09 us (7%)
  other arithmetic  3.72 us (4%)
  Pallas kernels  3.24 us (4%)
  between operations  0.99 us (1%)
    all_gather x1, blocking collectives, per_device(): lax.all_gather(jnp.concatenate([train_rows, key_mark_row[None, :]], axis=...  22.3 us
    all_to_all x1, blocking collectives, per_device(): lax.all_to_all(result_rows, 'rows', split_axis=0, concat_axis=0, tiled=True)  17.7 us
    all_to_all x1, starting transfers between devices, per_device(): lax.all_to_all(outbound, 'rows', split_axis=0, concat_axis=0, tiled=True)  12.9 us
    all_to_all x1, waiting for transfers between devices, per_device(): lax.all_to_all(outbound, 'rows', split_axis=0, concat_axis=0, tiled=True)  9.22 us
    pallas_call x1, Pallas kernels, item_tail(): pl.pallas_call(tail_kernel, out_shape=jax.ShapeDtypeStruct((source_count,...  3.24 us
    dot_general x1, matrix products, item_attention(): jnp.einsum('hqk,khd->hqd', weights_exp.astype(jnp.bfloat16), key_values[:...  2.85 us
    unnamed x22, local copies, waits for them, and re-layouts  2.35 us
    reduce_sum x1, other arithmetic, item_attention(): totals = jnp.sum(weights_exp, axis=-1)  2.34 us
  transfers between devices with their start and end apart: 1, of which 1 were waited for; matrix products, arithmetic and copies ran while one was open for 1% of the time, Pallas kernels for 0%

profile of v12, /device:TPU:1, one launch (start us, length us, event | category | flops | bytes accessed | tf_op | source)
XLA Modules:
  0.0 82.9 jit_solution(5335722162302900354)
XLA Ops:
  0.7 1.1 %pad_maximum_fusion.1 = bf16[6,64,192]{2,1,0:T(8,128)(2,1)S(1)} fusion(bf16[4,64,192]{2,1,0:T(8,128)(2,1)} %param.17, bf16[2,64,192]{2,1,0:T(8,128)(2,1)} %param.16), kind=kLoop, calls=%fused_computation.30 | loop fusion | flops 73728 | bytes 294912 | tf_op jit(solution)/shard_map/concatenate | solution.py:146
  1.8 0.1 copy.56
  2.0 0.4 convolution_convert_fusion.1
  2.4 0.6 reshape.91
  3.0 0.3 fusion.26
  3.3 0.6 fusion.27
  3.9 0.3 fusion.9
  4.2 0.2 copy.61
  4.4 0.3 reshape.92
  4.7 0.3 fusion.28
  5.0 0.1 add_convert_fusion
  5.2 0.1 copy.62
  5.5 0.8 %copy.64 = bf16[64,7,192]{2,1,0:T(8,128)(2,1)} copy(bf16[64,7,192]{2,0,1:T(8,128)(2,1)S(1)} %pad_maximum_fusion) | data formatting | bytes 344064 | tf_op jit(solution)/shard_map/concatenate | solution.py:150
  6.4 12.9 %all-to-all-start = ((bf16[64,7,192]{2,1,0:T(8,128)(2,1)}), bf16[64,7,192]{2,1,0:T(8,128)(2,1)S(1)}, u32[]{:S(2)}, u32[]{:S(2)}) async-start(bf16[64,7,192]{2,1,0:T(8,128)(2,1)} %copy.64), calls=%async_computation | async-start | bytes 524288 | tf_op jit(solution)/shard_map/all_to_all | solution.py:153
  19.3 0.1 broadcast_in_dim.46
  19.5 0.9 %copy.69.mlp_out_ref = bf16[768,192]{1,0:T(8,128)(2,1)} copy(bf16[768,192]{0,1:T(8,128)(2,1)S(1)} %copy-done.2) | data formatting | bytes 589824 | tf_op args[13]
  20.4 9.2 %all-to-all-done = bf16[64,7,192]{2,1,0:T(8,128)(2,1)S(1)} async-done(((bf16[64,7,192]{2,1,0:T(8,128)(2,1)}), bf16[64,7,192]{2,1,0:T(8,128)(2,1)S(1)}, u32[]{:S(2)}, u32[]{:S(2)}) %all-to-all-start) | async-done | bytes 172064 | tf_op jit(solution)/shard_map/all_to_all | solution.py:153
  29.6 0.1 slice_reduce_fusion
  29.8 0.1 copy.66
  30.0 0.2 reshape.95
  30.3 22.3 %all-gather.1 = bf16[8,129,192]{2,1,0:T(8,128)(2,1)S(1)} all-gather(bf16[1,129,192]{2,1,0:T(8,128)(2,1)S(1)} %maximum_bitcast_fusion), channel_id=2, replica_groups=mesh['rows'=64,'feat'=8] {'feat'}, dimensions={0}, use_global_device_ids=true | all-gather | bytes 445824 | tf_op jit(solution)/shard_map/all_gather | solution.py:161
  52.6 0.1 reshape.98.rows_ref
  52.8 0.5 convolution_convert_fusion
  53.3 0.3 convolution_convert_fusion.3
  53.6 0.1 squeeze.26
  53.7 1.6 %fusion.1 = (f32[6,384]{1,0:T(8,128)S(1)}, f32[6,384,1024]{2,1,0:T(8,128)S(1)}) fusion(pred[1024]{0:T(1024)(128)(4,1)S(1)} %compare_bitcast_fusion, bf16[384,6,32]{0,2,1:T(8,128)(2,1)S(1)} %bitcast.73, bf16[1024,2,6,32]{0,3,2,1:T(8,128)(2,1)S(1)} %bitcast.65), kind=kOutput, calls=%fused_computation.3 | convolution fusion | flops 158070528 | bytes 9988096 | tf_op jit(solution)/shard_map/qhd,khd->hqk/dot_general | solution.py:60
  55.3 2.3 %fusion.2 = f32[6,384]{1,0:T(8,128)S(1)} fusion(f32[6,384,1024]{2,1,0:T(8,128)S(1)} %get-tuple-element.20, f32[6,384]{1,0:T(8,128)S(1)} %get-tuple-element.19, pred[1024]{0:T(1024)(128)(4,1)S(1)} %compare_bitcast_fusion), kind=kLoop, calls=%fused_computation.4 | loop fusion | flops 9434880 | bytes 9456640 | tf_op jit(solution)/shard_map/reduce_sum | solution.py:67
  57.7 2.8 %fusion.16 = bf16[6,32,384]{2,1,0:T(8,128)(2,1)} fusion(f32[6,384,1024]{2,1,0:T(8,128)S(1)} %get-tuple-element.20, f32[6,384]{1,0:T(8,128)S(1)} %get-tuple-element.19, pred[1024]{0:T(1024)(128)(4,1)S(1)} %compare_bitcast_fusion, bf16[1024,2,6,32]{0,3,2,1:T(8,128)(2,1)S(1)} %bitcast.66, f32[6,384]{1,0:T(8,128)S(1)} %fusion.2, f32[384]{0:T(512)S(1)} %select_convert_fusion), kind=kOutput, calls=%fused_computation.20 | convolution fusion | flops 160653312 | bytes 10005504 | tf_op jit(solution)/shard_map/hqk,khd->hqd/dot_general | solution.py:68
  60.6 3.2 %shard_map.167 = bf16[64,6,192]{2,1,0:T(8,128)(2,1)} custom-call(bf16[192,384]{1,0:T(8,128)(2,1)} %bitcast.74, bf16[384,192]{1,0:T(8,128)(2,1)} %copy-done.1, bf16[192,192]{1,0:T(8,128)(2,1)} %item_out_ref.1, f32[1,192]{1,0:T(1,128)} %bitcast.77, f32[1,192]{1,0:T(1,128)} %bitcast.78, bf16[192,768]{1,0:T(8,128)(2,1)} %mlp_in_ref.1, ...), custom_call_target="tpu_custom_call" | custom-call | flops 254803968 | bytes 1105920 | tf_op jit(solution)/shard_map/pallas_call | solution.py:108
  63.8 17.7 %all_to_all.10 = bf16[64,6,192]{2,1,0:T(8,128)(2,1)S(1)} all-to-all(bf16[64,6,192]{2,1,0:T(8,128)(2,1)} %shard_map.167), channel_id=1, replica_groups=mesh['rows'=64,'feat'=8] {'rows'}, dimensions={0} | all-to-all | bytes 294912 | tf_op jit(solution)/shard_map/all_to_all | solution.py:175
  81.6 0.7 copy.71
  82.3 0.6 copy.70
  (42 shorter events, 0.7 us)
Async XLA Ops:
  0.6 1.3 %copy-start = (bf16[192,576]{1,0:T(8,128)(2,1)S(1)}, bf16[192,576]{1,0:T(8,128)(2,1)}, u32[]{:S(2)}) copy-start(bf16[192,576]{1,0:T(8,128)(2,1)} %param.20) | copy-start | bytes 663556
  0.6 4.0 %copy-start.4 = (bf16[192,192]{1,0:T(8,128)(2,1)S(1)}, bf16[192,192]{1,0:T(8,128)(2,1)}, u32[]{:S(2)}) copy-start(bf16[192,192]{1,0:T(8,128)(2,1)} %param.21) | copy-start | bytes 221188
  0.7 4.4 %copy-start.7 = (f32[192]{0:T(256)S(1)}, f32[192]{0:T(256)}, u32[]{:S(2)}) copy-start(f32[192]{0:T(256)} %param.22) | copy-start | bytes 2308
  0.7 4.4 %copy-start.6 = (f32[192]{0:T(256)S(1)}, f32[192]{0:T(256)}, u32[]{:S(2)}) copy-start(f32[192]{0:T(256)} %param.23) | copy-start | bytes 2308
  0.7 4.6 %copy-start.5 = (s32[4,64]{1,0:T(4,128)S(1)}, s32[4,64]{1,0:T(4,128)}, u32[]{:S(2)}) copy-start(s32[4,64]{1,0:T(4,128)} %param.19) | copy-start | bytes 3076
  0.7 4.6 %copy-start.8 = (s32[2,64]{1,0:T(2,128)S(1)}, s32[2,64]{1,0:T(2,128)}, u32[]{:S(2)}) copy-start(s32[2,64]{1,0:T(2,128)} %param.18) | copy-start | bytes 1540
  0.7 18.8 %copy-start.2 = (bf16[768,192]{0,1:T(8,128)(2,1)S(1)}, bf16[768,192]{0,1:T(8,128)(2,1)}, u32[]{:S(2)}) copy-start(bf16[768,192]{0,1:T(8,128)(2,1)} %param.29) | copy-start | bytes 884740
  2.3 50.4 %copy-start.3 = (bf16[192,576]{1,0:T(8,128)(2,1)S(1)}, bf16[192,576]{1,0:T(8,128)(2,1)}, u32[]{:S(2)}) copy-start(bf16[192,576]{1,0:T(8,128)(2,1)} %param.24) | copy-start | bytes 663556
  6.4 23.2 %all-to-all-start = ((bf16[64,7,192]{2,1,0:T(8,128)(2,1)}), bf16[64,7,192]{2,1,0:T(8,128)(2,1)S(1)}, u32[]{:S(2)}, u32[]{:S(2)}) async-start(bf16[64,7,192]{2,1,0:T(8,128)(2,1)} %copy.64), calls=%async_computation | async-start | bytes 524288 | tf_op jit(solution)/shard_map/all_to_all | solution.py:153
  52.8 4.9 %copy-start.1 = (bf16[384,192]{1,0:T(8,128)(2,1)}, bf16[384,192]{1,0:T(8,128)(2,1)S(1)}, u32[]{:S(2)}) copy-start(bf16[384,192]{1,0:T(8,128)(2,1)S(1)} %reshape.98.rows_ref) | copy-start | bytes 442372
